TPU v7x, 32 devices: a whole 2x2x4 slice. The times are simulated.
32 devices in a mesh: col: 8 (over y, x, core), row: 4 (over z).
Axes of the slice: x: 2, y: 2, z: 4, core: 2. Of those that a mesh axis runs over, the one named last changes fastest.
Arguments:
- p_blocks: bfloat16 [4, 72, 4096], P('row', 'col'), may hold values from -0.5390625 to 0.5390625
- p_slots: int32 [4, 72], P('row', 'col'), may hold values from 0 to 18, as said below
- out_slots: int32 [4, 104], P('row', 'col'), may hold values from 0 to 18, as said below
Outputs:
- purified: float32 [4, 104, 4096], P('row', 'col')
Inputs may be any that keep to these rules, and one draw needn't show every extreme that they name: `p_slots`: on each device the used slots (entries below 18) come first and name distinct positions; the remaining slots hold 18. Each device uses between half of its 9 slots (rounded up) and all of them, and some device uses all. `out_slots`: on each device the used slots (entries below 18) come first and name distinct positions; the remaining slots hold 18. Each device uses between half of its 13 slots (rounded up) and all of them, and some device uses all.
All inputs are finite; a program needn't handle non-finite values.
Results may differ from a plain program's by a relative error of at most 0.0003.
Values may be sent and summed in bfloat16 or wider, within the bound.
No kernel may reach another device: no remote copies, remote signals or barrier semaphores. Data moves between devices by JAX's collectives and lax.ppermute only.
A program may use at most 192 MiB of HBM per device.

v0:
```python
from functools import partial

import jax
import jax.numpy as jnp
from jax import lax
from jax.sharding import PartitionSpec as P

BLK = 64
COLS_DEV = 3


def add_terms(accum, portion, offset, table, capacity, rows_dev, block_edge, full_precision):
    block_vals, slot_ids = portion
    amount = slot_ids.shape[0]
    source = jnp.arange(amount, dtype=jnp.int32) // capacity
    local_row = slot_ids // COLS_DEV
    panel_row = source * COLS_DEV + slot_ids % COLS_DEV
    matching = table[panel_row]
    left = block_vals.reshape(amount, block_edge, block_edge)
    products = jnp.einsum("mab,mbw->maw", left, matching, preferred_element_type=jnp.float32)
    selector = (local_row[:, None] == jnp.arange(rows_dev, dtype=jnp.int32)[None, :]).astype(
        jnp.float32
    )
    return accum + jnp.einsum(
        "mr,maw->raw",
        selector,
        products,
        precision=lax.Precision.HIGHEST,
        preferred_element_type=jnp.float32,
    )


def on_device(p_blocks, p_slots, out_slots):
    n_row = lax.axis_size("row")
    n_col = lax.axis_size("col")
    capacity = p_slots.shape[1]
    block_edge = BLK
    rows_dev = COLS_DEV * n_col // n_row
    cells = rows_dev * COLS_DEV
    blocks_total = rows_dev * n_row
    width = COLS_DEV * block_edge
    own_blocks = p_blocks[0]
    own_ids = p_slots[0]
    down_blocks, down_ids = (
        lax.all_gather(own_blocks, "row", axis=0, tiled=True),
        lax.all_gather(own_ids, "row", axis=0, tiled=True),
    )
    source = jnp.arange(n_row * capacity, dtype=jnp.int32) // capacity
    panel_row = source * rows_dev + down_ids // COLS_DEV
    flat_index = jnp.where(
        down_ids < cells, panel_row * COLS_DEV + down_ids % COLS_DEV, blocks_total * COLS_DEV
    )
    column_panel = jnp.zeros((blocks_total * COLS_DEV, block_edge * block_edge), jnp.bfloat16)
    column_panel = column_panel.at[flat_index].set(down_blocks, mode="drop")
    column_panel = column_panel.reshape(blocks_total, COLS_DEV, block_edge, block_edge)
    column_panel = column_panel.transpose(0, 2, 1, 3).reshape(blocks_total, block_edge, width)
    empty = jnp.zeros((rows_dev, block_edge, width), jnp.float32)
    first_terms = partial(
        add_terms,
        table=column_panel,
        capacity=capacity,
        rows_dev=rows_dev,
        block_edge=block_edge,
        full_precision=False,
    )
    square = first_terms(
        empty,
        (
            lax.all_gather(own_blocks, "col", axis=0, tiled=True),
            lax.all_gather(own_ids, "col", axis=0, tiled=True),
        ),
        jnp.int32(0),
    )
    square_flat = square.reshape(rows_dev * block_edge, width)
    column_matrix = column_panel.reshape(blocks_total * block_edge, width).astype(jnp.float32)
    cube = jnp.dot(
        lax.all_gather(square_flat, "col", axis=1, tiled=True),
        column_matrix,
        precision=lax.Precision.HIGHEST,
        preferred_element_type=jnp.float32,
    )
    combined = 3.0 * square_flat - 2.0 * cube
    new_grid = combined.reshape(rows_dev, block_edge, COLS_DEV, block_edge).transpose(0, 2, 1, 3)
    new_grid = new_grid.reshape(cells, block_edge * block_edge)
    out_ids = out_slots[0]
    picked = new_grid[jnp.minimum(out_ids, cells - 1)]
    picked = jnp.where((out_ids < cells)[:, None], picked, jnp.zeros_like(picked))
    return picked[None]


def solution(mesh):
    in_specs = (P("row", "col", None), P("row", "col"), P("row", "col"))
    out_specs = P("row", "col", None)
    return jax.shard_map(
        on_device, mesh=mesh, in_specs=in_specs, out_specs=out_specs, check_vma=False
    )
```

profile of v0, /device:TPU:0, one launch (start us, length us, event | category | flops | bytes accessed | tf_op | source)
XLA Modules:
  0.0 116.2 jit_solution(5685451700651422301)
XLA Ops:
  6.5 1.1 copy.30
  7.6 18.3 %all-gather.2 = bf16[1,36,4096]{2,0,1:T(2,128)(2,1)S(1)} all-gather(bf16[1,9,4096]{2,0,1:T(2,128)(2,1)S(1)} %copy.30), channel_id=4, replica_groups=mesh['col'=8,'row'=4] {'row'}, dimensions={1}, use_global_device_ids=true | all-gather | bytes 368640 | tf_op jit(solution)/shard_map/all_gather | solution.py:45
  25.9 11.5 %all-gather.3 = bf16[1,72,4096]{2,0,1:T(2,128)(2,1)S(1)} all-gather(bf16[1,9,4096]{2,0,1:T(2,128)(2,1)S(1)} %copy.30), channel_id=5, replica_groups=mesh['col'=8,'row'=4] {'col'}, dimensions={1}, use_global_device_ids=true | all-gather | bytes 663552 | tf_op jit(solution)/shard_map/all_gather | solution.py:69
  37.4 0.7 dynamic-slice.1
  38.1 0.6 dynamic-slice
  40.1 7.0 %all-reduce = s32[72]{0:T(128)S(1)} all-reduce(s32[72]{0:T(128)S(1)} %get-tuple-element.7), channel_id=2, replica_groups=mesh['col'=8,'row'=4] {'col'}, use_global_device_ids=true, to_apply=%add | all-reduce | flops 72 | bytes 576
  47.2 8.0 %all-reduce.1 = s32[36]{0:T(128)S(1)} all-reduce(s32[36]{0:T(128)S(1)} %get-tuple-element.8), channel_id=3, replica_groups=mesh['col'=8,'row'=4] {'row'}, use_global_device_ids=true, to_apply=%add.1 | all-reduce | flops 36 | bytes 288
  55.2 1.5 %scatter_custom_fusion = bf16[72,4096]{1,0:T(8,128)(2,1)S(1)} fusion(s32[36]{0:T(128)S(1)} %compare_select_fusion.2, bf16[1,36,4096]{2,0,1:T(2,128)(2,1)S(1)} %all-gather.2, bf16[]{:T(256)} %constant.56.clone.1), kind=kCustom, calls=%fused_computation.8 | custom fusion | bytes 1179650 | tf_op jit(solution)/shard_map/scatter | solution.py:54
  56.7 1.3 %reshape.73 = bf16[24,3,64,64]{3,2,1,0:T(8,128)(2,1)S(1)} reshape(bf16[72,4096]{1,0:T(8,128)(2,1)S(1)} %scatter_custom_fusion) | data formatting | bytes 1179648 | tf_op jit(solution)/shard_map/reshape | solution.py:55
  58.0 3.6 %reduce = bf16[72,4096]{1,0:T(8,128)(2,1)S(1)} reduce(bf16[1,72,4096]{2,0,1:T(2,128)(2,1)S(1)} %all-gather.3, bf16[]{:T(256)} %constant.80), dimensions={0}, to_apply=%all-gather.3.reduce_sub_computation | reduce | bytes 1179650 | tf_op jit(solution)/shard_map/all_gather | solution.py:69
  61.5 1.3 %reshape.75 = bf16[72,64,64]{2,1,0:T(8,128)(2,1)S(1)} reshape(bf16[72,4096]{1,0:T(8,128)(2,1)S(1)} %reduce) | data formatting | bytes 1179648 | tf_op jit(solution)/shard_map/reshape | solution.py:19
  62.8 0.9 copy.31
  63.7 3.0 %gather_fusion = bf16[72,64,192]{1,2,0:T(8,128)(2,1)} fusion(bf16[24,64,192]{1,2,0:T(8,128)(2,1)S(1)} %bitcast.40, s32[1024]{0:T(1024)S(1)} %pad_clamp_fusion.1), kind=kCustom, calls=%fused_computation | custom fusion | bytes 3539232 | tf_op jit(solution)/shard_map/gather | solution.py:18
  66.7 4.4 %convolution_bitcast_fusion = f32[72,64,192]{2,1,0:T(8,128)S(1)} fusion(bf16[72,64,192]{1,2,0:T(8,128)(2,1)} %gather_fusion, bf16[72,64,64]{2,1,0:T(8,128)(2,1)S(1)} %reshape.75), kind=kOutput, calls=%fused_computation.5 | convolution fusion | flops 113246208 | bytes 5898240 | tf_op jit(solution)/shard_map/mab,mbw->maw/dot_general | solution.py:20
  71.1 4.3 %fusion = f32[6,64,192]{2,0,1:T(8,128)S(1)} fusion(f32[72,64,192]{2,1,0:T(8,128)S(1)} %convolution_bitcast_fusion, s32[72]{0:T(128)S(1)} %get-tuple-element.5), kind=kOutput, calls=%fused_computation.3 | convolution fusion | flops 63701424 | bytes 3834144 | tf_op jit(solution)/shard_map/mr,maw->raw/dot_general | solution.py:24
  75.5 0.9 copy.36
  76.4 1.3 %copy.38 = bf16[24,64,3,64]{1,0,3,2:T(8,128)(2,1)S(1)} copy(bf16[24,64,3,64]{3,1,2,0:T(8,128)(2,1)S(1)} %bitcast.39) | data formatting | bytes 1179648 | tf_op jit(solution)/shard_map/transpose | solution.py:56
  77.8 0.7 reshape_reshape.3
  78.5 25.6 %all-gather.6.cloned.1.call-done = f32[384,1536]{0,1:T(8,128)} async-done(((f32[384,192]{0,1:T(8,128)}), f32[384,1536]{0,1:T(8,128)}) %all-gather.6.cloned.1.call-update) | async-done | bytes 2359312 | tf_op jit(solution)/shard_map/all_gather | solution.py:77
  104.1 2.9 %fusion.2 = f32[384,192]{0,1:T(8,128)S(1)} fusion(f32[384,1536]{0,1:T(8,128)} %all-gather.6.cloned.1.call-done, bf16[1536,192]{0,1:T(8,128)(2,1)S(1)} %reshape_reshape.3, f32[384,192]{0,1:T(8,128)S(1)} %copy-done), kind=kOutput, calls=%fused_computation.7 | convolution fusion | flops 1359175680 | bytes 3538944 | tf_op jit(solution)/shard_map/dot_general | solution.py:76
  107.3 0.3 copy.39
  107.5 0.2 reshape.78
  107.7 0.6 gather_fusion.1
  108.5 0.9 copy.40
  (24 shorter events, 0.6 us)
Async XLA Ops:
  6.5 30.9 %copy-start.4 = (u32[32]{0:T(128)S(1)}, u32[32]{0:T(128)}, u32[]{:S(2)}) copy-start(u32[32]{0:T(128)} %constant.75) | copy-start | bytes 388
  6.5 31.5 %copy-start.3 = (u32[32]{0:T(128)S(1)}, u32[32]{0:T(128)}, u32[]{:S(2)}) copy-start(u32[32]{0:T(128)} %constant.70) | copy-start | bytes 388
  6.5 33.5 %copy-start.1 = (s32[1,9]{1,0:T(1,128)S(1)}, s32[1,9]{1,0:T(1,128)}, u32[]{:S(2)}) copy-start(s32[1,9]{1,0:T(1,128)} %param.4) | copy-start | bytes 112
  6.5 97.6 %all-gather.6.cloned.1.call-start = ((), (), s32[]{:S(2)}) async-start(), calls=%async_computation | async-start | bytes 2654208 | tf_op jit(solution)/shard_map/all_gather | solution.py:77
  76.4 2.1 %copy-start.2 = (s32[1,13]{1,0:T(1,128)S(1)}, s32[1,13]{1,0:T(1,128)}, u32[]{:S(2)}) copy-start(s32[1,13]{1,0:T(1,128)} %param.5) | copy-start | bytes 160
  76.4 27.7 %copy-start = (f32[384,192]{0,1:T(8,128)S(1)}, f32[384,192]{0,1:T(8,128)}, u32[]{:S(2)}) copy-start(f32[384,192]{0,1:T(8,128)} %copy.36) | copy-start | bytes 884740
Sparse Core Ops, SparseCore 0:
  76.5 27.5 all-gather.5
where the time goes:
time: 116 us
  blocking collectives  44.8 us (39%)
  waiting for transfers between devices  25.6 us (22%)
  local copies, waits for them, and re-layouts  15.6 us (13%)
  between operations  14.9 us (13%)
  matrix products  11.6 us (10%)
  other arithmetic  3.71 us (3%)
    all_gather x1, waiting for transfers between devices, on_device(): lax.all_gather(square_flat, 'col', axis=1, tiled=True)  25.6 us
    all_gather x1, blocking collectives, on_device(): lax.all_gather(own_blocks, 'row', axis=0, tiled=True)  18.3 us
    unnamed x2, blocking collectives  15 us
    all_gather x1, blocking collectives, on_device(): lax.all_gather(own_blocks, 'col', axis=0, tiled=True)  11.5 us
    dot_general x1, matrix products, add_terms(): jnp.einsum('mab,mbw->maw', left, matching, preferred_element_type=jnp.flo...  4.36 us
    dot_general x1, matrix products, add_terms(): jnp.einsum('mr,maw->raw', selector, products, precision=lax.Precision.HIG...  4.29 us
    all_gather x1, other arithmetic, on_device(): lax.all_gather(own_blocks, 'col', axis=0, tiled=True)  3.56 us
    gather x1, local copies, waits for them, and re-layouts, add_terms(): matching = table[panel_row]  3.03 us
  transfers between devices with their start and end apart: 1, of which 1 were waited for; matrix products, arithmetic and copies ran while one was open for 2% of the time, Pallas kernels for 0%

commit v1 on v0

v1 whole, which is shorter than its diff:
```python
import jax
import jax.numpy as jnp
from jax import lax
from jax.sharding import PartitionSpec as P

BLK = 64
COLS_DEV = 3


def on_device(p_blocks, p_slots, out_slots):
    n_row = lax.axis_size("row")
    n_col = lax.axis_size("col")
    capacity = p_slots.shape[1]
    block_edge = BLK
    area = block_edge * block_edge
    rows_dev = COLS_DEV * n_col // n_row
    cells = rows_dev * COLS_DEV
    blocks_total = rows_dev * n_row
    width = COLS_DEV * block_edge
    height = rows_dev * block_edge

    own_ids = p_slots[0]
    id_row = jnp.zeros((1, area), jnp.bfloat16)
    id_row = id_row.at[0, :capacity].set(own_ids.astype(jnp.bfloat16))
    payload = jnp.concatenate([p_blocks[0], id_row], axis=0)

    down = lax.all_gather(payload, "row", axis=0, tiled=False)
    down_ids = down[:, capacity, :capacity].astype(jnp.int32)
    down_row = jnp.arange(n_row, dtype=jnp.int32)[:, None] * rows_dev + down_ids // COLS_DEV
    down_index = jnp.where(
        down_ids < cells, down_row * COLS_DEV + down_ids % COLS_DEV, blocks_total * COLS_DEV
    )
    column_grid = jnp.zeros((blocks_total * COLS_DEV, area), jnp.bfloat16)
    column_grid = column_grid.at[down_index.reshape(-1)].set(
        down[:, :capacity].reshape(n_row * capacity, area), mode="drop"
    )
    column_panel = (
        column_grid.reshape(blocks_total, COLS_DEV, block_edge, block_edge)
        .transpose(0, 2, 1, 3)
        .reshape(blocks_total * block_edge, width)
    )

    across = lax.all_gather(payload, "col", axis=0, tiled=False)
    across_ids = across[:, capacity, :capacity].astype(jnp.int32)
    across_col = jnp.arange(n_col, dtype=jnp.int32)[:, None] * COLS_DEV + across_ids % COLS_DEV
    across_index = jnp.where(
        across_ids < cells,
        (across_ids // COLS_DEV) * blocks_total + across_col,
        rows_dev * blocks_total,
    )
    row_grid = jnp.zeros((rows_dev * blocks_total, area), jnp.bfloat16)
    row_grid = row_grid.at[across_index.reshape(-1)].set(
        across[:, :capacity].reshape(n_col * capacity, area), mode="drop"
    )
    row_panel = (
        row_grid.reshape(rows_dev, blocks_total, block_edge, block_edge)
        .transpose(0, 2, 1, 3)
        .reshape(height, blocks_total * block_edge)
    )

    square = jnp.dot(row_panel, column_panel, preferred_element_type=jnp.float32)
    square_panel = lax.all_gather(square, "row", axis=0, tiled=True)
    cube = jnp.dot(
        row_panel.astype(jnp.float32),
        square_panel,
        precision=lax.Precision.HIGHEST,
        preferred_element_type=jnp.float32,
    )
    combined = 3.0 * square - 2.0 * cube
    new_grid = combined.reshape(rows_dev, block_edge, COLS_DEV, block_edge).transpose(0, 2, 1, 3)
    new_grid = new_grid.reshape(cells, area)
    out_ids = out_slots[0]
    picked = new_grid[jnp.minimum(out_ids, cells - 1)]
    picked = jnp.where((out_ids < cells)[:, None], picked, jnp.zeros_like(picked))
    return picked[None]


def solution(mesh):
    in_specs = (P("row", "col", None), P("row", "col"), P("row", "col"))
    out_specs = P("row", "col", None)
    return jax.shard_map(
        on_device, mesh=mesh, in_specs=in_specs, out_specs=out_specs, check_vma=False
    )
```

time: 116 us -> 101 us (0.87)
  blocking collectives: 44.8 us -> 28.8 us
  matrix products: 11.6 us -> 3.83 us
  waiting for transfers between devices: 25.6 us -> 30.9 us
  local copies, waits for them, and re-layouts: 15.6 us -> 19.6 us
  between operations: 14.9 us -> 13.6 us
    unnamed x2 -> x0, blocking collectives: 15 us -> none
    dot_general x3 -> x2, matrix products: 11.6 us -> 3.83 us  [the longest x1 2.56 us: on_device(): jnp.dot(row_panel.astype(jnp.float32), square_panel, precision=lax.Precis...]
    all_gather x1, waiting for transfers between devices: 25.6 us -> 30.9 us  [on_device(): square_panel = lax.all_gather(square, 'row', axis=0, tiled=True)]
    reshape x4 -> x7, local copies, waits for them, and re-layouts: 3.6 us -> 8.63 us  [the longest x1 3.5 us: on_device(): row_panel = row_grid.reshape(rows_dev, blocks_total, block_edge, block_ed...]
    all_gather x1 -> x0, other arithmetic: 3.56 us -> none  [on_device(): lax.all_gather(own_blocks, 'col', axis=0, tiled=True)]
    gather x1 -> x0, local copies, waits for them, and re-layouts: 3.03 us -> none  [add_terms(): matching = table[panel_row]]
    transpose x2, local copies, waits for them, and re-layouts: 2.23 us -> 4.28 us  [the longest x1 2.94 us: on_device(): row_panel = row_grid.reshape(rows_dev, blocks_total, block_edge, block_ed...]
    another operation x0 -> x2, other arithmetic: none -> 1.94 us
  transfers between devices with their start and end apart: 1 -> 1, of which waited for: 1 -> 1; matrix products, arithmetic and copies ran while one was open for 2% -> 0% of each run, Pallas kernels for 0% -> 0%
where the time goes in v1:
time: 101 us; the launch traced here: 100 us
  waiting for transfers between devices  30.9 us (31%)
  blocking collectives  28.8 us (29%)
  local copies, waits for them, and re-layouts  19.6 us (19%)
  between operations  13.6 us (13%)
  matrix products  3.83 us (4%)
  other arithmetic  3.67 us (4%)
    all_gather x1, waiting for transfers between devices, on_device(): square_panel = lax.all_gather(square, 'row', axis=0, tiled=True)  30.9 us
    all_gather x1, blocking collectives, on_device(): down = lax.all_gather(payload, 'row', axis=0, tiled=False)  16.3 us
    all_gather x1, blocking collectives, on_device(): across = lax.all_gather(payload, 'col', axis=0, tiled=False)  12.4 us
    reshape x1, local copies, waits for them, and re-layouts, on_device(): row_panel = row_grid.reshape(rows_dev, blocks_total, block_edge, block_ed...  3.5 us
    transpose x1, local copies, waits for them, and re-layouts, on_device(): row_panel = row_grid.reshape(rows_dev, blocks_total, block_edge, block_ed...  2.94 us
    reshape x1, local copies, waits for them, and re-layouts, on_device(): row_grid.reshape(rows_dev, blocks_total, block_edge, block_edge)  2.57 us
    dot_general x1, matrix products, on_device(): jnp.dot(row_panel.astype(jnp.float32), square_panel, precision=lax.Precis...  2.56 us
  transfers between devices with their start and end apart: 1, of which 1 were waited for; matrix products, arithmetic and copies ran while one was open for 0% of the time, Pallas kernels for 0%

profile of v1, /device:TPU:0, one launch (start us, length us, event | category | flops | bytes accessed | tf_op | source)
XLA Modules:
  0.0 100.4 jit_solution(6214441134641464494)
XLA Ops:
  6.5 0.6 compare_reduce_fusion.4
  7.2 1.3 %broadcast_select_fusion = bf16[1,9]{1,0:T(2,128)(2,1)S(1)} fusion(pred[]{:T(512)} %compare_reduce_fusion.4, s32[1,9]{1,0:T(1,128)} %param.6), kind=kLoop, calls=%fused_computation.34 | loop fusion | flops 18 | bytes 55 | tf_op jit(solution)/shard_map/select.3
  8.5 0.9 fusion.7
  9.4 12.4 %all-gather.2 = bf16[8,10,4096]{2,1,0:T(8,128)(2,1)S(1)} all-gather(bf16[1,10,4096]{2,1,0:T(8,128)(2,1)S(1)} %fusion.7), channel_id=2, replica_groups=mesh['col'=8,'row'=4] {'col'}, dimensions={0}, use_global_device_ids=true | all-gather | bytes 737280 | tf_op jit(solution)/shard_map/all_gather | solution.py:43
  21.9 16.3 %all-gather.3 = bf16[4,10,4096]{2,1,0:T(8,128)(2,1)S(1)} all-gather(bf16[1,10,4096]{2,1,0:T(8,128)(2,1)S(1)} %fusion.7), channel_id=3, replica_groups=mesh['col'=8,'row'=4] {'row'}, dimensions={0}, use_global_device_ids=true | all-gather | bytes 409600 | tf_op jit(solution)/shard_map/all_gather | solution.py:27
  38.3 0.8 copy-done
  39.1 0.5 compare_reduce_fusion.2
  40.1 0.3 reshape.316
  40.4 1.8 %scatter_custom_fusion = bf16[144,4096]{1,0:T(8,128)(2,1)S(1)} fusion(s32[72]{0:T(128)S(1)} %fusion.12, bf16[72,4096]{1,0:T(8,128)(2,1)S(1)} %reshape.316, bf16[]{:T(256)} %constant.75.clone.1), kind=kCustom, calls=%fused_computation.5 | custom fusion | bytes 1179650 | tf_op jit(solution)/shard_map/scatter | solution.py:52
  42.2 2.6 %reshape.297 = bf16[6,24,64,64]{3,2,1,0:T(8,128)(2,1)S(1)} reshape(bf16[144,4096]{1,0:T(8,128)(2,1)S(1)} %scatter_custom_fusion) | data formatting | bytes 2359296 | tf_op jit(solution)/shard_map/reshape | solution.py:56
  44.8 2.9 %copy.12 = bf16[6,64,24,64]{3,2,1,0:T(8,128)(2,1)} copy(bf16[6,64,24,64]{3,1,2,0:T(8,128)(2,1)S(1)} %bitcast.34) | data formatting | bytes 2359296 | tf_op jit(solution)/shard_map/transpose | solution.py:57
  47.7 3.5 %reshape.298 = bf16[384,1536]{1,0:T(8,128)(2,1)S(1)} reshape(bf16[6,64,24,64]{3,2,1,0:T(8,128)(2,1)} %copy.12) | data formatting | bytes 2359296 | tf_op jit(solution)/shard_map/reshape | solution.py:58
  51.9 1.2 %scatter_custom_fusion.1 = bf16[72,4096]{1,0:T(8,128)(2,1)S(1)} fusion(s32[36]{0:T(128)S(1)} %fusion.13, bf16[36,4096]{1,0:T(8,128)(2,1)S(1)} %reshape.324, bf16[]{:T(256)} %constant.75.clone.1), kind=kCustom, calls=%fused_computation.7 | custom fusion | bytes 589826 | tf_op jit(solution)/shard_map/scatter | solution.py:34
  53.1 1.3 %reshape.300 = bf16[24,3,64,64]{3,2,1,0:T(8,128)(2,1)S(1)} reshape(bf16[72,4096]{1,0:T(8,128)(2,1)S(1)} %scatter_custom_fusion.1) | data formatting | bytes 1179648 | tf_op jit(solution)/shard_map/reshape | solution.py:38
  54.4 1.3 %copy.13 = bf16[24,64,3,64]{1,0,3,2:T(8,128)(2,1)S(1)} copy(bf16[24,64,3,64]{3,1,2,0:T(8,128)(2,1)S(1)} %bitcast.35) | data formatting | bytes 1179648 | tf_op jit(solution)/shard_map/transpose | solution.py:39
  55.7 0.7 reshape.301
  56.4 1.3 %fusion.15 = f32[384,192]{0,1:T(8,128)} fusion(bf16[384,1536]{1,0:T(8,128)(2,1)S(1)} %reshape.298, bf16[1536,192]{0,1:T(8,128)(2,1)S(1)} %reshape.301), kind=kOutput, calls=%fused_computation.44 | convolution fusion | flops 226492416 | bytes 2064384 | tf_op jit(solution)/shard_map/dot_general | solution.py:61
  57.8 30.9 %all-gather.6.cloned.1.call-done = f32[1536,192]{0,1:T(8,128)} async-done(((f32[384,192]{0,1:T(8,128)}), f32[1536,192]{0,1:T(8,128)}) %all-gather.6.cloned.1.call-update) | async-done | bytes 1179664 | tf_op jit(solution)/shard_map/all_gather | solution.py:62
  88.7 2.6 %fusion = f32[384,192]{0,1:T(8,128)S(1)} fusion(bf16[384,1536]{1,0:T(8,128)(2,1)S(1)} %reshape.298, f32[1536,192]{0,1:T(8,128)} %all-gather.6.cloned.1.call-done, f32[384,192]{0,1:T(8,128)} %fusion.15), kind=kOutput, calls=%fused_computation.4 | convolution fusion | flops 1359175680 | bytes 2949120 | tf_op jit(solution)/shard_map/dot_general | solution.py:63
  91.3 0.2 reshape.302
  91.4 0.3 copy.14
  91.7 0.2 reshape.303
  91.9 0.6 gather_fusion
  92.6 0.9 copy.15
  (33 shorter events, 1.4 us)
Async XLA Ops:
  6.5 82.2 %all-gather.6.cloned.1.call-start = ((), (), s32[]{:S(2)}) async-start(), calls=%async_computation | async-start | bytes 1474560 | tf_op jit(solution)/shard_map/all_gather | solution.py:62
  38.3 0.8 copy-start
  47.7 3.7 %copy-start.2 = (pred[4,9]{1,0:T(4,128)(4,1)S(1)}, pred[4,9]{1,0:T(4,128)(4,1)}, u32[]{:S(2)}) copy-start(pred[4,9]{1,0:T(4,128)(4,1)} %get-tuple-element.22) | copy-start | bytes 112
  47.7 4.0 %copy-start.1 = (bf16[4,10,4096]{2,1,0:T(8,128)(2,1)S(1)}, bf16[4,10,4096]{2,1,0:T(8,128)(2,1)}, u32[]{:S(2)}) copy-start(bf16[4,10,4096]{2,1,0:T(8,128)(2,1)} %copy-done) | copy-start | bytes 983044
  56.4 1.3 %copy-start.3 = (s32[1,13]{1,0:T(1,128)S(1)}, s32[1,13]{1,0:T(1,128)}, u32[]{:S(2)}) copy-start(s32[1,13]{1,0:T(1,128)} %param.7) | copy-start | bytes 160
Sparse Core Ops, SparseCore 0:
  57.9 30.7 all-gather.5

commit v2 on v1

--- a/solution.py
+++ b/solution.py
@@ -5,6 +5,14 @@
 
 BLK = 64
 COLS_DEV = 3
+
+
+def shifted_copies(value, axis, size):
+    pieces = [value]
+    for shift in range(1, size):
+        pairs = [(i, (i + shift) % size) for i in range(size)]
+        pieces.append(lax.ppermute(value, axis, pairs))
+    return jax.tree.map(lambda *xs: jnp.stack(xs), *pieces)
 
 
 def on_device(p_blocks, p_slots, out_slots):
@@ -18,21 +26,22 @@
     blocks_total = rows_dev * n_row
     width = COLS_DEV * block_edge
     height = rows_dev * block_edge
+    row_idx = lax.axis_index("row")
+    col_idx = lax.axis_index("col")
+    own = (p_blocks[0], p_slots[0])
 
-    own_ids = p_slots[0]
-    id_row = jnp.zeros((1, area), jnp.bfloat16)
-    id_row = id_row.at[0, :capacity].set(own_ids.astype(jnp.bfloat16))
-    payload = jnp.concatenate([p_blocks[0], id_row], axis=0)
+    def shift_order(block):
+        owner = block // rows_dev
+        return ((row_idx - owner) % n_row) * rows_dev + block % rows_dev
 
-    down = lax.all_gather(payload, "row", axis=0, tiled=False)
-    down_ids = down[:, capacity, :capacity].astype(jnp.int32)
+    down_blocks, down_ids = shifted_copies(own, "row", n_row)
     down_row = jnp.arange(n_row, dtype=jnp.int32)[:, None] * rows_dev + down_ids // COLS_DEV
     down_index = jnp.where(
         down_ids < cells, down_row * COLS_DEV + down_ids % COLS_DEV, blocks_total * COLS_DEV
     )
     column_grid = jnp.zeros((blocks_total * COLS_DEV, area), jnp.bfloat16)
     column_grid = column_grid.at[down_index.reshape(-1)].set(
-        down[:, :capacity].reshape(n_row * capacity, area), mode="drop"
+        down_blocks.reshape(n_row * capacity, area), mode="drop"
     )
     column_panel = (
         column_grid.reshape(blocks_total, COLS_DEV, block_edge, block_edge)
@@ -40,9 +49,9 @@
         .reshape(blocks_total * block_edge, width)
     )
 
-    across = lax.all_gather(payload, "col", axis=0, tiled=False)
-    across_ids = across[:, capacity, :capacity].astype(jnp.int32)
-    across_col = jnp.arange(n_col, dtype=jnp.int32)[:, None] * COLS_DEV + across_ids % COLS_DEV
+    across_blocks, across_ids = shifted_copies(own, "col", n_col)
+    across_src = (col_idx - jnp.arange(n_col, dtype=jnp.int32)[:, None]) % n_col
+    across_col = shift_order(across_src * COLS_DEV + across_ids % COLS_DEV)
     across_index = jnp.where(
         across_ids < cells,
         (across_ids // COLS_DEV) * blocks_total + across_col,
@@ -50,7 +59,7 @@
     )
     row_grid = jnp.zeros((rows_dev * blocks_total, area), jnp.bfloat16)
     row_grid = row_grid.at[across_index.reshape(-1)].set(
-        across[:, :capacity].reshape(n_col * capacity, area), mode="drop"
+        across_blocks.reshape(n_col * capacity, area), mode="drop"
     )
     row_panel = (
         row_grid.reshape(rows_dev, blocks_total, block_edge, block_edge)
@@ -59,7 +68,7 @@
     )
 
     square = jnp.dot(row_panel, column_panel, preferred_element_type=jnp.float32)
-    square_panel = lax.all_gather(square, "row", axis=0, tiled=True)
+    square_panel = shifted_copies(square, "row", n_row).reshape(blocks_total * block_edge, width)
     cube = jnp.dot(
         row_panel.astype(jnp.float32),
         square_panel,

time: 101 us -> 88.5 us (0.88)
  the two profiles are of different devices: /device:TPU:0 before, /device:TPU:9 now
where the time goes in v2:
time: 88.5 us; the launch traced here: 88.3 us
  starting transfers between devices  33.9 us (38%)
  waiting for transfers between devices  28.1 us (32%)
  local copies, waits for them, and re-layouts  20.6 us (23%)
  other arithmetic  3.47 us (4%)
  matrix products  1.83 us (2%)
    ppermute x23, starting transfers between devices, shifted_copies(): pieces.append(lax.ppermute(value, axis, pairs))  33.9 us
    ppermute x23, waiting for transfers between devices, shifted_copies(): pieces.append(lax.ppermute(value, axis, pairs))  28.1 us
    reshape x1, local copies, waits for them, and re-layouts, on_device(): row_panel = row_grid.reshape(rows_dev, blocks_total, block_edge, block_ed...  3.44 us
    transpose x1, local copies, waits for them, and re-layouts, on_device(): row_panel = row_grid.reshape(rows_dev, blocks_total, block_edge, block_ed...  2.97 us
    reshape x1, local copies, waits for them, and re-layouts, on_device(): row_grid.reshape(rows_dev, blocks_total, block_edge, block_edge)  2.57 us
    scatter x1, local copies, waits for them, and re-layouts, on_device(): row_grid.at[across_index.reshape(-1)]  1.8 us
  transfers between devices with their start and end apart: 23, of which 6 were waited for; matrix products, arithmetic and copies ran while one was open for 18% of the time, Pallas kernels for 0%

profile of v2, /device:TPU:9, one launch (start us, length us, event | category | flops | bytes accessed | tf_op | source)
XLA Modules:
  0.0 88.3 jit_solution(5801923536951227797)
XLA Ops:
  0.0 1.8 %collective-permute-start = (s32[9]{0:T(128)}, s32[9]{0:T(128)S(1)}, u32[]{:S(2)}, u32[]{:S(2)}) collective-permute-start(s32[9]{0:T(128)} %bitcast.73), channel_id=1, source_target_pairs={{0,4},{4,8},{8,12},{12,16},{16,20},{20,24},{24,28},{28,0},{1,5},{5... | collective-permute-start | bytes 116 | tf_op jit(solution)/shard_map/ppermute | solution.py:14
  3.5 2.6 %collective-permute-start.4 = (s32[9]{0:T(128)}, s32[9]{0:T(128)S(1)}, u32[]{:S(2)}, u32[]{:S(2)}) collective-permute-start(s32[9]{0:T(128)} %bitcast.77), channel_id=1, source_target_pairs={{0,20},{4,24},{8,28},{12,0},{16,4},{20,8},{24,12},{28,16},{1,21},{... | collective-permute-start | bytes 116 | tf_op jit(solution)/shard_map/ppermute | solution.py:14
  8.0 1.3 %collective-permute-start.5 = (s32[9]{0:T(128)}, s32[9]{0:T(128)S(1)}, u32[]{:S(2)}, u32[]{:S(2)}) collective-permute-start(s32[9]{0:T(128)} %bitcast.78), channel_id=1, source_target_pairs={{0,24},{4,28},{8,0},{12,4},{16,8},{20,12},{24,16},{28,20},{1,25},{... | collective-permute-start | bytes 116 | tf_op jit(solution)/shard_map/ppermute | solution.py:14
  9.3 1.7 %collective-permute-start.7 = (bf16[9,4096]{1,0:T(8,128)(2,1)}, bf16[9,4096]{1,0:T(8,128)(2,1)S(1)}, u32[]{:S(2)}, u32[]{:S(2)}) collective-permute-start(bf16[9,4096]{1,0:T(8,128)(2,1)} %bitcast.10), channel_id=1, source_target_pairs={{0,4},{4,8},{8,12},{12,16},{16,20},{20,24},{24,28},{28,0},{1,5},{5... | collective-permute-start | bytes 221192 | tf_op jit(solution)/shard_map/ppermute | solution.py:14
  12.2 1.3 %collective-permute-start.10 = (bf16[9,4096]{1,0:T(8,128)(2,1)}, bf16[9,4096]{1,0:T(8,128)(2,1)S(1)}, u32[]{:S(2)}, u32[]{:S(2)}) collective-permute-start(bf16[9,4096]{1,0:T(8,128)(2,1)} %bitcast.10), channel_id=1, source_target_pairs={{0,16},{4,20},{8,24},{12,28},{16,0},{20,4},{24,8},{28,12},{1,17},{... | collective-permute-start | bytes 221192 | tf_op jit(solution)/shard_map/ppermute | solution.py:14
  13.5 1.3 %collective-permute-start.14 = (s32[9]{0:T(128)}, s32[9]{0:T(128)S(1)}, u32[]{:S(2)}, u32[]{:S(2)}) collective-permute-start(s32[9]{0:T(128)} %bitcast.80), channel_id=1, source_target_pairs={{0,1},{1,2},{2,3},{3,0},{4,5},{5,6},{6,7},{7,4},{8,9},{9,10},{10,1... | collective-permute-start | bytes 116 | tf_op jit(solution)/shard_map/ppermute | solution.py:14
  16.3 2.3 %collective-permute-start.15 = (s32[9]{0:T(128)}, s32[9]{0:T(128)S(1)}, u32[]{:S(2)}, u32[]{:S(2)}) collective-permute-start(s32[9]{0:T(128)} %bitcast.81), channel_id=1, source_target_pairs={{0,2},{1,3},{2,0},{3,1},{4,6},{5,7},{6,4},{7,5},{8,10},{9,11},{10,... | collective-permute-start | bytes 116 | tf_op jit(solution)/shard_map/ppermute | solution.py:14
  19.8 1.7 %collective-permute-start.16 = (s32[9]{0:T(128)}, s32[9]{0:T(128)S(1)}, u32[]{:S(2)}, u32[]{:S(2)}) collective-permute-start(s32[9]{0:T(128)} %bitcast.82), channel_id=1, source_target_pairs={{0,3},{1,0},{2,1},{3,2},{4,7},{5,4},{6,5},{7,6},{8,11},{9,8},{10,9... | collective-permute-start | bytes 116 | tf_op jit(solution)/shard_map/ppermute | solution.py:14
  22.6 5.7 %collective-permute-start.11 = (bf16[9,4096]{1,0:T(8,128)(2,1)}, bf16[9,4096]{1,0:T(8,128)(2,1)S(1)}, u32[]{:S(2)}, u32[]{:S(2)}) collective-permute-start(bf16[9,4096]{1,0:T(8,128)(2,1)} %bitcast.10), channel_id=1, source_target_pairs={{0,20},{4,24},{8,28},{12,0},{16,4},{20,8},{24,12},{28,16},{1,21},{... | collective-permute-start | bytes 221192 | tf_op jit(solution)/shard_map/ppermute | solution.py:14
  31.0 1.4 %collective-permute-start.17 = (bf16[9,4096]{1,0:T(8,128)(2,1)}, bf16[9,4096]{1,0:T(8,128)(2,1)}, u32[]{:S(2)}, u32[]{:S(2)}) collective-permute-start(bf16[9,4096]{1,0:T(8,128)(2,1)} %bitcast.10), channel_id=1, source_target_pairs={{0,1},{1,2},{2,3},{3,0},{4,5},{5,6},{6,7},{7,4},{8,9},{9,10},{10,1... | collective-permute-start | bytes 221192 | tf_op jit(solution)/shard_map/ppermute | solution.py:14
  32.4 2.9 %collective-permute-start.18 = (bf16[9,4096]{1,0:T(8,128)(2,1)}, bf16[9,4096]{1,0:T(8,128)(2,1)}, u32[]{:S(2)}, u32[]{:S(2)}) collective-permute-start(bf16[9,4096]{1,0:T(8,128)(2,1)} %bitcast.10), channel_id=1, source_target_pairs={{0,2},{1,3},{2,0},{3,1},{4,6},{5,7},{6,4},{7,5},{8,10},{9,11},{10,... | collective-permute-start | bytes 221192 | tf_op jit(solution)/shard_map/ppermute | solution.py:14
  35.3 1.5 %collective-permute-start.19 = (bf16[9,4096]{1,0:T(8,128)(2,1)}, bf16[9,4096]{1,0:T(8,128)(2,1)}, u32[]{:S(2)}, u32[]{:S(2)}) collective-permute-start(bf16[9,4096]{1,0:T(8,128)(2,1)} %bitcast.10), channel_id=1, source_target_pairs={{0,3},{1,0},{2,1},{3,2},{4,7},{5,4},{6,5},{7,6},{8,11},{9,8},{10,9... | collective-permute-start | bytes 221192 | tf_op jit(solution)/shard_map/ppermute | solution.py:14
  37.1 1.8 %scatter_custom_fusion = bf16[144,4096]{1,0:T(8,128)(2,1)S(1)} fusion(s32[72]{0:T(128)S(1)} %fusion.14, bf16[72,4096]{1,0:T(8,128)(2,1)S(1)} %reshape.417, bf16[]{:T(256)} %constant.87.clone.1), kind=kCustom, calls=%fused_computation.6 | custom fusion | bytes 1179650 | tf_op jit(solution)/shard_map/scatter | solution.py:61
  38.9 2.6 %reshape.397 = bf16[6,24,64,64]{3,2,1,0:T(8,128)(2,1)S(1)} reshape(bf16[144,4096]{1,0:T(8,128)(2,1)S(1)} %scatter_custom_fusion) | data formatting | bytes 2359296 | tf_op jit(solution)/shard_map/reshape | solution.py:65
  41.5 3.0 %copy.9 = bf16[6,64,24,64]{3,2,1,0:T(8,128)(2,1)} copy(bf16[6,64,24,64]{3,1,2,0:T(8,128)(2,1)S(1)} %bitcast.65) | data formatting | bytes 2359296 | tf_op jit(solution)/shard_map/transpose | solution.py:66
  44.5 3.4 %reshape.398 = bf16[384,1536]{1,0:T(8,128)(2,1)S(1)} reshape(bf16[6,64,24,64]{3,2,1,0:T(8,128)(2,1)} %copy.9) | data formatting | bytes 2359296 | tf_op jit(solution)/shard_map/reshape | solution.py:67
  50.5 1.3 %reshape.400 = bf16[24,3,64,64]{3,2,1,0:T(8,128)(2,1)S(1)} reshape(bf16[72,4096]{1,0:T(8,128)(2,1)S(1)} %scatter_custom_fusion.1) | data formatting | bytes 1179648 | tf_op jit(solution)/shard_map/reshape | solution.py:47
  51.8 1.3 %copy.10 = bf16[24,64,3,64]{1,0,3,2:T(8,128)(2,1)S(1)} copy(bf16[24,64,3,64]{3,1,2,0:T(8,128)(2,1)S(1)} %bitcast.66) | data formatting | bytes 1179648 | tf_op jit(solution)/shard_map/transpose | solution.py:48
  55.2 2.9 %collective-permute-start.21 = (f32[384,192]{0,1:T(8,128)S(1)}, f32[384,192]{0,1:T(8,128)S(1)}, u32[]{:S(2)}, u32[]{:S(2)}) collective-permute-start(f32[384,192]{0,1:T(8,128)S(1)} %fusion.17), channel_id=1, source_target_pairs={{0,2},{1,3},{2,0},{3,1},{4,6},{5,7},{6,4},{7,5},{8,10},{9,11},{10,... | collective-permute-start | bytes 884744 | tf_op jit(solution)/shard_map/ppermute | solution.py:14
  58.1 1.4 %collective-permute-start.22 = (f32[384,192]{0,1:T(8,128)S(1)}, f32[384,192]{0,1:T(8,128)S(1)}, u32[]{:S(2)}, u32[]{:S(2)}) collective-permute-start(f32[384,192]{0,1:T(8,128)S(1)} %fusion.17), channel_id=1, source_target_pairs={{0,3},{1,0},{2,1},{3,2},{4,7},{5,4},{6,5},{7,6},{8,11},{9,8},{10,9... | collective-permute-start | bytes 884744 | tf_op jit(solution)/shard_map/ppermute | solution.py:14
  59.5 1.2 %collective-permute-done.20 = f32[384,192]{0,1:T(8,128)S(1)} collective-permute-done((f32[384,192]{0,1:T(8,128)S(1)}, f32[384,192]{0,1:T(8,128)S(1)}, u32[]{:S(2)}, u32[]{:S(2)}) %collective-permute-start.20) | collective-permute-done | bytes 294944 | tf_op jit(solution)/shard_map/ppermute | solution.py:14
  60.7 18.6 %collective-permute-done.21 = f32[384,192]{0,1:T(8,128)S(1)} collective-permute-done((f32[384,192]{0,1:T(8,128)S(1)}, f32[384,192]{0,1:T(8,128)S(1)}, u32[]{:S(2)}, u32[]{:S(2)}) %collective-permute-start.21) | collective-permute-done | bytes 294944 | tf_op jit(solution)/shard_map/ppermute | solution.py:14
  79.3 5.2 %collective-permute-done.22 = f32[384,192]{0,1:T(8,128)S(1)} collective-permute-done((f32[384,192]{0,1:T(8,128)S(1)}, f32[384,192]{0,1:T(8,128)S(1)}, u32[]{:S(2)}, u32[]{:S(2)}) %collective-permute-start.22) | collective-permute-done | bytes 294944 | tf_op jit(solution)/shard_map/ppermute | solution.py:14
  84.7 1.3 %fusion = f32[384,192]{0,1:T(8,128)S(1)} fusion(bf16[384,1536]{1,0:T(8,128)(2,1)S(1)} %reshape.398, f32[1536,192]{0,1:T(8,128)S(1)} %bitcast.67, f32[384,192]{0,1:T(8,128)S(1)} %fusion.17), kind=kOutput, calls=%fused_computation.5 | convolution fusion | flops 1359175680 | bytes 2949120 | tf_op jit(solution)/shard_map/dot_general | solution.py:72
  (77 shorter events, 18.6 us)
Async XLA Ops:
  0.0 8.0 %collective-permute-start = (s32[9]{0:T(128)}, s32[9]{0:T(128)S(1)}, u32[]{:S(2)}, u32[]{:S(2)}) collective-permute-start(s32[9]{0:T(128)} %bitcast.73), channel_id=1, source_target_pairs={{0,4},{4,8},{8,12},{12,16},{16,20},{20,24},{24,28},{28,0},{1,5},{5... | collective-permute-start | bytes 116 | tf_op jit(solution)/shard_map/ppermute | solution.py:14
  1.8 7.5 %collective-permute-start.1 = (s32[9]{0:T(128)}, s32[9]{0:T(128)S(1)}, u32[]{:S(2)}, u32[]{:S(2)}) collective-permute-start(s32[9]{0:T(128)} %bitcast.74), channel_id=1, source_target_pairs={{0,8},{4,12},{8,16},{12,20},{16,24},{20,28},{24,0},{28,4},{1,9},{5... | collective-permute-start | bytes 116 | tf_op jit(solution)/shard_map/ppermute | solution.py:14
  3.0 6.3 %collective-permute-start.2 = (s32[9]{0:T(128)}, s32[9]{0:T(128)S(1)}, u32[]{:S(2)}, u32[]{:S(2)}) collective-permute-start(s32[9]{0:T(128)} %bitcast.75), channel_id=1, source_target_pairs={{0,12},{4,16},{8,20},{12,24},{16,28},{20,0},{24,4},{28,8},{1,13},{... | collective-permute-start | bytes 116 | tf_op jit(solution)/shard_map/ppermute | solution.py:14
  3.3 7.8 %collective-permute-start.3 = (s32[9]{0:T(128)}, s32[9]{0:T(128)S(1)}, u32[]{:S(2)}, u32[]{:S(2)}) collective-permute-start(s32[9]{0:T(128)} %bitcast.76), channel_id=1, source_target_pairs={{0,16},{4,20},{8,24},{12,28},{16,0},{20,4},{24,8},{28,12},{1,17},{... | collective-permute-start | bytes 116 | tf_op jit(solution)/shard_map/ppermute | solution.py:14
  3.5 8.7 %collective-permute-start.4 = (s32[9]{0:T(128)}, s32[9]{0:T(128)S(1)}, u32[]{:S(2)}, u32[]{:S(2)}) collective-permute-start(s32[9]{0:T(128)} %bitcast.77), channel_id=1, source_target_pairs={{0,20},{4,24},{8,28},{12,0},{16,4},{20,8},{24,12},{28,16},{1,21},{... | collective-permute-start | bytes 116 | tf_op jit(solution)/shard_map/ppermute | solution.py:14
  8.0 4.1 %collective-permute-start.5 = (s32[9]{0:T(128)}, s32[9]{0:T(128)S(1)}, u32[]{:S(2)}, u32[]{:S(2)}) collective-permute-start(s32[9]{0:T(128)} %bitcast.78), channel_id=1, source_target_pairs={{0,24},{4,28},{8,0},{12,4},{16,8},{20,12},{24,16},{28,20},{1,25},{... | collective-permute-start | bytes 116 | tf_op jit(solution)/shard_map/ppermute | solution.py:14
  9.3 4.2 %collective-permute-start.6 = (s32[9]{0:T(128)}, s32[9]{0:T(128)S(1)}, u32[]{:S(2)}, u32[]{:S(2)}) collective-permute-start(s32[9]{0:T(128)} %bitcast.79), channel_id=1, source_target_pairs={{0,28},{4,0},{8,4},{12,8},{16,12},{20,16},{24,20},{28,24},{1,29},{... | collective-permute-start | bytes 116 | tf_op jit(solution)/shard_map/ppermute | solution.py:14
  9.3 21.1 %collective-permute-start.7 = (bf16[9,4096]{1,0:T(8,128)(2,1)}, bf16[9,4096]{1,0:T(8,128)(2,1)S(1)}, u32[]{:S(2)}, u32[]{:S(2)}) collective-permute-start(bf16[9,4096]{1,0:T(8,128)(2,1)} %bitcast.10), channel_id=1, source_target_pairs={{0,4},{4,8},{8,12},{12,16},{16,20},{20,24},{24,28},{28,0},{1,5},{5... | collective-permute-start | bytes 221192 | tf_op jit(solution)/shard_map/ppermute | solution.py:14
  11.1 19.5 %collective-permute-start.8 = (bf16[9,4096]{1,0:T(8,128)(2,1)}, bf16[9,4096]{1,0:T(8,128)(2,1)S(1)}, u32[]{:S(2)}, u32[]{:S(2)}) collective-permute-start(bf16[9,4096]{1,0:T(8,128)(2,1)} %bitcast.10), channel_id=1, source_target_pairs={{0,8},{4,12},{8,16},{12,20},{16,24},{20,28},{24,0},{28,4},{1,9},{5... | collective-permute-start | bytes 221192 | tf_op jit(solution)/shard_map/ppermute | solution.py:14
  12.2 18.8 %collective-permute-start.9 = (bf16[9,4096]{1,0:T(8,128)(2,1)}, bf16[9,4096]{1,0:T(8,128)(2,1)S(1)}, u32[]{:S(2)}, u32[]{:S(2)}) collective-permute-start(bf16[9,4096]{1,0:T(8,128)(2,1)} %bitcast.10), channel_id=1, source_target_pairs={{0,12},{4,16},{8,20},{12,24},{16,28},{20,0},{24,4},{28,8},{1,13},{... | collective-permute-start | bytes 221192 | tf_op jit(solution)/shard_map/ppermute | solution.py:14
  12.2 20.2 %collective-permute-start.10 = (bf16[9,4096]{1,0:T(8,128)(2,1)}, bf16[9,4096]{1,0:T(8,128)(2,1)S(1)}, u32[]{:S(2)}, u32[]{:S(2)}) collective-permute-start(bf16[9,4096]{1,0:T(8,128)(2,1)} %bitcast.10), channel_id=1, source_target_pairs={{0,16},{4,20},{8,24},{12,28},{16,0},{20,4},{24,8},{28,12},{1,17},{... | collective-permute-start | bytes 221192 | tf_op jit(solution)/shard_map/ppermute | solution.py:14
  13.5 2.8 %collective-permute-start.14 = (s32[9]{0:T(128)}, s32[9]{0:T(128)S(1)}, u32[]{:S(2)}, u32[]{:S(2)}) collective-permute-start(s32[9]{0:T(128)} %bitcast.80), channel_id=1, source_target_pairs={{0,1},{1,2},{2,3},{3,0},{4,5},{5,6},{6,7},{7,4},{8,9},{9,10},{10,1... | collective-permute-start | bytes 116 | tf_op jit(solution)/shard_map/ppermute | solution.py:14
  16.3 3.5 %collective-permute-start.15 = (s32[9]{0:T(128)}, s32[9]{0:T(128)S(1)}, u32[]{:S(2)}, u32[]{:S(2)}) collective-permute-start(s32[9]{0:T(128)} %bitcast.81), channel_id=1, source_target_pairs={{0,2},{1,3},{2,0},{3,1},{4,6},{5,7},{6,4},{7,5},{8,10},{9,11},{10,... | collective-permute-start | bytes 116 | tf_op jit(solution)/shard_map/ppermute | solution.py:14
  19.8 2.8 %collective-permute-start.16 = (s32[9]{0:T(128)}, s32[9]{0:T(128)S(1)}, u32[]{:S(2)}, u32[]{:S(2)}) collective-permute-start(s32[9]{0:T(128)} %bitcast.82), channel_id=1, source_target_pairs={{0,3},{1,0},{2,1},{3,2},{4,7},{5,4},{6,5},{7,6},{8,11},{9,8},{10,9... | collective-permute-start | bytes 116 | tf_op jit(solution)/shard_map/ppermute | solution.py:14
  22.6 12.6 %collective-permute-start.11 = (bf16[9,4096]{1,0:T(8,128)(2,1)}, bf16[9,4096]{1,0:T(8,128)(2,1)S(1)}, u32[]{:S(2)}, u32[]{:S(2)}) collective-permute-start(bf16[9,4096]{1,0:T(8,128)(2,1)} %bitcast.10), channel_id=1, source_target_pairs={{0,20},{4,24},{8,28},{12,0},{16,4},{20,8},{24,12},{28,16},{1,21},{... | collective-permute-start | bytes 221192 | tf_op jit(solution)/shard_map/ppermute | solution.py:14
  30.5 6.4 %collective-permute-start.12 = (bf16[9,4096]{1,0:T(8,128)(2,1)}, bf16[9,4096]{1,0:T(8,128)(2,1)S(1)}, u32[]{:S(2)}, u32[]{:S(2)}) collective-permute-start(bf16[9,4096]{1,0:T(8,128)(2,1)} %bitcast.10), channel_id=1, source_target_pairs={{0,24},{4,28},{8,0},{12,4},{16,8},{20,12},{24,16},{28,20},{1,25},{... | collective-permute-start | bytes 221192 | tf_op jit(solution)/shard_map/ppermute | solution.py:14
  30.5 6.3 %collective-permute-start.13 = (bf16[9,4096]{1,0:T(8,128)(2,1)}, bf16[9,4096]{1,0:T(8,128)(2,1)S(1)}, u32[]{:S(2)}, u32[]{:S(2)}) collective-permute-start(bf16[9,4096]{1,0:T(8,128)(2,1)} %bitcast.10), channel_id=1, source_target_pairs={{0,28},{4,0},{8,4},{12,8},{16,12},{20,16},{24,20},{28,24},{1,29},{... | collective-permute-start | bytes 221192 | tf_op jit(solution)/shard_map/ppermute | solution.py:14
  31.0 16.9 %collective-permute-start.17 = (bf16[9,4096]{1,0:T(8,128)(2,1)}, bf16[9,4096]{1,0:T(8,128)(2,1)}, u32[]{:S(2)}, u32[]{:S(2)}) collective-permute-start(bf16[9,4096]{1,0:T(8,128)(2,1)} %bitcast.10), channel_id=1, source_target_pairs={{0,1},{1,2},{2,3},{3,0},{4,5},{5,6},{6,7},{7,4},{8,9},{9,10},{10,1... | collective-permute-start | bytes 221192 | tf_op jit(solution)/shard_map/ppermute | solution.py:14
  32.4 15.6 %collective-permute-start.18 = (bf16[9,4096]{1,0:T(8,128)(2,1)}, bf16[9,4096]{1,0:T(8,128)(2,1)}, u32[]{:S(2)}, u32[]{:S(2)}) collective-permute-start(bf16[9,4096]{1,0:T(8,128)(2,1)} %bitcast.10), channel_id=1, source_target_pairs={{0,2},{1,3},{2,0},{3,1},{4,6},{5,7},{6,4},{7,5},{8,10},{9,11},{10,... | collective-permute-start | bytes 221192 | tf_op jit(solution)/shard_map/ppermute | solution.py:14
  35.3 12.7 %collective-permute-start.19 = (bf16[9,4096]{1,0:T(8,128)(2,1)}, bf16[9,4096]{1,0:T(8,128)(2,1)}, u32[]{:S(2)}, u32[]{:S(2)}) collective-permute-start(bf16[9,4096]{1,0:T(8,128)(2,1)} %bitcast.10), channel_id=1, source_target_pairs={{0,3},{1,0},{2,1},{3,2},{4,7},{5,4},{6,5},{7,6},{8,11},{9,8},{10,9... | collective-permute-start | bytes 221192 | tf_op jit(solution)/shard_map/ppermute | solution.py:14
  53.8 5.7 %copy-start = (s32[1,13]{1,0:T(1,128)S(1)}, s32[1,13]{1,0:T(1,128)}, u32[]{:S(2)}) copy-start(s32[1,13]{1,0:T(1,128)} %param.5) | copy-start | bytes 160
  54.4 6.4 %collective-permute-start.20 = (f32[384,192]{0,1:T(8,128)S(1)}, f32[384,192]{0,1:T(8,128)S(1)}, u32[]{:S(2)}, u32[]{:S(2)}) collective-permute-start(f32[384,192]{0,1:T(8,128)S(1)} %fusion.17), channel_id=1, source_target_pairs={{0,1},{1,2},{2,3},{3,0},{4,5},{5,6},{6,7},{7,4},{8,9},{9,10},{10,1... | collective-permute-start | bytes 884744 | tf_op jit(solution)/shard_map/ppermute | solution.py:14
  55.2 24.1 %collective-permute-start.21 = (f32[384,192]{0,1:T(8,128)S(1)}, f32[384,192]{0,1:T(8,128)S(1)}, u32[]{:S(2)}, u32[]{:S(2)}) collective-permute-start(f32[384,192]{0,1:T(8,128)S(1)} %fusion.17), channel_id=1, source_target_pairs={{0,2},{1,3},{2,0},{3,1},{4,6},{5,7},{6,4},{7,5},{8,10},{9,11},{10,... | collective-permute-start | bytes 884744 | tf_op jit(solution)/shard_map/ppermute | solution.py:14
  58.1 26.4 %collective-permute-start.22 = (f32[384,192]{0,1:T(8,128)S(1)}, f32[384,192]{0,1:T(8,128)S(1)}, u32[]{:S(2)}, u32[]{:S(2)}) collective-permute-start(f32[384,192]{0,1:T(8,128)S(1)} %fusion.17), channel_id=1, source_target_pairs={{0,3},{1,0},{2,1},{3,2},{4,7},{5,4},{6,5},{7,6},{8,11},{9,8},{10,9... | collective-permute-start | bytes 884744 | tf_op jit(solution)/shard_map/ppermute | solution.py:14

commit v3 on v2

--- a/solution.py
+++ b/solution.py
@@ -28,13 +28,19 @@
     height = rows_dev * block_edge
     row_idx = lax.axis_index("row")
     col_idx = lax.axis_index("col")
-    own = (p_blocks[0], p_slots[0])
+    id_row = jnp.zeros((1, area), jnp.bfloat16)
+    id_row = id_row.at[0, :capacity].set(p_slots[0].astype(jnp.bfloat16))
+    own = jnp.concatenate([p_blocks[0], id_row], axis=0)
+
+    def unpack(payloads):
+        ids = payloads[:, capacity, :capacity].astype(jnp.int32)
+        return payloads[:, :capacity], ids
 
     def shift_order(block):
         owner = block // rows_dev
         return ((row_idx - owner) % n_row) * rows_dev + block % rows_dev
 
-    down_blocks, down_ids = shifted_copies(own, "row", n_row)
+    down_blocks, down_ids = unpack(shifted_copies(own, "row", n_row))
     down_row = jnp.arange(n_row, dtype=jnp.int32)[:, None] * rows_dev + down_ids // COLS_DEV
     down_index = jnp.where(
         down_ids < cells, down_row * COLS_DEV + down_ids % COLS_DEV, blocks_total * COLS_DEV
@@ -49,7 +55,7 @@
         .reshape(blocks_total * block_edge, width)
     )
 
-    across_blocks, across_ids = shifted_copies(own, "col", n_col)
+    across_blocks, across_ids = unpack(shifted_copies(own, "col", n_col))
     across_src = (col_idx - jnp.arange(n_col, dtype=jnp.int32)[:, None]) % n_col
     across_col = shift_order(across_src * COLS_DEV + across_ids % COLS_DEV)
     across_index = jnp.where(

time: 88.5 us -> 82.1 us (0.928)
  the two profiles are of different devices: /device:TPU:9 before, /device:TPU:0 now
where the time goes in v3:
time: 82.1 us; the launch traced here: 81.9 us
  waiting for transfers between devices  35.2 us (43%)
  starting transfers between devices  20.3 us (25%)
  local copies, waits for them, and re-layouts  19.1 us (23%)
  other arithmetic  5.29 us (6%)
  matrix products  1.83 us (2%)
    ppermute x13, waiting for transfers between devices, shifted_copies(): pieces.append(lax.ppermute(value, axis, pairs))  35.2 us
    ppermute x13, starting transfers between devices, shifted_copies(): pieces.append(lax.ppermute(value, axis, pairs))  20.3 us
    reshape x1, local copies, waits for them, and re-layouts, on_device(): row_panel = row_grid.reshape(rows_dev, blocks_total, block_edge, block_ed...  3.5 us
    transpose x1, local copies, waits for them, and re-layouts, on_device(): row_panel = row_grid.reshape(rows_dev, blocks_total, block_edge, block_ed...  2.94 us
    reshape x1, local copies, waits for them, and re-layouts, on_device(): row_grid.reshape(rows_dev, blocks_total, block_edge, block_edge)  2.57 us
    another operation x2, other arithmetic  1.94 us
    scatter x1, local copies, waits for them, and re-layouts, on_device(): row_grid.at[across_index.reshape(-1)]  1.8 us
  transfers between devices with their start and end apart: 13, of which 5 were waited for; matrix products, arithmetic and copies ran while one was open for 2% of the time, Pallas kernels for 0%

profile of v3, /device:TPU:0, one launch (start us, length us, event | category | flops | bytes accessed | tf_op | source)
XLA Modules:
  0.0 81.9 jit_solution(11359194563404501390)
XLA Ops:
  0.6 1.3 %broadcast_select_fusion = bf16[1,9]{1,0:T(2,128)(2,1)S(1)} fusion(pred[]{:T(512)} %compare_reduce_fusion.4, s32[1,9]{1,0:T(1,128)} %param.6), kind=kLoop, calls=%fused_computation.53 | loop fusion | flops 18 | bytes 55 | tf_op jit(solution)/shard_map/select.11
  1.9 0.9 %constant_dynamic-update-slice_fusion = (bf16[8,10,4096]{2,1,0:T(8,128)(2,1)S(1)}, bf16[10,4096]{1,0:T(8,128)(2,1)S(1)}) fusion(bf16[1,9]{1,0:T(2,128)(2,1)S(1)} %broadcast_select_fusion, bf16[9,4096]{1,0:T(8,128)(2,1)} %bitcast.74), kind=kLoop, calls=%fused_computation.24 | loop fusion | flops 245759 | bytes 335890
  3.4 2.5 %collective-permute-start.1 = (bf16[10,4096]{1,0:T(8,128)(2,1)S(1)}, bf16[10,4096]{1,0:T(8,128)(2,1)S(1)}, u32[]{:S(2)}, u32[]{:S(2)}) collective-permute-start(bf16[10,4096]{1,0:T(8,128)(2,1)S(1)} %get-tuple-element.27), channel_id=1, source_target_pairs={{0,8},{4,12},{8,16},{12,20},{16,24},{20,28},{24,0},{28,4},{1,9},{5... | collective-permute-start | bytes 245768 | tf_op jit(solution)/shard_map/ppermute | solution.py:14
  6.0 2.4 %collective-permute-start.2 = (bf16[10,4096]{1,0:T(8,128)(2,1)S(1)}, bf16[10,4096]{1,0:T(8,128)(2,1)S(1)}, u32[]{:S(2)}, u32[]{:S(2)}) collective-permute-start(bf16[10,4096]{1,0:T(8,128)(2,1)S(1)} %get-tuple-element.27), channel_id=1, source_target_pairs={{0,12},{4,16},{8,20},{12,24},{16,28},{20,0},{24,4},{28,8},{1,13},{... | collective-permute-start | bytes 245768 | tf_op jit(solution)/shard_map/ppermute | solution.py:14
  9.1 1.2 %fusion.18 = s32[13]{0:T(128)} fusion(s32[1,13]{1,0:T(1,128)} %param.7), kind=kLoop, calls=%fused_computation.65 | loop fusion | flops 52 | bytes 104 | tf_op jit(solution)/shard_map/select_n | solution.py:88
  10.4 1.6 %collective-permute-start.5 = (bf16[10,4096]{1,0:T(8,128)(2,1)S(1)}, bf16[10,4096]{1,0:T(8,128)(2,1)S(1)}, u32[]{:S(2)}, u32[]{:S(2)}) collective-permute-start(bf16[10,4096]{1,0:T(8,128)(2,1)S(1)} %get-tuple-element.27), channel_id=1, source_target_pairs={{0,24},{4,28},{8,0},{12,4},{16,8},{20,12},{24,16},{28,20},{1,25},{... | collective-permute-start | bytes 245768 | tf_op jit(solution)/shard_map/ppermute | solution.py:14
  12.0 2.5 %collective-permute-start.6 = (bf16[10,4096]{1,0:T(8,128)(2,1)S(1)}, bf16[10,4096]{1,0:T(8,128)(2,1)S(1)}, u32[]{:S(2)}, u32[]{:S(2)}) collective-permute-start(bf16[10,4096]{1,0:T(8,128)(2,1)S(1)} %get-tuple-element.27), channel_id=1, source_target_pairs={{0,28},{4,0},{8,4},{12,8},{16,12},{20,16},{24,20},{28,24},{1,29},{... | collective-permute-start | bytes 245768 | tf_op jit(solution)/shard_map/ppermute | solution.py:14
  14.5 1.3 %collective-permute-done.2 = bf16[10,4096]{1,0:T(8,128)(2,1)S(1)} collective-permute-done((bf16[10,4096]{1,0:T(8,128)(2,1)S(1)}, bf16[10,4096]{1,0:T(8,128)(2,1)S(1)}, u32[]{:S(2)}, u32[]{:S(2)}) %collective-permute-start.2) | collective-permute-done | bytes 81952 | tf_op jit(solution)/shard_map/ppermute | solution.py:14
  15.9 4.4 %collective-permute-start.9 = (bf16[10,4096]{1,0:T(8,128)(2,1)S(1)}, bf16[10,4096]{1,0:T(8,128)(2,1)S(1)}, u32[]{:S(2)}, u32[]{:S(2)}) collective-permute-start(bf16[10,4096]{1,0:T(8,128)(2,1)S(1)} %get-tuple-element.27), channel_id=1, source_target_pairs={{0,3},{1,0},{2,1},{3,2},{4,7},{5,4},{6,5},{7,6},{8,11},{9,8},{10,9... | collective-permute-start | bytes 245768 | tf_op jit(solution)/shard_map/ppermute | solution.py:14
  20.4 1.0 %collective-permute-start.7 = (bf16[10,4096]{1,0:T(8,128)(2,1)S(1)}, bf16[10,4096]{1,0:T(8,128)(2,1)S(1)}, u32[]{:S(2)}, u32[]{:S(2)}) collective-permute-start(bf16[10,4096]{1,0:T(8,128)(2,1)S(1)} %get-tuple-element.27), channel_id=1, source_target_pairs={{0,1},{1,2},{2,3},{3,0},{4,5},{5,6},{6,7},{7,4},{8,9},{9,10},{10,1... | collective-permute-start | bytes 245768 | tf_op jit(solution)/shard_map/ppermute | solution.py:14
  21.6 1.9 %collective-permute-done.9 = bf16[10,4096]{1,0:T(8,128)(2,1)S(1)} collective-permute-done((bf16[10,4096]{1,0:T(8,128)(2,1)S(1)}, bf16[10,4096]{1,0:T(8,128)(2,1)S(1)}, u32[]{:S(2)}, u32[]{:S(2)}) %collective-permute-start.9) | collective-permute-done | bytes 81952 | tf_op jit(solution)/shard_map/ppermute | solution.py:14
  23.5 7.6 %collective-permute-done.8 = bf16[10,4096]{1,0:T(8,128)(2,1)S(1)} collective-permute-done((bf16[10,4096]{1,0:T(8,128)(2,1)S(1)}, bf16[10,4096]{1,0:T(8,128)(2,1)S(1)}, u32[]{:S(2)}, u32[]{:S(2)}) %collective-permute-start.8) | collective-permute-done | bytes 81952 | tf_op jit(solution)/shard_map/ppermute | solution.py:14
  32.7 1.8 %scatter_custom_fusion = bf16[144,4096]{1,0:T(8,128)(2,1)S(1)} fusion(s32[72]{0:T(128)S(1)} %fusion.16, bf16[72,4096]{1,0:T(8,128)(2,1)S(1)} %reshape.417, bf16[]{:T(256)} %constant.114.clone.1), kind=kCustom, calls=%fused_computation.6 | custom fusion | bytes 1179650 | tf_op jit(solution)/shard_map/scatter | solution.py:67
  34.5 2.6 %reshape.397 = bf16[6,24,64,64]{3,2,1,0:T(8,128)(2,1)S(1)} reshape(bf16[144,4096]{1,0:T(8,128)(2,1)S(1)} %scatter_custom_fusion) | data formatting | bytes 2359296 | tf_op jit(solution)/shard_map/reshape | solution.py:71
  37.0 2.9 %copy.9 = bf16[6,64,24,64]{3,2,1,0:T(8,128)(2,1)} copy(bf16[6,64,24,64]{3,1,2,0:T(8,128)(2,1)S(1)} %bitcast.57) | data formatting | bytes 2359296 | tf_op jit(solution)/shard_map/transpose | solution.py:72
  40.0 3.5 %reshape.398 = bf16[384,1536]{1,0:T(8,128)(2,1)S(1)} reshape(bf16[6,64,24,64]{3,2,1,0:T(8,128)(2,1)} %copy.9) | data formatting | bytes 2359296 | tf_op jit(solution)/shard_map/reshape | solution.py:73
  44.0 1.2 %scatter_custom_fusion.1 = bf16[72,4096]{1,0:T(8,128)(2,1)S(1)} fusion(s32[36]{0:T(128)S(1)} %fusion.17, bf16[36,4096]{1,0:T(8,128)(2,1)S(1)} %reshape.425, bf16[]{:T(256)} %constant.114.clone.1), kind=kCustom, calls=%fused_computation.11 | custom fusion | bytes 589826 | tf_op jit(solution)/shard_map/scatter | solution.py:49
  45.2 1.3 %reshape.400 = bf16[24,3,64,64]{3,2,1,0:T(8,128)(2,1)S(1)} reshape(bf16[72,4096]{1,0:T(8,128)(2,1)S(1)} %scatter_custom_fusion.1) | data formatting | bytes 1179648 | tf_op jit(solution)/shard_map/reshape | solution.py:53
  46.5 1.3 %copy.10 = bf16[24,64,3,64]{1,0,3,2:T(8,128)(2,1)S(1)} copy(bf16[24,64,3,64]{3,1,2,0:T(8,128)(2,1)S(1)} %bitcast.58) | data formatting | bytes 1179648 | tf_op jit(solution)/shard_map/transpose | solution.py:54
  49.8 2.0 %collective-permute-start.11 = (f32[384,192]{0,1:T(8,128)S(1)}, f32[384,192]{0,1:T(8,128)S(1)}, u32[]{:S(2)}, u32[]{:S(2)}) collective-permute-start(f32[384,192]{0,1:T(8,128)S(1)} %fusion.20), channel_id=1, source_target_pairs={{0,2},{1,3},{2,0},{3,1},{4,6},{5,7},{6,4},{7,5},{8,10},{9,11},{10,... | collective-permute-start | bytes 884744 | tf_op jit(solution)/shard_map/ppermute | solution.py:14
  51.8 1.9 %collective-permute-start.10 = (f32[384,192]{0,1:T(8,128)S(1)}, f32[384,192]{0,1:T(8,128)S(1)}, u32[]{:S(2)}, u32[]{:S(2)}) collective-permute-start(f32[384,192]{0,1:T(8,128)S(1)} %fusion.20), channel_id=1, source_target_pairs={{0,1},{1,2},{2,3},{3,0},{4,5},{5,6},{6,7},{7,4},{8,9},{9,10},{10,1... | collective-permute-start | bytes 884744 | tf_op jit(solution)/shard_map/ppermute | solution.py:14
  53.8 3.8 %collective-permute-done.12 = f32[384,192]{0,1:T(8,128)S(1)} collective-permute-done((f32[384,192]{0,1:T(8,128)S(1)}, f32[384,192]{0,1:T(8,128)S(1)}, u32[]{:S(2)}, u32[]{:S(2)}) %collective-permute-start.12) | collective-permute-done | bytes 294944 | tf_op jit(solution)/shard_map/ppermute | solution.py:14
  57.6 20.6 %collective-permute-done.11 = f32[384,192]{0,1:T(8,128)S(1)} collective-permute-done((f32[384,192]{0,1:T(8,128)S(1)}, f32[384,192]{0,1:T(8,128)S(1)}, u32[]{:S(2)}, u32[]{:S(2)}) %collective-permute-start.11) | collective-permute-done | bytes 294944 | tf_op jit(solution)/shard_map/ppermute | solution.py:14
  78.4 1.3 %fusion = f32[384,192]{0,1:T(8,128)S(1)} fusion(bf16[384,1536]{1,0:T(8,128)(2,1)S(1)} %reshape.398, f32[1536,192]{0,1:T(8,128)S(1)} %bitcast.59, f32[384,192]{0,1:T(8,128)S(1)} %fusion.20), kind=kOutput, calls=%fused_computation.5 | convolution fusion | flops 1359175680 | bytes 2949120 | tf_op jit(solution)/shard_map/dot_general | solution.py:78
  (62 shorter events, 8.9 us)
Async XLA Ops:
  2.9 7.6 %collective-permute-start = (bf16[10,4096]{1,0:T(8,128)(2,1)S(1)}, bf16[10,4096]{1,0:T(8,128)(2,1)S(1)}, u32[]{:S(2)}, u32[]{:S(2)}) collective-permute-start(bf16[10,4096]{1,0:T(8,128)(2,1)S(1)} %get-tuple-element.27), channel_id=1, source_target_pairs={{0,4},{4,8},{8,12},{12,16},{16,20},{20,24},{24,28},{28,0},{1,5},{5... | collective-permute-start | bytes 245768 | tf_op jit(solution)/shard_map/ppermute | solution.py:14
  3.4 8.6 %collective-permute-start.1 = (bf16[10,4096]{1,0:T(8,128)(2,1)S(1)}, bf16[10,4096]{1,0:T(8,128)(2,1)S(1)}, u32[]{:S(2)}, u32[]{:S(2)}) collective-permute-start(bf16[10,4096]{1,0:T(8,128)(2,1)S(1)} %get-tuple-element.27), channel_id=1, source_target_pairs={{0,8},{4,12},{8,16},{12,20},{16,24},{20,28},{24,0},{28,4},{1,9},{5... | collective-permute-start | bytes 245768 | tf_op jit(solution)/shard_map/ppermute | solution.py:14
  6.0 9.9 %collective-permute-start.2 = (bf16[10,4096]{1,0:T(8,128)(2,1)S(1)}, bf16[10,4096]{1,0:T(8,128)(2,1)S(1)}, u32[]{:S(2)}, u32[]{:S(2)}) collective-permute-start(bf16[10,4096]{1,0:T(8,128)(2,1)S(1)} %get-tuple-element.27), channel_id=1, source_target_pairs={{0,12},{4,16},{8,20},{12,24},{16,28},{20,0},{24,4},{28,8},{1,13},{... | collective-permute-start | bytes 245768 | tf_op jit(solution)/shard_map/ppermute | solution.py:14
  8.3 11.9 %collective-permute-start.3 = (bf16[10,4096]{1,0:T(8,128)(2,1)S(1)}, bf16[10,4096]{1,0:T(8,128)(2,1)S(1)}, u32[]{:S(2)}, u32[]{:S(2)}) collective-permute-start(bf16[10,4096]{1,0:T(8,128)(2,1)S(1)} %get-tuple-element.27), channel_id=1, source_target_pairs={{0,16},{4,20},{8,24},{12,28},{16,0},{20,4},{24,8},{28,12},{1,17},{... | collective-permute-start | bytes 245768 | tf_op jit(solution)/shard_map/ppermute | solution.py:14
  8.8 11.5 %collective-permute-start.4 = (bf16[10,4096]{1,0:T(8,128)(2,1)S(1)}, bf16[10,4096]{1,0:T(8,128)(2,1)S(1)}, u32[]{:S(2)}, u32[]{:S(2)}) collective-permute-start(bf16[10,4096]{1,0:T(8,128)(2,1)S(1)} %get-tuple-element.27), channel_id=1, source_target_pairs={{0,20},{4,24},{8,28},{12,0},{16,4},{20,8},{24,12},{28,16},{1,21},{... | collective-permute-start | bytes 245768 | tf_op jit(solution)/shard_map/ppermute | solution.py:14
  10.4 11.0 %collective-permute-start.5 = (bf16[10,4096]{1,0:T(8,128)(2,1)S(1)}, bf16[10,4096]{1,0:T(8,128)(2,1)S(1)}, u32[]{:S(2)}, u32[]{:S(2)}) collective-permute-start(bf16[10,4096]{1,0:T(8,128)(2,1)S(1)} %get-tuple-element.27), channel_id=1, source_target_pairs={{0,24},{4,28},{8,0},{12,4},{16,8},{20,12},{24,16},{28,20},{1,25},{... | collective-permute-start | bytes 245768 | tf_op jit(solution)/shard_map/ppermute | solution.py:14
  12.0 9.4 %collective-permute-start.6 = (bf16[10,4096]{1,0:T(8,128)(2,1)S(1)}, bf16[10,4096]{1,0:T(8,128)(2,1)S(1)}, u32[]{:S(2)}, u32[]{:S(2)}) collective-permute-start(bf16[10,4096]{1,0:T(8,128)(2,1)S(1)} %get-tuple-element.27), channel_id=1, source_target_pairs={{0,28},{4,0},{8,4},{12,8},{16,12},{20,16},{24,20},{28,24},{1,29},{... | collective-permute-start | bytes 245768 | tf_op jit(solution)/shard_map/ppermute | solution.py:14
  15.9 7.6 %collective-permute-start.9 = (bf16[10,4096]{1,0:T(8,128)(2,1)S(1)}, bf16[10,4096]{1,0:T(8,128)(2,1)S(1)}, u32[]{:S(2)}, u32[]{:S(2)}) collective-permute-start(bf16[10,4096]{1,0:T(8,128)(2,1)S(1)} %get-tuple-element.27), channel_id=1, source_target_pairs={{0,3},{1,0},{2,1},{3,2},{4,7},{5,4},{6,5},{7,6},{8,11},{9,8},{10,9... | collective-permute-start | bytes 245768 | tf_op jit(solution)/shard_map/ppermute | solution.py:14
  20.2 10.9 %collective-permute-start.8 = (bf16[10,4096]{1,0:T(8,128)(2,1)S(1)}, bf16[10,4096]{1,0:T(8,128)(2,1)S(1)}, u32[]{:S(2)}, u32[]{:S(2)}) collective-permute-start(bf16[10,4096]{1,0:T(8,128)(2,1)S(1)} %get-tuple-element.27), channel_id=1, source_target_pairs={{0,2},{1,3},{2,0},{3,1},{4,6},{5,7},{6,4},{7,5},{8,10},{9,11},{10,... | collective-permute-start | bytes 245768 | tf_op jit(solution)/shard_map/ppermute | solution.py:14
  20.4 10.8 %collective-permute-start.7 = (bf16[10,4096]{1,0:T(8,128)(2,1)S(1)}, bf16[10,4096]{1,0:T(8,128)(2,1)S(1)}, u32[]{:S(2)}, u32[]{:S(2)}) collective-permute-start(bf16[10,4096]{1,0:T(8,128)(2,1)S(1)} %get-tuple-element.27), channel_id=1, source_target_pairs={{0,1},{1,2},{2,3},{3,0},{4,5},{5,6},{6,7},{7,4},{8,9},{9,10},{10,1... | collective-permute-start | bytes 245768 | tf_op jit(solution)/shard_map/ppermute | solution.py:14
  40.0 3.9 %copy-start = (bf16[4,9,4096]{2,1,0:T(8,128)(2,1)S(1)}, bf16[4,9,4096]{2,1,0:T(8,128)(2,1)}, u32[]{:S(2)}) copy-start(bf16[4,9,4096]{2,1,0:T(8,128)(2,1)} %pad_maximum_fusion) | copy-start | bytes 884740
  48.5 5.2 %copy-start.1 = (s32[13]{0:T(128)S(1)}, s32[13]{0:T(128)}, u32[]{:S(2)}) copy-start(s32[13]{0:T(128)} %fusion.18) | copy-start | bytes 160
  48.5 5.2 %copy-start.2 = (s32[1,13]{1,0:T(1,128)S(1)}, s32[1,13]{1,0:T(1,128)}, u32[]{:S(2)}) copy-start(s32[1,13]{1,0:T(1,128)} %param.7) | copy-start | bytes 160
  49.1 8.5 %collective-permute-start.12 = (f32[384,192]{0,1:T(8,128)S(1)}, f32[384,192]{0,1:T(8,128)S(1)}, u32[]{:S(2)}, u32[]{:S(2)}) collective-permute-start(f32[384,192]{0,1:T(8,128)S(1)} %fusion.20), channel_id=1, source_target_pairs={{0,3},{1,0},{2,1},{3,2},{4,7},{5,4},{6,5},{7,6},{8,11},{9,8},{10,9... | collective-permute-start | bytes 884744 | tf_op jit(solution)/shard_map/ppermute | solution.py:14
  49.8 28.3 %collective-permute-start.11 = (f32[384,192]{0,1:T(8,128)S(1)}, f32[384,192]{0,1:T(8,128)S(1)}, u32[]{:S(2)}, u32[]{:S(2)}) collective-permute-start(f32[384,192]{0,1:T(8,128)S(1)} %fusion.20), channel_id=1, source_target_pairs={{0,2},{1,3},{2,0},{3,1},{4,6},{5,7},{6,4},{7,5},{8,10},{9,11},{10,... | collective-permute-start | bytes 884744 | tf_op jit(solution)/shard_map/ppermute | solution.py:14
  51.8 26.3 %collective-permute-start.10 = (f32[384,192]{0,1:T(8,128)S(1)}, f32[384,192]{0,1:T(8,128)S(1)}, u32[]{:S(2)}, u32[]{:S(2)}) collective-permute-start(f32[384,192]{0,1:T(8,128)S(1)} %fusion.20), channel_id=1, source_target_pairs={{0,1},{1,2},{2,3},{3,0},{4,5},{5,6},{6,7},{7,4},{8,9},{9,10},{10,1... | collective-permute-start | bytes 884744 | tf_op jit(solution)/shard_map/ppermute | solution.py:14

commit v4 on v2

v4 whole, which is shorter than its diff:
```python
import jax
import jax.numpy as jnp
from jax import lax
from jax.sharding import PartitionSpec as P

BLK = 64
COLS_DEV = 3


def shifted_copies(value, axis, size):
    pieces = [value]
    for shift in range(1, size):
        pairs = [(i, (i + shift) % size) for i in range(size)]
        pieces.append(lax.ppermute(value, axis, pairs))
    return jnp.stack(pieces)


def on_device(p_blocks, p_slots, out_slots):
    n_row = lax.axis_size("row")
    n_col = lax.axis_size("col")
    block_edge = BLK
    area = block_edge * block_edge
    rows_dev = COLS_DEV * n_col // n_row
    cells = rows_dev * COLS_DEV
    width = COLS_DEV * block_edge
    height = rows_dev * block_edge
    group = rows_dev // COLS_DEV
    row_idx = lax.axis_index("row")
    col_idx = lax.axis_index("col")

    own_ids = p_slots[0]
    grid = jnp.zeros((cells, area), jnp.bfloat16)
    grid = grid.at[jnp.where(own_ids < cells, own_ids, cells)].set(p_blocks[0], mode="drop")
    tile = (
        grid.reshape(rows_dev, COLS_DEV, block_edge, block_edge)
        .transpose(0, 2, 1, 3)
        .reshape(height, width)
    )

    column_panel = shifted_copies(tile, "row", n_row).reshape(n_col, width, width)
    row_pieces = shifted_copies(tile, "col", n_col)
    place = jnp.arange(n_col, dtype=jnp.int32)
    owner = ((row_idx - place // group) % n_row) * group + place % group
    row_panel = row_pieces[(col_idx - owner) % n_col]

    square = jnp.einsum(
        "pab,pbn->an", row_panel, column_panel, preferred_element_type=jnp.float32
    )
    square_panel = shifted_copies(square, "row", n_row).reshape(n_col, width, width)
    cube = jnp.einsum(
        "pab,pbn->an",
        row_panel.astype(jnp.float32),
        square_panel,
        precision=lax.Precision.HIGHEST,
        preferred_element_type=jnp.float32,
    )
    combined = 3.0 * square - 2.0 * cube
    new_grid = combined.reshape(rows_dev, block_edge, COLS_DEV, block_edge).transpose(0, 2, 1, 3)
    new_grid = new_grid.reshape(cells, area)
    out_ids = out_slots[0]
    picked = new_grid[jnp.minimum(out_ids, cells - 1)]
    picked = jnp.where((out_ids < cells)[:, None], picked, jnp.zeros_like(picked))
    return picked[None]


def solution(mesh):
    in_specs = (P("row", "col", None), P("row", "col"), P("row", "col"))
    out_specs = P("row", "col", None)
    return jax.shard_map(
        on_device, mesh=mesh, in_specs=in_specs, out_specs=out_specs, check_vma=False
    )
```

time: 88.5 us -> 72.2 us (0.82)
  the two profiles are of different devices: /device:TPU:9 before, /device:TPU:11 now
where the time goes in v4:
time: 72.2 us; the launch traced here: 72 us
  waiting for transfers between devices  43.8 us (61%)
  starting transfers between devices  13.1 us (18%)
  local copies, waits for them, and re-layouts  10.7 us (15%)
  matrix products  3.15 us (4%)
  other arithmetic  1.01 us (1%)
    ppermute x13, waiting for transfers between devices, shifted_copies(): pieces.append(lax.ppermute(value, axis, pairs))  43.8 us
    ppermute x13, starting transfers between devices, shifted_copies(): pieces.append(lax.ppermute(value, axis, pairs))  13.1 us
    another operation x4, local copies, waits for them, and re-layouts, shifted_copies(): return jnp.stack(pieces)  2.55 us
    reshape x1, local copies, waits for them, and re-layouts, on_device(): shifted_copies(square, 'row', n_row).reshape(n_col, width, width)  1.84 us
    dot_general x1, matrix products, on_device(): jnp.einsum('pab,pbn->an', row_panel, column_panel, preferred_element_type...  1.68 us
    dot_general x1, matrix products, on_device(): jnp.einsum('pab,pbn->an', row_panel.astype(jnp.float32), square_panel, pr...  1.47 us
  transfers between devices with their start and end apart: 13, of which 7 were waited for; matrix products, arithmetic and copies ran while one was open for 3% of the time, Pallas kernels for 0%

profile of v4, /device:TPU:11, one launch (start us, length us, event | category | flops | bytes accessed | tf_op | source)
XLA Modules:
  0.0 72.0 jit_solution(15859661978636782979)
XLA Ops:
  0.0 0.7 fusion.23
  0.9 0.8 %scatter_custom_fusion = bf16[18,4096]{1,0:T(8,128)(2,1)S(1)} fusion(s32[9]{0:T(128)S(1)} %fusion.23, bf16[1,9,4096]{2,1,0:T(8,128)(2,1)S(1)} %copy-done, bf16[]{:T(256)} %constant.63.clone.1), kind=kCustom, calls=%fused_computation.20 | custom fusion | bytes 278530 | tf_op jit(solution)/shard_map/scatter | solution.py:33
  2.6 1.8 %collective-permute-start = (bf16[384,192]{0,1:T(8,128)(2,1)S(1)}, bf16[384,192]{0,1:T(8,128)(2,1)S(1)}, u32[]{:S(2)}, u32[]{:S(2)}) collective-permute-start(bf16[384,192]{0,1:T(8,128)(2,1)S(1)} %reshape.237), channel_id=1, source_target_pairs={{0,4},{4,8},{8,12},{12,16},{16,20},{20,24},{24,28},{28,0},{1,5},{5... | collective-permute-start | bytes 442376 | tf_op jit(solution)/shard_map/ppermute | solution.py:14
  4.4 1.2 %collective-permute-start.1 = (bf16[384,192]{0,1:T(8,128)(2,1)S(1)}, bf16[384,192]{0,1:T(8,128)(2,1)S(1)}, u32[]{:S(2)}, u32[]{:S(2)}) collective-permute-start(bf16[384,192]{0,1:T(8,128)(2,1)S(1)} %reshape.237), channel_id=1, source_target_pairs={{0,8},{4,12},{8,16},{12,20},{16,24},{20,28},{24,0},{28,4},{1,9},{5... | collective-permute-start | bytes 442376 | tf_op jit(solution)/shard_map/ppermute | solution.py:14
  5.6 1.3 %collective-permute-start.7 = (bf16[384,192]{0,1:T(8,128)(2,1)S(1)}, bf16[384,192]{0,1:T(8,128)(2,1)S(1)}, u32[]{:S(2)}, u32[]{:S(2)}) collective-permute-start(bf16[384,192]{0,1:T(8,128)(2,1)S(1)} %reshape.237), channel_id=1, source_target_pairs={{0,1},{1,2},{2,3},{3,0},{4,5},{5,6},{6,7},{7,4},{8,9},{9,10},{10,1... | collective-permute-start | bytes 442376 | tf_op jit(solution)/shard_map/ppermute | solution.py:14
  6.9 1.0 %collective-permute-start.8 = (bf16[384,192]{0,1:T(8,128)(2,1)S(1)}, bf16[384,192]{0,1:T(8,128)(2,1)S(1)}, u32[]{:S(2)}, u32[]{:S(2)}) collective-permute-start(bf16[384,192]{0,1:T(8,128)(2,1)S(1)} %reshape.237), channel_id=1, source_target_pairs={{0,2},{1,3},{2,0},{3,1},{4,6},{5,7},{6,4},{7,5},{8,10},{9,11},{10,... | collective-permute-start | bytes 442376 | tf_op jit(solution)/shard_map/ppermute | solution.py:14
  7.9 1.5 %collective-permute-start.9 = (bf16[384,192]{0,1:T(8,128)(2,1)S(1)}, bf16[384,192]{0,1:T(8,128)(2,1)S(1)}, u32[]{:S(2)}, u32[]{:S(2)}) collective-permute-start(bf16[384,192]{0,1:T(8,128)(2,1)S(1)} %reshape.237), channel_id=1, source_target_pairs={{0,3},{1,0},{2,1},{3,2},{4,7},{5,4},{6,5},{7,6},{8,11},{9,8},{10,9... | collective-permute-start | bytes 442376 | tf_op jit(solution)/shard_map/ppermute | solution.py:14
  9.7 1.4 %collective-permute-done.7 = bf16[384,192]{0,1:T(8,128)(2,1)S(1)} collective-permute-done((bf16[384,192]{0,1:T(8,128)(2,1)S(1)}, bf16[384,192]{0,1:T(8,128)(2,1)S(1)}, u32[]{:S(2)}, u32[]{:S(2)}) %collective-permute-start.7) | collective-permute-done | bytes 147488 | tf_op jit(solution)/shard_map/ppermute | solution.py:14
  11.4 8.4 %collective-permute-done.8 = bf16[384,192]{0,1:T(8,128)(2,1)S(1)} collective-permute-done((bf16[384,192]{0,1:T(8,128)(2,1)S(1)}, bf16[384,192]{0,1:T(8,128)(2,1)S(1)}, u32[]{:S(2)}, u32[]{:S(2)}) %collective-permute-start.8) | collective-permute-done | bytes 147488 | tf_op jit(solution)/shard_map/ppermute | solution.py:14
  20.0 1.5 %collective-permute-done.9 = bf16[384,192]{0,1:T(8,128)(2,1)S(1)} collective-permute-done((bf16[384,192]{0,1:T(8,128)(2,1)S(1)}, bf16[384,192]{0,1:T(8,128)(2,1)S(1)}, u32[]{:S(2)}, u32[]{:S(2)}) %collective-permute-start.9) | collective-permute-done | bytes 147488 | tf_op jit(solution)/shard_map/ppermute | solution.py:14
  22.5 1.4 %reshape.238 = bf16[8,192,192]{1,0,2:T(8,128)(2,1)} reshape(bf16[4,384,192]{1,0,2:T(4,128)(2,1)S(1)} %copy.14) | data formatting | bytes 1179648 | tf_op jit(solution)/shard_map/reshape | solution.py:40
  23.9 0.9 %collective-permute-start.5 = (bf16[384,192]{0,1:T(8,128)(2,1)S(1)}, bf16[384,192]{0,1:T(8,128)(2,1)S(1)}, u32[]{:S(2)}, u32[]{:S(2)}) collective-permute-start(bf16[384,192]{0,1:T(8,128)(2,1)S(1)} %reshape.237), channel_id=1, source_target_pairs={{0,24},{4,28},{8,0},{12,4},{16,8},{20,12},{24,16},{28,20},{1,25},{... | collective-permute-start | bytes 442376 | tf_op jit(solution)/shard_map/ppermute | solution.py:14
  25.1 8.1 %collective-permute-done.4 = bf16[384,192]{0,1:T(8,128)(2,1)S(1)} collective-permute-done((bf16[384,192]{0,1:T(8,128)(2,1)S(1)}, bf16[384,192]{0,1:T(8,128)(2,1)S(1)}, u32[]{:S(2)}, u32[]{:S(2)}) %collective-permute-start.4) | collective-permute-done | bytes 147488 | tf_op jit(solution)/shard_map/ppermute | solution.py:14
  33.3 0.8 %gather_fusion = bf16[8,384,192]{1,2,0:T(8,128)(2,1)S(1)} fusion(bf16[8,384,192]{1,2,0:T(8,128)(2,1)S(1)} %bitcast_dynamic-update-slice_fusion, s32[1024]{0:T(1024)S(1)} %pad_clamp_fusion.1), kind=kCustom, calls=%fused_computation | custom fusion | bytes 2359328 | tf_op jit(solution)/shard_map/gather | solution.py:44
  34.1 1.7 %fusion.11 = f32[384,192,1]{0,1,2:T(8,128)S(1)} fusion(bf16[8,384,192]{1,2,0:T(8,128)(2,1)S(1)} %gather_fusion, bf16[8,192,192]{1,0,2:T(8,128)(2,1)} %reshape.238), kind=kOutput, calls=%fused_computation.9 | convolution fusion | flops 226492416 | bytes 2064384 | tf_op jit(solution)/shard_map/pab,pbn->an/dot_general | solution.py:46
  35.9 2.9 %collective-permute-start.11 = (f32[384,192]{0,1:T(8,128)S(1)}, f32[384,192]{0,1:T(8,128)S(1)}, u32[]{:S(2)}, u32[]{:S(2)}) collective-permute-start(f32[384,192]{0,1:T(8,128)S(1)} %bitcast.64), channel_id=1, source_target_pairs={{0,2},{1,3},{2,0},{3,1},{4,6},{5,7},{6,4},{7,5},{8,10},{9,11},{10,... | collective-permute-start | bytes 884744 | tf_op jit(solution)/shard_map/ppermute | solution.py:14
  38.8 1.4 %collective-permute-start.12 = (f32[384,192]{0,1:T(8,128)S(1)}, f32[384,192]{0,1:T(8,128)S(1)}, u32[]{:S(2)}, u32[]{:S(2)}) collective-permute-start(f32[384,192]{0,1:T(8,128)S(1)} %bitcast.65), channel_id=1, source_target_pairs={{0,3},{1,0},{2,1},{3,2},{4,7},{5,4},{6,5},{7,6},{8,11},{9,8},{10,9... | collective-permute-start | bytes 884744 | tf_op jit(solution)/shard_map/ppermute | solution.py:14
  40.2 4.4 %collective-permute-done.10 = f32[384,192]{0,1:T(8,128)S(1)} collective-permute-done((f32[384,192]{0,1:T(8,128)S(1)}, f32[384,192]{0,1:T(8,128)S(1)}, u32[]{:S(2)}, u32[]{:S(2)}) %collective-permute-start.10) | collective-permute-done | bytes 294944 | tf_op jit(solution)/shard_map/ppermute | solution.py:14
  44.6 16.6 %collective-permute-done.11 = f32[384,192]{0,1:T(8,128)S(1)} collective-permute-done((f32[384,192]{0,1:T(8,128)S(1)}, f32[384,192]{0,1:T(8,128)S(1)}, u32[]{:S(2)}, u32[]{:S(2)}) %collective-permute-start.11) | collective-permute-done | bytes 294944 | tf_op jit(solution)/shard_map/ppermute | solution.py:14
  61.2 3.3 %collective-permute-done.12 = f32[384,192]{0,1:T(8,128)S(1)} collective-permute-done((f32[384,192]{0,1:T(8,128)S(1)}, f32[384,192]{0,1:T(8,128)S(1)}, u32[]{:S(2)}, u32[]{:S(2)}) %collective-permute-start.12) | collective-permute-done | bytes 294944 | tf_op jit(solution)/shard_map/ppermute | solution.py:14
  64.7 1.8 %copy.16 = f32[4,384,192]{1,0,2:T(4,128)} copy(f32[4,384,192]{1,2,0:T(8,128)S(1)} %pad_maximum_fusion) | data formatting | bytes 2359296 | tf_op jit(solution)/shard_map/stack | solution.py:15
  66.4 1.8 %reshape.239 = f32[8,192,192]{1,0,2:T(8,128)S(1)} reshape(f32[4,384,192]{1,0,2:T(4,128)} %copy.16) | data formatting | bytes 2359296 | tf_op jit(solution)/shard_map/reshape | solution.py:49
  68.3 1.5 %fusion.8 = f32[384,192]{0,1:T(8,128)S(1)} fusion(bf16[8,384,192]{1,2,0:T(8,128)(2,1)S(1)} %gather_fusion, f32[8,192,192]{1,0,2:T(8,128)S(1)} %reshape.239, f32[384,192,1]{0,1,2:T(8,128)S(1)} %fusion.11), kind=kOutput, calls=%fused_computation.8 | convolution fusion | flops 1359175680 | bytes 2949120 | tf_op jit(solution)/shard_map/pab,pbn->an/dot_general | solution.py:50
  71.1 0.9 %copy.19 = f32[1,13,4096]{2,0,1:T(1,128)} copy(f32[1,13,4096]{2,1,0:T(8,128)S(1)} %bitcast_select_fusion) | data formatting | bytes 425984 | tf_op jit(solution)/shard_map/jit(_where)/select_n | solution.py:62
  (40 shorter events, 4.7 us)
Async XLA Ops:
  0.0 0.9 %copy-start = (bf16[1,9,4096]{2,1,0:T(8,128)(2,1)S(1)}, bf16[1,9,4096]{2,1,0:T(8,128)(2,1)}, u32[]{:S(2)}) copy-start(bf16[1,9,4096]{2,1,0:T(8,128)(2,1)} %param.3) | copy-start | bytes 221188
  1.7 8.0 %copy-start.1 = (s32[1,13]{1,0:T(1,128)S(1)}, s32[1,13]{1,0:T(1,128)}, u32[]{:S(2)}) copy-start(s32[1,13]{1,0:T(1,128)} %param.5) | copy-start | bytes 160
  2.6 21.3 %collective-permute-start = (bf16[384,192]{0,1:T(8,128)(2,1)S(1)}, bf16[384,192]{0,1:T(8,128)(2,1)S(1)}, u32[]{:S(2)}, u32[]{:S(2)}) collective-permute-start(bf16[384,192]{0,1:T(8,128)(2,1)S(1)} %reshape.237), channel_id=1, source_target_pairs={{0,4},{4,8},{8,12},{12,16},{16,20},{20,24},{24,28},{28,0},{1,5},{5... | collective-permute-start | bytes 442376 | tf_op jit(solution)/shard_map/ppermute | solution.py:14
  4.4 20.5 %collective-permute-start.1 = (bf16[384,192]{0,1:T(8,128)(2,1)S(1)}, bf16[384,192]{0,1:T(8,128)(2,1)S(1)}, u32[]{:S(2)}, u32[]{:S(2)}) collective-permute-start(bf16[384,192]{0,1:T(8,128)(2,1)S(1)} %reshape.237), channel_id=1, source_target_pairs={{0,8},{4,12},{8,16},{12,20},{16,24},{20,28},{24,0},{28,4},{1,9},{5... | collective-permute-start | bytes 442376 | tf_op jit(solution)/shard_map/ppermute | solution.py:14
  5.6 5.6 %collective-permute-start.7 = (bf16[384,192]{0,1:T(8,128)(2,1)S(1)}, bf16[384,192]{0,1:T(8,128)(2,1)S(1)}, u32[]{:S(2)}, u32[]{:S(2)}) collective-permute-start(bf16[384,192]{0,1:T(8,128)(2,1)S(1)} %reshape.237), channel_id=1, source_target_pairs={{0,1},{1,2},{2,3},{3,0},{4,5},{5,6},{6,7},{7,4},{8,9},{9,10},{10,1... | collective-permute-start | bytes 442376 | tf_op jit(solution)/shard_map/ppermute | solution.py:14
  6.9 12.9 %collective-permute-start.8 = (bf16[384,192]{0,1:T(8,128)(2,1)S(1)}, bf16[384,192]{0,1:T(8,128)(2,1)S(1)}, u32[]{:S(2)}, u32[]{:S(2)}) collective-permute-start(bf16[384,192]{0,1:T(8,128)(2,1)S(1)} %reshape.237), channel_id=1, source_target_pairs={{0,2},{1,3},{2,0},{3,1},{4,6},{5,7},{6,4},{7,5},{8,10},{9,11},{10,... | collective-permute-start | bytes 442376 | tf_op jit(solution)/shard_map/ppermute | solution.py:14
  7.9 13.5 %collective-permute-start.9 = (bf16[384,192]{0,1:T(8,128)(2,1)S(1)}, bf16[384,192]{0,1:T(8,128)(2,1)S(1)}, u32[]{:S(2)}, u32[]{:S(2)}) collective-permute-start(bf16[384,192]{0,1:T(8,128)(2,1)S(1)} %reshape.237), channel_id=1, source_target_pairs={{0,3},{1,0},{2,1},{3,2},{4,7},{5,4},{6,5},{7,6},{8,11},{9,8},{10,9... | collective-permute-start | bytes 442376 | tf_op jit(solution)/shard_map/ppermute | solution.py:14
  11.2 13.8 %collective-permute-start.2 = (bf16[384,192]{0,1:T(8,128)(2,1)S(1)}, bf16[384,192]{0,1:T(8,128)(2,1)S(1)}, u32[]{:S(2)}, u32[]{:S(2)}) collective-permute-start(bf16[384,192]{0,1:T(8,128)(2,1)S(1)} %reshape.237), channel_id=1, source_target_pairs={{0,12},{4,16},{8,20},{12,24},{16,28},{20,0},{24,4},{28,8},{1,13},{... | collective-permute-start | bytes 442376 | tf_op jit(solution)/shard_map/ppermute | solution.py:14
  19.7 5.3 %collective-permute-start.3 = (bf16[384,192]{0,1:T(8,128)(2,1)S(1)}, bf16[384,192]{0,1:T(8,128)(2,1)S(1)}, u32[]{:S(2)}, u32[]{:S(2)}) collective-permute-start(bf16[384,192]{0,1:T(8,128)(2,1)S(1)} %reshape.237), channel_id=1, source_target_pairs={{0,16},{4,20},{8,24},{12,28},{16,0},{20,4},{24,8},{28,12},{1,17},{... | collective-permute-start | bytes 442376 | tf_op jit(solution)/shard_map/ppermute | solution.py:14
  21.4 11.8 %collective-permute-start.4 = (bf16[384,192]{0,1:T(8,128)(2,1)S(1)}, bf16[384,192]{0,1:T(8,128)(2,1)S(1)}, u32[]{:S(2)}, u32[]{:S(2)}) collective-permute-start(bf16[384,192]{0,1:T(8,128)(2,1)S(1)} %reshape.237), channel_id=1, source_target_pairs={{0,20},{4,24},{8,28},{12,0},{16,4},{20,8},{24,12},{28,16},{1,21},{... | collective-permute-start | bytes 442376 | tf_op jit(solution)/shard_map/ppermute | solution.py:14
  23.9 9.4 %collective-permute-start.5 = (bf16[384,192]{0,1:T(8,128)(2,1)S(1)}, bf16[384,192]{0,1:T(8,128)(2,1)S(1)}, u32[]{:S(2)}, u32[]{:S(2)}) collective-permute-start(bf16[384,192]{0,1:T(8,128)(2,1)S(1)} %reshape.237), channel_id=1, source_target_pairs={{0,24},{4,28},{8,0},{12,4},{16,8},{20,12},{24,16},{28,20},{1,25},{... | collective-permute-start | bytes 442376 | tf_op jit(solution)/shard_map/ppermute | solution.py:14
  24.9 8.4 %collective-permute-start.6 = (bf16[384,192]{0,1:T(8,128)(2,1)S(1)}, bf16[384,192]{0,1:T(8,128)(2,1)S(1)}, u32[]{:S(2)}, u32[]{:S(2)}) collective-permute-start(bf16[384,192]{0,1:T(8,128)(2,1)S(1)} %reshape.237), channel_id=1, source_target_pairs={{0,28},{4,0},{8,4},{12,8},{16,12},{20,16},{24,20},{28,24},{1,29},{... | collective-permute-start | bytes 442376 | tf_op jit(solution)/shard_map/ppermute | solution.py:14
  35.8 8.8 %collective-permute-start.10 = (f32[384,192]{0,1:T(8,128)S(1)}, f32[384,192]{0,1:T(8,128)S(1)}, u32[]{:S(2)}, u32[]{:S(2)}) collective-permute-start(f32[384,192]{0,1:T(8,128)S(1)} %bitcast.63), channel_id=1, source_target_pairs={{0,1},{1,2},{2,3},{3,0},{4,5},{5,6},{6,7},{7,4},{8,9},{9,10},{10,1... | collective-permute-start | bytes 884744 | tf_op jit(solution)/shard_map/ppermute | solution.py:14
  35.9 25.3 %collective-permute-start.11 = (f32[384,192]{0,1:T(8,128)S(1)}, f32[384,192]{0,1:T(8,128)S(1)}, u32[]{:S(2)}, u32[]{:S(2)}) collective-permute-start(f32[384,192]{0,1:T(8,128)S(1)} %bitcast.64), channel_id=1, source_target_pairs={{0,2},{1,3},{2,0},{3,1},{4,6},{5,7},{6,4},{7,5},{8,10},{9,11},{10,... | collective-permute-start | bytes 884744 | tf_op jit(solution)/shard_map/ppermute | solution.py:14
  38.8 25.8 %collective-permute-start.12 = (f32[384,192]{0,1:T(8,128)S(1)}, f32[384,192]{0,1:T(8,128)S(1)}, u32[]{:S(2)}, u32[]{:S(2)}) collective-permute-start(f32[384,192]{0,1:T(8,128)S(1)} %bitcast.65), channel_id=1, source_target_pairs={{0,3},{1,0},{2,1},{3,2},{4,7},{5,4},{6,5},{7,6},{8,11},{9,8},{10,9... | collective-permute-start | bytes 884744 | tf_op jit(solution)/shard_map/ppermute | solution.py:14

commit v5 on v4

--- a/solution.py
+++ b/solution.py
@@ -15,6 +15,17 @@
     return jnp.stack(pieces)
 
 
+def paired_copies(value, axis, size):
+    pieces = [value]
+    for step in range(1, size // 2):
+        pairs = [(i, i ^ (2 * step)) for i in range(size)]
+        pieces.append(lax.ppermute(value, axis, pairs))
+    first = jnp.stack(pieces)
+    second = lax.ppermute(first, axis, [(i, i ^ 1) for i in range(size)])
+    both = jnp.stack([first, second], axis=1)
+    return both.reshape((size,) + value.shape)
+
+
 def on_device(p_blocks, p_slots, out_slots):
     n_row = lax.axis_size("row")
     n_col = lax.axis_size("col")
@@ -27,6 +38,7 @@
     group = rows_dev // COLS_DEV
     row_idx = lax.axis_index("row")
     col_idx = lax.axis_index("col")
+    assert n_col % 2 == 0 and (n_col // 2) & (n_col // 2 - 1) == 0
 
     own_ids = p_slots[0]
     grid = jnp.zeros((cells, area), jnp.bfloat16)
@@ -37,20 +49,19 @@
         .reshape(height, width)
     )
 
-    column_panel = shifted_copies(tile, "row", n_row).reshape(n_col, width, width)
-    row_pieces = shifted_copies(tile, "col", n_col)
-    place = jnp.arange(n_col, dtype=jnp.int32)
-    owner = ((row_idx - place // group) % n_row) * group + place % group
-    row_panel = row_pieces[(col_idx - owner) % n_col]
+    row_panel = paired_copies(tile, "col", n_col)
+    down = shifted_copies(tile, "row", n_row).reshape(n_row * group, width, width)
+    source = col_idx ^ jnp.arange(n_col, dtype=jnp.int32)
+    column_panel = down[((row_idx - source // group) % n_row) * group + source % group]
 
     square = jnp.einsum(
         "pab,pbn->an", row_panel, column_panel, preferred_element_type=jnp.float32
     )
-    square_panel = shifted_copies(square, "row", n_row).reshape(n_col, width, width)
+    square_panel = paired_copies(square, "col", n_col)
     cube = jnp.einsum(
         "pab,pbn->an",
-        row_panel.astype(jnp.float32),
         square_panel,
+        column_panel.astype(jnp.float32),
         precision=lax.Precision.HIGHEST,
         preferred_element_type=jnp.float32,
     )

time: 72.2 us -> 48.9 us (0.68)
  the two profiles are of different devices: /device:TPU:11 before, /device:TPU:17 now
where the time goes in v5:
time: 48.9 us; the launch traced here: 48.8 us
  waiting for transfers between devices  22.9 us (47%)
  starting transfers between devices  16.9 us (35%)
  local copies, waits for them, and re-layouts  5.42 us (11%)
  matrix products  1.91 us (4%)
  other arithmetic  1.47 us (3%)
    ppermute x6, waiting for transfers between devices, paired_copies(): pieces.append(lax.ppermute(value, axis, pairs))  12.9 us
    ppermute x2, starting transfers between devices, paired_copies(): second = lax.ppermute(first, axis, [(i, i ^ 1) for i in range(size)])  7.24 us
    ppermute x6, starting transfers between devices, paired_copies(): pieces.append(lax.ppermute(value, axis, pairs))  7.05 us
    ppermute x3, waiting for transfers between devices, shifted_copies(): pieces.append(lax.ppermute(value, axis, pairs))  6.89 us
    ppermute x2, waiting for transfers between devices, paired_copies(): second = lax.ppermute(first, axis, [(i, i ^ 1) for i in range(size)])  3.15 us
    ppermute x3, starting transfers between devices, shifted_copies(): pieces.append(lax.ppermute(value, axis, pairs))  2.6 us
    dot_general x1, matrix products, on_device(): jnp.einsum('pab,pbn->an', square_panel, column_panel.astype(jnp.float32),...  1.38 us
  transfers between devices with their start and end apart: 11, of which 7 were waited for; matrix products, arithmetic and copies ran while one was open for 2% of the time, Pallas kernels for 0%

profile of v5, /device:TPU:17, one launch (start us, length us, event | category | flops | bytes accessed | tf_op | source)
XLA Modules:
  0.0 48.8 jit_solution(11792992197703173460)
XLA Ops:
  0.0 0.7 %fusion.12 = s32[9]{0:T(128)S(1)} fusion(s32[1,9]{1,0:T(1,128)} %param.4), kind=kLoop, calls=%fused_computation.37 | loop fusion | flops 45 | bytes 72 | tf_op jit(solution)/shard_map/select_n | solution.py:45
  0.9 0.8 %scatter_custom_fusion = bf16[18,4096]{1,0:T(8,128)(2,1)S(1)} fusion(s32[9]{0:T(128)S(1)} %fusion.12, bf16[1,9,4096]{2,1,0:T(8,128)(2,1)S(1)} %copy-done, bf16[]{:T(256)} %constant.51.clone.1), kind=kCustom, calls=%fused_computation.16 | custom fusion | bytes 278530 | tf_op jit(solution)/shard_map/scatter | solution.py:45
  1.7 0.3 reshape.225
  2.5 1.3 %collective-permute-start.4 = (bf16[384,192]{0,1:T(8,128)(2,1)S(1)}, bf16[384,192]{0,1:T(8,128)(2,1)S(1)}, u32[]{:S(2)}, u32[]{:S(2)}) collective-permute-start(bf16[384,192]{0,1:T(8,128)(2,1)S(1)} %reshape.226), channel_id=1, source_target_pairs={{0,1},{1,2},{2,3},{3,0},{4,5},{5,6},{6,7},{7,4},{8,9},{9,10},{10,1... | collective-permute-start | bytes 442376 | tf_op jit(solution)/shard_map/ppermute | solution.py:14
  3.9 1.2 %collective-permute-start.6 = (bf16[384,192]{0,1:T(8,128)(2,1)S(1)}, bf16[384,192]{0,1:T(8,128)(2,1)S(1)}, u32[]{:S(2)}, u32[]{:S(2)}) collective-permute-start(bf16[384,192]{0,1:T(8,128)(2,1)S(1)} %reshape.226), channel_id=1, source_target_pairs={{0,3},{1,0},{2,1},{3,2},{4,7},{5,4},{6,5},{7,6},{8,11},{9,8},{10,9... | collective-permute-start | bytes 442376 | tf_op jit(solution)/shard_map/ppermute | solution.py:14
  5.1 1.2 %collective-permute-start = (bf16[384,192]{0,1:T(8,128)(2,1)S(1)}, bf16[384,192]{0,1:T(8,128)(2,1)S(1)}, u32[]{:S(2)}, u32[]{:S(2)}) collective-permute-start(bf16[384,192]{0,1:T(8,128)(2,1)S(1)} %reshape.226), channel_id=1, source_target_pairs={{0,8},{4,12},{8,0},{12,4},{16,24},{20,28},{24,16},{28,20},{1,9},{5... | collective-permute-start | bytes 442376 | tf_op jit(solution)/shard_map/ppermute | solution.py:22
  6.4 1.2 %collective-permute-start.1 = (bf16[384,192]{0,1:T(8,128)(2,1)S(1)}, bf16[384,192]{0,1:T(8,128)(2,1)S(1)}, u32[]{:S(2)}, u32[]{:S(2)}) collective-permute-start(bf16[384,192]{0,1:T(8,128)(2,1)S(1)} %reshape.226), channel_id=1, source_target_pairs={{0,16},{4,20},{8,24},{12,28},{16,0},{20,4},{24,8},{28,12},{1,17},{... | collective-permute-start | bytes 442376 | tf_op jit(solution)/shard_map/ppermute | solution.py:22
  7.6 1.9 %collective-permute-start.2 = (bf16[384,192]{0,1:T(8,128)(2,1)S(1)}, bf16[384,192]{0,1:T(8,128)(2,1)S(1)}, u32[]{:S(2)}, u32[]{:S(2)}) collective-permute-start(bf16[384,192]{0,1:T(8,128)(2,1)S(1)} %reshape.226), channel_id=1, source_target_pairs={{0,24},{4,28},{8,16},{12,20},{16,8},{20,12},{24,0},{28,4},{1,25},{... | collective-permute-start | bytes 442376 | tf_op jit(solution)/shard_map/ppermute | solution.py:22
  9.8 3.7 %collective-permute-done.5 = bf16[384,192]{0,1:T(8,128)(2,1)S(1)} collective-permute-done((bf16[384,192]{0,1:T(8,128)(2,1)S(1)}, bf16[384,192]{0,1:T(8,128)(2,1)S(1)}, u32[]{:S(2)}, u32[]{:S(2)}) %collective-permute-start.5) | collective-permute-done | bytes 147488 | tf_op jit(solution)/shard_map/ppermute | solution.py:14
  13.5 3.2 %collective-permute-done.6 = bf16[384,192]{0,1:T(8,128)(2,1)S(1)} collective-permute-done((bf16[384,192]{0,1:T(8,128)(2,1)S(1)}, bf16[384,192]{0,1:T(8,128)(2,1)S(1)}, u32[]{:S(2)}, u32[]{:S(2)}) %collective-permute-start.6) | collective-permute-done | bytes 147488 | tf_op jit(solution)/shard_map/ppermute | solution.py:14
  16.9 5.7 %collective-permute-start.3 = (bf16[4,384,192]{1,2,0:T(8,128)(2,1)S(1)}, bf16[4,384,192]{1,2,0:T(8,128)(2,1)S(1)}, u32[]{:S(2)}, u32[]{:S(2)}) collective-permute-start(bf16[4,384,192]{1,2,0:T(8,128)(2,1)S(1)} %get-tuple-element.8), channel_id=1, source_target_pairs={{0,4},{4,0},{8,12},{12,8},{16,20},{20,16},{24,28},{28,24},{1,5},{5... | collective-permute-start | bytes 1769480 | tf_op jit(solution)/shard_map/ppermute | solution.py:24
  22.9 0.6 %gather_fusion = bf16[8,192,192]{2,1,0:T(8,128)(2,1)S(1)} fusion(bf16[8,192,192]{2,1,0:T(8,128)(2,1)S(1)} %bitcast.60, s32[1024]{0:T(1024)S(1)} %pad_clamp_fusion.1), kind=kCustom, calls=%fused_computation | custom fusion | bytes 1179680 | tf_op jit(solution)/shard_map/gather | solution.py:55
  23.5 0.7 %collective-permute-done.3 = bf16[4,384,192]{1,2,0:T(8,128)(2,1)S(1)} collective-permute-done((bf16[4,384,192]{1,2,0:T(8,128)(2,1)S(1)}, bf16[4,384,192]{1,2,0:T(8,128)(2,1)S(1)}, u32[]{:S(2)}, u32[]{:S(2)}) %collective-permute-start.3) | collective-permute-done | bytes 589856 | tf_op jit(solution)/shard_map/ppermute | solution.py:24
  24.5 0.5 %fusion.17 = f32[384,192,1]{0,1,2:T(8,128)S(1)} fusion(bf16[8,384,192]{1,2,0:T(8,128)(2,1)S(1)} %bitcast.59, bf16[8,192,192]{2,1,0:T(8,128)(2,1)S(1)} %gather_fusion), kind=kOutput, calls=%fused_computation.42 | convolution fusion | flops 226492416 | bytes 2064384 | tf_op jit(solution)/shard_map/pab,pbn->an/dot_general | solution.py:57
  25.0 1.3 %collective-permute-start.7 = (f32[384,192]{0,1:T(8,128)S(1)}, f32[384,192]{0,1:T(8,128)S(1)}, u32[]{:S(2)}, u32[]{:S(2)}) collective-permute-start(f32[384,192]{0,1:T(8,128)S(1)} %bitcast.62), channel_id=1, source_target_pairs={{0,8},{4,12},{8,0},{12,4},{16,24},{20,28},{24,16},{28,20},{1,9},{5... | collective-permute-start | bytes 884744 | tf_op jit(solution)/shard_map/ppermute | solution.py:22
  26.3 1.2 %collective-permute-start.8 = (f32[384,192]{0,1:T(8,128)S(1)}, f32[384,192]{0,1:T(8,128)S(1)}, u32[]{:S(2)}, u32[]{:S(2)}) collective-permute-start(f32[384,192]{0,1:T(8,128)S(1)} %bitcast.63), channel_id=1, source_target_pairs={{0,16},{4,20},{8,24},{12,28},{16,0},{20,4},{24,8},{28,12},{1,17},{... | collective-permute-start | bytes 884744 | tf_op jit(solution)/shard_map/ppermute | solution.py:22
  27.8 5.5 %collective-permute-done.7 = f32[384,192]{0,1:T(8,128)S(1)} collective-permute-done((f32[384,192]{0,1:T(8,128)S(1)}, f32[384,192]{0,1:T(8,128)S(1)}, u32[]{:S(2)}, u32[]{:S(2)}) %collective-permute-start.7) | collective-permute-done | bytes 294944 | tf_op jit(solution)/shard_map/ppermute | solution.py:22
  33.3 0.9 %collective-permute-done.8 = f32[384,192]{0,1:T(8,128)S(1)} collective-permute-done((f32[384,192]{0,1:T(8,128)S(1)}, f32[384,192]{0,1:T(8,128)S(1)}, u32[]{:S(2)}, u32[]{:S(2)}) %collective-permute-start.8) | collective-permute-done | bytes 294944 | tf_op jit(solution)/shard_map/ppermute | solution.py:22
  34.2 6.4 %collective-permute-done.9 = f32[384,192]{0,1:T(8,128)S(1)} collective-permute-done((f32[384,192]{0,1:T(8,128)S(1)}, f32[384,192]{0,1:T(8,128)S(1)}, u32[]{:S(2)}, u32[]{:S(2)}) %collective-permute-start.9) | collective-permute-done | bytes 294944 | tf_op jit(solution)/shard_map/ppermute | solution.py:22
  40.8 1.5 %collective-permute-start.10 = (f32[4,384,192]{1,2,0:T(8,128)S(1)}, f32[4,384,192]{1,2,0:T(8,128)S(1)}, u32[]{:S(2)}, u32[]{:S(2)}) collective-permute-start(f32[4,384,192]{1,2,0:T(8,128)S(1)} %get-tuple-element.6), channel_id=1, source_target_pairs={{0,4},{4,0},{8,12},{12,8},{16,20},{20,16},{24,28},{28,24},{1,5},{5... | collective-permute-start | bytes 3538952 | tf_op jit(solution)/shard_map/ppermute | solution.py:24
  42.3 2.4 %collective-permute-done.10 = f32[4,384,192]{1,2,0:T(8,128)S(1)} collective-permute-done((f32[4,384,192]{1,2,0:T(8,128)S(1)}, f32[4,384,192]{1,2,0:T(8,128)S(1)}, u32[]{:S(2)}, u32[]{:S(2)}) %collective-permute-start.10) | collective-permute-done | bytes 1179680 | tf_op jit(solution)/shard_map/ppermute | solution.py:24
  45.1 1.4 %fusion.1 = f32[384,192]{0,1:T(8,128)S(1)} fusion(f32[8,384,192]{1,2,0:T(8,128)S(1)} %bitcast.58, bf16[8,192,192]{2,1,0:T(8,128)(2,1)S(1)} %gather_fusion, f32[384,192,1]{0,1,2:T(8,128)S(1)} %fusion.17), kind=kOutput, calls=%fused_computation.8 | convolution fusion | flops 1359175680 | bytes 3538944 | tf_op jit(solution)/shard_map/pab,pbn->an/dot_general | solution.py:61
  47.1 0.6 %gather_fusion.1 = f32[13,4096]{1,0:T(8,128)S(1)} fusion(f32[18,4096]{1,0:T(8,128)S(1)} %reshape.231, s32[1024]{0:T(1024)S(1)} %pad_clamp_fusion), kind=kCustom, calls=%fused_computation.1 | custom fusion | bytes 426036 | tf_op jit(solution)/shard_map/gather | solution.py:72
  47.9 0.9 %copy.16 = f32[1,13,4096]{2,0,1:T(1,128)} copy(f32[1,13,4096]{2,1,0:T(8,128)S(1)} %bitcast_select_fusion) | data formatting | bytes 425984 | tf_op jit(solution)/shard_map/jit(_where)/select_n | solution.py:73
  (29 shorter events, 3.3 us)
Async XLA Ops:
  0.0 0.9 %copy-start = (bf16[1,9,4096]{2,1,0:T(8,128)(2,1)S(1)}, bf16[1,9,4096]{2,1,0:T(8,128)(2,1)}, u32[]{:S(2)}) copy-start(bf16[1,9,4096]{2,1,0:T(8,128)(2,1)} %param.3) | copy-start | bytes 221188
  2.5 5.1 %collective-permute-start.4 = (bf16[384,192]{0,1:T(8,128)(2,1)S(1)}, bf16[384,192]{0,1:T(8,128)(2,1)S(1)}, u32[]{:S(2)}, u32[]{:S(2)}) collective-permute-start(bf16[384,192]{0,1:T(8,128)(2,1)S(1)} %reshape.226), channel_id=1, source_target_pairs={{0,1},{1,2},{2,3},{3,0},{4,5},{5,6},{6,7},{7,4},{8,9},{9,10},{10,1... | collective-permute-start | bytes 442376 | tf_op jit(solution)/shard_map/ppermute | solution.py:14
  3.9 9.6 %collective-permute-start.5 = (bf16[384,192]{0,1:T(8,128)(2,1)S(1)}, bf16[384,192]{0,1:T(8,128)(2,1)S(1)}, u32[]{:S(2)}, u32[]{:S(2)}) collective-permute-start(bf16[384,192]{0,1:T(8,128)(2,1)S(1)} %reshape.226), channel_id=1, source_target_pairs={{0,2},{1,3},{2,0},{3,1},{4,6},{5,7},{6,4},{7,5},{8,10},{9,11},{10,... | collective-permute-start | bytes 442376 | tf_op jit(solution)/shard_map/ppermute | solution.py:14
  3.9 12.7 %collective-permute-start.6 = (bf16[384,192]{0,1:T(8,128)(2,1)S(1)}, bf16[384,192]{0,1:T(8,128)(2,1)S(1)}, u32[]{:S(2)}, u32[]{:S(2)}) collective-permute-start(bf16[384,192]{0,1:T(8,128)(2,1)S(1)} %reshape.226), channel_id=1, source_target_pairs={{0,3},{1,0},{2,1},{3,2},{4,7},{5,4},{6,5},{7,6},{8,11},{9,8},{10,9... | collective-permute-start | bytes 442376 | tf_op jit(solution)/shard_map/ppermute | solution.py:14
  5.1 11.5 %collective-permute-start = (bf16[384,192]{0,1:T(8,128)(2,1)S(1)}, bf16[384,192]{0,1:T(8,128)(2,1)S(1)}, u32[]{:S(2)}, u32[]{:S(2)}) collective-permute-start(bf16[384,192]{0,1:T(8,128)(2,1)S(1)} %reshape.226), channel_id=1, source_target_pairs={{0,8},{4,12},{8,0},{12,4},{16,24},{20,28},{24,16},{28,20},{1,9},{5... | collective-permute-start | bytes 442376 | tf_op jit(solution)/shard_map/ppermute | solution.py:22
  6.4 10.3 %collective-permute-start.1 = (bf16[384,192]{0,1:T(8,128)(2,1)S(1)}, bf16[384,192]{0,1:T(8,128)(2,1)S(1)}, u32[]{:S(2)}, u32[]{:S(2)}) collective-permute-start(bf16[384,192]{0,1:T(8,128)(2,1)S(1)} %reshape.226), channel_id=1, source_target_pairs={{0,16},{4,20},{8,24},{12,28},{16,0},{20,4},{24,8},{28,12},{1,17},{... | collective-permute-start | bytes 442376 | tf_op jit(solution)/shard_map/ppermute | solution.py:22
  7.6 9.1 %collective-permute-start.2 = (bf16[384,192]{0,1:T(8,128)(2,1)S(1)}, bf16[384,192]{0,1:T(8,128)(2,1)S(1)}, u32[]{:S(2)}, u32[]{:S(2)}) collective-permute-start(bf16[384,192]{0,1:T(8,128)(2,1)S(1)} %reshape.226), channel_id=1, source_target_pairs={{0,24},{4,28},{8,16},{12,20},{16,8},{20,12},{24,0},{28,4},{1,25},{... | collective-permute-start | bytes 442376 | tf_op jit(solution)/shard_map/ppermute | solution.py:22
  16.9 7.4 %collective-permute-start.3 = (bf16[4,384,192]{1,2,0:T(8,128)(2,1)S(1)}, bf16[4,384,192]{1,2,0:T(8,128)(2,1)S(1)}, u32[]{:S(2)}, u32[]{:S(2)}) collective-permute-start(bf16[4,384,192]{1,2,0:T(8,128)(2,1)S(1)} %get-tuple-element.8), channel_id=1, source_target_pairs={{0,4},{4,0},{8,12},{12,8},{16,20},{20,16},{24,28},{28,24},{1,5},{5... | collective-permute-start | bytes 1769480 | tf_op jit(solution)/shard_map/ppermute | solution.py:24
  25.0 8.3 %collective-permute-start.7 = (f32[384,192]{0,1:T(8,128)S(1)}, f32[384,192]{0,1:T(8,128)S(1)}, u32[]{:S(2)}, u32[]{:S(2)}) collective-permute-start(f32[384,192]{0,1:T(8,128)S(1)} %bitcast.62), channel_id=1, source_target_pairs={{0,8},{4,12},{8,0},{12,4},{16,24},{20,28},{24,16},{28,20},{1,9},{5... | collective-permute-start | bytes 884744 | tf_op jit(solution)/shard_map/ppermute | solution.py:22
  26.3 7.9 %collective-permute-start.8 = (f32[384,192]{0,1:T(8,128)S(1)}, f32[384,192]{0,1:T(8,128)S(1)}, u32[]{:S(2)}, u32[]{:S(2)}) collective-permute-start(f32[384,192]{0,1:T(8,128)S(1)} %bitcast.63), channel_id=1, source_target_pairs={{0,16},{4,20},{8,24},{12,28},{16,0},{20,4},{24,8},{28,12},{1,17},{... | collective-permute-start | bytes 884744 | tf_op jit(solution)/shard_map/ppermute | solution.py:22
  27.6 13.1 %collective-permute-start.9 = (f32[384,192]{0,1:T(8,128)S(1)}, f32[384,192]{0,1:T(8,128)S(1)}, u32[]{:S(2)}, u32[]{:S(2)}) collective-permute-start(f32[384,192]{0,1:T(8,128)S(1)} %bitcast.64), channel_id=1, source_target_pairs={{0,24},{4,28},{8,16},{12,20},{16,8},{20,12},{24,0},{28,4},{1,25},{... | collective-permute-start | bytes 884744 | tf_op jit(solution)/shard_map/ppermute | solution.py:22
  40.6 1.7 %copy-start.1 = (s32[1,13]{1,0:T(1,128)S(1)}, s32[1,13]{1,0:T(1,128)}, u32[]{:S(2)}) copy-start(s32[1,13]{1,0:T(1,128)} %param.5) | copy-start | bytes 160
  40.8 4.0 %collective-permute-start.10 = (f32[4,384,192]{1,2,0:T(8,128)S(1)}, f32[4,384,192]{1,2,0:T(8,128)S(1)}, u32[]{:S(2)}, u32[]{:S(2)}) collective-permute-start(f32[4,384,192]{1,2,0:T(8,128)S(1)} %get-tuple-element.6), channel_id=1, source_target_pairs={{0,4},{4,0},{8,12},{12,8},{16,20},{20,16},{24,28},{28,24},{1,5},{5... | collective-permute-start | bytes 3538952 | tf_op jit(solution)/shard_map/ppermute | solution.py:24

commit v6 on v5

--- a/solution.py
+++ b/solution.py
@@ -20,9 +20,8 @@
     for step in range(1, size // 2):
         pairs = [(i, i ^ (2 * step)) for i in range(size)]
         pieces.append(lax.ppermute(value, axis, pairs))
-    first = jnp.stack(pieces)
-    second = lax.ppermute(first, axis, [(i, i ^ 1) for i in range(size)])
-    both = jnp.stack([first, second], axis=1)
+    second = [lax.ppermute(piece, axis, [(i, i ^ 1) for i in range(size)]) for piece in pieces]
+    both = jnp.stack([jnp.stack(pieces), jnp.stack(second)], axis=1)
     return both.reshape((size,) + value.shape)
 
 

time: 48.9 us -> 46.2 us (0.945)
  the two profiles are of different devices: /device:TPU:17 before, /device:TPU:0 now
where the time goes in v6:
time: 46.2 us; the launch traced here: 46 us
  waiting for transfers between devices  20.8 us (45%)
  starting transfers between devices  16.1 us (35%)
  local copies, waits for them, and re-layouts  5.42 us (12%)
  matrix products  1.91 us (4%)
  other arithmetic  1.53 us (3%)
    ppermute x6, waiting for transfers between devices, paired_copies(): pieces.append(lax.ppermute(value, axis, pairs))  13.4 us
    ppermute x6, starting transfers between devices, paired_copies(): pieces.append(lax.ppermute(value, axis, pairs))  8.12 us
    ppermute x3, starting transfers between devices, shifted_copies(): pieces.append(lax.ppermute(value, axis, pairs))  6.92 us
    ppermute x3, waiting for transfers between devices, shifted_copies(): pieces.append(lax.ppermute(value, axis, pairs))  5.94 us
    dot_general x1, matrix products, on_device(): jnp.einsum('pab,pbn->an', square_panel, column_panel.astype(jnp.float32),...  1.38 us
    ppermute x8, waiting for transfers between devices, paired_copies(): lax.ppermute(piece, axis, [(i, i ^ 1) for i in range(size)])  1.38 us
    ppermute x8, starting transfers between devices, paired_copies(): lax.ppermute(piece, axis, [(i, i ^ 1) for i in range(size)])  1.08 us
  transfers between devices with their start and end apart: 17, of which 6 were waited for; matrix products, arithmetic and copies ran while one was open for 3% of the time, Pallas kernels for 0%

profile of v6, /device:TPU:0, one launch (start us, length us, event | category | flops | bytes accessed | tf_op | source)
XLA Modules:
  0.0 46.0 jit_solution(7696296804105244790)
XLA Ops:
  0.0 0.7 %fusion.13 = s32[9]{0:T(128)S(1)} fusion(s32[1,9]{1,0:T(1,128)} %param.4), kind=kLoop, calls=%fused_computation.40 | loop fusion | flops 45 | bytes 72 | tf_op jit(solution)/shard_map/select_n | solution.py:44
  0.9 0.8 %scatter_custom_fusion = bf16[18,4096]{1,0:T(8,128)(2,1)S(1)} fusion(s32[9]{0:T(128)S(1)} %fusion.13, bf16[1,9,4096]{2,1,0:T(8,128)(2,1)S(1)} %copy-done, bf16[]{:T(256)} %constant.51.clone.1), kind=kCustom, calls=%fused_computation.19 | custom fusion | bytes 278530 | tf_op jit(solution)/shard_map/scatter | solution.py:44
  1.7 0.3 reshape.225
  2.5 3.0 %collective-permute-start = (bf16[384,192]{0,1:T(8,128)(2,1)S(1)}, bf16[384,192]{0,1:T(8,128)(2,1)S(1)}, u32[]{:S(2)}, u32[]{:S(2)}) collective-permute-start(bf16[384,192]{0,1:T(8,128)(2,1)S(1)} %reshape.226), channel_id=1, source_target_pairs={{0,8},{4,12},{8,0},{12,4},{16,24},{20,28},{24,16},{28,20},{1,9},{5... | collective-permute-start | bytes 442376 | tf_op jit(solution)/shard_map/ppermute | solution.py:22
  5.6 1.5 %collective-permute-start.1 = (bf16[384,192]{0,1:T(8,128)(2,1)S(1)}, bf16[384,192]{0,1:T(8,128)(2,1)S(1)}, u32[]{:S(2)}, u32[]{:S(2)}) collective-permute-start(bf16[384,192]{0,1:T(8,128)(2,1)S(1)} %reshape.226), channel_id=1, source_target_pairs={{0,16},{4,20},{8,24},{12,28},{16,0},{20,4},{24,8},{28,12},{1,17},{... | collective-permute-start | bytes 442376 | tf_op jit(solution)/shard_map/ppermute | solution.py:22
  7.1 2.0 %collective-permute-start.7 = (bf16[384,192]{0,1:T(8,128)(2,1)S(1)}, bf16[384,192]{0,1:T(8,128)(2,1)S(1)}, u32[]{:S(2)}, u32[]{:S(2)}) collective-permute-start(bf16[384,192]{0,1:T(8,128)(2,1)S(1)} %reshape.226), channel_id=1, source_target_pairs={{0,1},{1,2},{2,3},{3,0},{4,5},{5,6},{6,7},{7,4},{8,9},{9,10},{10,1... | collective-permute-start | bytes 442376 | tf_op jit(solution)/shard_map/ppermute | solution.py:14
  9.1 2.6 %collective-permute-start.8 = (bf16[384,192]{0,1:T(8,128)(2,1)S(1)}, bf16[384,192]{0,1:T(8,128)(2,1)S(1)}, u32[]{:S(2)}, u32[]{:S(2)}) collective-permute-start(bf16[384,192]{0,1:T(8,128)(2,1)S(1)} %reshape.226), channel_id=1, source_target_pairs={{0,2},{1,3},{2,0},{3,1},{4,6},{5,7},{6,4},{7,5},{8,10},{9,11},{10,... | collective-permute-start | bytes 442376 | tf_op jit(solution)/shard_map/ppermute | solution.py:14
  11.7 2.3 %collective-permute-start.9 = (bf16[384,192]{0,1:T(8,128)(2,1)S(1)}, bf16[384,192]{0,1:T(8,128)(2,1)S(1)}, u32[]{:S(2)}, u32[]{:S(2)}) collective-permute-start(bf16[384,192]{0,1:T(8,128)(2,1)S(1)} %reshape.226), channel_id=1, source_target_pairs={{0,3},{1,0},{2,1},{3,2},{4,7},{5,4},{6,5},{7,6},{8,11},{9,8},{10,9... | collective-permute-start | bytes 442376 | tf_op jit(solution)/shard_map/ppermute | solution.py:14
  14.2 0.5 %collective-permute-start.4 = (bf16[384,192]{0,1:T(8,128)(2,1)S(1)}, bf16[384,192]{0,1:T(8,128)(2,1)S(1)}, u32[]{:S(2)}, u32[]{:S(2)}) collective-permute-start(bf16[384,192]{0,1:T(8,128)(2,1)S(1)} %collective-permute-done), channel_id=1, source_target_pairs={{0,4},{4,0},{8,12},{12,8},{16,20},{20,16},{24,28},{28,24},{1,5},{5... | collective-permute-start | bytes 442376 | tf_op jit(solution)/shard_map/ppermute | solution.py:23
  14.6 1.4 %collective-permute-done.7 = bf16[384,192]{0,1:T(8,128)(2,1)S(1)} collective-permute-done((bf16[384,192]{0,1:T(8,128)(2,1)S(1)}, bf16[384,192]{0,1:T(8,128)(2,1)S(1)}, u32[]{:S(2)}, u32[]{:S(2)}) %collective-permute-start.7) | collective-permute-done | bytes 147488 | tf_op jit(solution)/shard_map/ppermute | solution.py:14
  16.0 4.6 %collective-permute-done.8 = bf16[384,192]{0,1:T(8,128)(2,1)S(1)} collective-permute-done((bf16[384,192]{0,1:T(8,128)(2,1)S(1)}, bf16[384,192]{0,1:T(8,128)(2,1)S(1)}, u32[]{:S(2)}, u32[]{:S(2)}) %collective-permute-start.8) | collective-permute-done | bytes 147488 | tf_op jit(solution)/shard_map/ppermute | solution.py:14
  21.3 0.6 %gather_fusion = bf16[8,192,192]{2,1,0:T(8,128)(2,1)S(1)} fusion(bf16[8,192,192]{2,1,0:T(8,128)(2,1)S(1)} %bitcast.70, s32[1024]{0:T(1024)S(1)} %pad_clamp_fusion.1), kind=kCustom, calls=%fused_computation | custom fusion | bytes 1179680 | tf_op jit(solution)/shard_map/gather | solution.py:54
  22.4 0.5 %fusion.16 = f32[384,192,1]{0,1,2:T(8,128)S(1)} fusion(bf16[8,384,192]{1,2,0:T(8,128)(2,1)S(1)} %bitcast.69, bf16[8,192,192]{2,1,0:T(8,128)(2,1)S(1)} %gather_fusion), kind=kOutput, calls=%fused_computation.43 | convolution fusion | flops 226492416 | bytes 2064384 | tf_op jit(solution)/shard_map/pab,pbn->an/dot_general | solution.py:56
  22.9 1.6 %collective-permute-start.10 = (f32[384,192]{0,1:T(8,128)S(1)}, f32[384,192]{0,1:T(8,128)S(1)}, u32[]{:S(2)}, u32[]{:S(2)}) collective-permute-start(f32[384,192]{0,1:T(8,128)S(1)} %bitcast.72), channel_id=1, source_target_pairs={{0,8},{4,12},{8,0},{12,4},{16,24},{20,28},{24,16},{28,20},{1,9},{5... | collective-permute-start | bytes 884744 | tf_op jit(solution)/shard_map/ppermute | solution.py:22
  24.5 1.5 %collective-permute-start.11 = (f32[384,192]{0,1:T(8,128)S(1)}, f32[384,192]{0,1:T(8,128)S(1)}, u32[]{:S(2)}, u32[]{:S(2)}) collective-permute-start(f32[384,192]{0,1:T(8,128)S(1)} %bitcast.73), channel_id=1, source_target_pairs={{0,16},{4,20},{8,24},{12,28},{16,0},{20,4},{24,8},{28,12},{1,17},{... | collective-permute-start | bytes 884744 | tf_op jit(solution)/shard_map/ppermute | solution.py:22
  26.0 0.5 %collective-permute-start.12 = (f32[384,192]{0,1:T(8,128)S(1)}, f32[384,192]{0,1:T(8,128)S(1)}, u32[]{:S(2)}, u32[]{:S(2)}) collective-permute-start(f32[384,192]{0,1:T(8,128)S(1)} %bitcast.74), channel_id=1, source_target_pairs={{0,24},{4,28},{8,16},{12,20},{16,8},{20,12},{24,0},{28,4},{1,25},{... | collective-permute-start | bytes 884744 | tf_op jit(solution)/shard_map/ppermute | solution.py:22
  26.5 6.4 %collective-permute-done.10 = f32[384,192]{0,1:T(8,128)S(1)} collective-permute-done((f32[384,192]{0,1:T(8,128)S(1)}, f32[384,192]{0,1:T(8,128)S(1)}, u32[]{:S(2)}, u32[]{:S(2)}) %collective-permute-start.10) | collective-permute-done | bytes 294944 | tf_op jit(solution)/shard_map/ppermute | solution.py:22
  32.9 7.1 %collective-permute-done.11 = f32[384,192]{0,1:T(8,128)S(1)} collective-permute-done((f32[384,192]{0,1:T(8,128)S(1)}, f32[384,192]{0,1:T(8,128)S(1)}, u32[]{:S(2)}, u32[]{:S(2)}) %collective-permute-start.11) | collective-permute-done | bytes 294944 | tf_op jit(solution)/shard_map/ppermute | solution.py:22
  39.9 0.5 %collective-permute-start.16 = (f32[384,192]{0,1:T(8,128)S(1)}, f32[384,192]{0,1:T(8,128)S(1)}, u32[]{:S(2)}, u32[]{:S(2)}) collective-permute-start(f32[384,192]{0,1:T(8,128)S(1)} %collective-permute-done.12), channel_id=1, source_target_pairs={{0,4},{4,0},{8,12},{12,8},{16,20},{20,16},{24,28},{28,24},{1,5},{5... | collective-permute-start | bytes 884744 | tf_op jit(solution)/shard_map/ppermute | solution.py:23
  40.6 0.9 %collective-permute-done.15 = f32[384,192]{0,1:T(8,128)S(1)} collective-permute-done((f32[384,192]{0,1:T(8,128)S(1)}, f32[384,192]{0,1:T(8,128)S(1)}, u32[]{:S(2)}, u32[]{:S(2)}) %collective-permute-start.15) | collective-permute-done | bytes 294944 | tf_op jit(solution)/shard_map/ppermute | solution.py:23
  41.5 0.4 collective-permute-done.16
  42.3 1.4 %fusion.1 = f32[384,192]{0,1:T(8,128)S(1)} fusion(f32[8,384,192]{1,2,0:T(8,128)S(1)} %bitcast.68, bf16[8,192,192]{2,1,0:T(8,128)(2,1)S(1)} %gather_fusion, f32[384,192,1]{0,1,2:T(8,128)S(1)} %fusion.16), kind=kOutput, calls=%fused_computation.9 | convolution fusion | flops 1359175680 | bytes 3538944 | tf_op jit(solution)/shard_map/pab,pbn->an/dot_general | solution.py:60
  44.4 0.6 %gather_fusion.1 = f32[13,4096]{1,0:T(8,128)S(1)} fusion(f32[18,4096]{1,0:T(8,128)S(1)} %reshape.231, s32[1024]{0:T(1024)S(1)} %pad_clamp_fusion), kind=kCustom, calls=%fused_computation.1 | custom fusion | bytes 426036 | tf_op jit(solution)/shard_map/gather | solution.py:71
  45.1 0.9 %copy.16 = f32[1,13,4096]{2,0,1:T(1,128)} copy(f32[1,13,4096]{2,1,0:T(8,128)S(1)} %bitcast_select_fusion) | data formatting | bytes 425984 | tf_op jit(solution)/shard_map/jit(_where)/select_n | solution.py:72
  (43 shorter events, 3.2 us)
Async XLA Ops:
  0.0 0.9 %copy-start = (bf16[1,9,4096]{2,1,0:T(8,128)(2,1)S(1)}, bf16[1,9,4096]{2,1,0:T(8,128)(2,1)}, u32[]{:S(2)}) copy-start(bf16[1,9,4096]{2,1,0:T(8,128)(2,1)} %param.3) | copy-start | bytes 221188
  2.5 9.2 %collective-permute-start = (bf16[384,192]{0,1:T(8,128)(2,1)S(1)}, bf16[384,192]{0,1:T(8,128)(2,1)S(1)}, u32[]{:S(2)}, u32[]{:S(2)}) collective-permute-start(bf16[384,192]{0,1:T(8,128)(2,1)S(1)} %reshape.226), channel_id=1, source_target_pairs={{0,8},{4,12},{8,0},{12,4},{16,24},{20,28},{24,16},{28,20},{1,9},{5... | collective-permute-start | bytes 442376 | tf_op jit(solution)/shard_map/ppermute | solution.py:22
  5.6 8.5 %collective-permute-start.1 = (bf16[384,192]{0,1:T(8,128)(2,1)S(1)}, bf16[384,192]{0,1:T(8,128)(2,1)S(1)}, u32[]{:S(2)}, u32[]{:S(2)}) collective-permute-start(bf16[384,192]{0,1:T(8,128)(2,1)S(1)} %reshape.226), channel_id=1, source_target_pairs={{0,16},{4,20},{8,24},{12,28},{16,0},{20,4},{24,8},{28,12},{1,17},{... | collective-permute-start | bytes 442376 | tf_op jit(solution)/shard_map/ppermute | solution.py:22
  7.1 7.1 %collective-permute-start.2 = (bf16[384,192]{0,1:T(8,128)(2,1)S(1)}, bf16[384,192]{0,1:T(8,128)(2,1)S(1)}, u32[]{:S(2)}, u32[]{:S(2)}) collective-permute-start(bf16[384,192]{0,1:T(8,128)(2,1)S(1)} %reshape.226), channel_id=1, source_target_pairs={{0,24},{4,28},{8,16},{12,20},{16,8},{20,12},{24,0},{28,4},{1,25},{... | collective-permute-start | bytes 442376 | tf_op jit(solution)/shard_map/ppermute | solution.py:22
  7.1 8.9 %collective-permute-start.7 = (bf16[384,192]{0,1:T(8,128)(2,1)S(1)}, bf16[384,192]{0,1:T(8,128)(2,1)S(1)}, u32[]{:S(2)}, u32[]{:S(2)}) collective-permute-start(bf16[384,192]{0,1:T(8,128)(2,1)S(1)} %reshape.226), channel_id=1, source_target_pairs={{0,1},{1,2},{2,3},{3,0},{4,5},{5,6},{6,7},{7,4},{8,9},{9,10},{10,1... | collective-permute-start | bytes 442376 | tf_op jit(solution)/shard_map/ppermute | solution.py:14
  9.1 11.4 %collective-permute-start.8 = (bf16[384,192]{0,1:T(8,128)(2,1)S(1)}, bf16[384,192]{0,1:T(8,128)(2,1)S(1)}, u32[]{:S(2)}, u32[]{:S(2)}) collective-permute-start(bf16[384,192]{0,1:T(8,128)(2,1)S(1)} %reshape.226), channel_id=1, source_target_pairs={{0,2},{1,3},{2,0},{3,1},{4,6},{5,7},{6,4},{7,5},{8,10},{9,11},{10,... | collective-permute-start | bytes 442376 | tf_op jit(solution)/shard_map/ppermute | solution.py:14
  11.7 9.1 %collective-permute-start.9 = (bf16[384,192]{0,1:T(8,128)(2,1)S(1)}, bf16[384,192]{0,1:T(8,128)(2,1)S(1)}, u32[]{:S(2)}, u32[]{:S(2)}) collective-permute-start(bf16[384,192]{0,1:T(8,128)(2,1)S(1)} %reshape.226), channel_id=1, source_target_pairs={{0,3},{1,0},{2,1},{3,2},{4,7},{5,4},{6,5},{7,6},{8,11},{9,8},{10,9... | collective-permute-start | bytes 442376 | tf_op jit(solution)/shard_map/ppermute | solution.py:14
  14.1 7.9 %collective-permute-start.3 = (bf16[384,192]{0,1:T(8,128)(2,1)S(1)}, bf16[384,192]{0,1:T(8,128)(2,1)S(1)}, u32[]{:S(2)}, u32[]{:S(2)}) collective-permute-start(bf16[384,192]{0,1:T(8,128)(2,1)S(1)} %reshape.226), channel_id=1, source_target_pairs={{0,4},{4,0},{8,12},{12,8},{16,20},{20,16},{24,28},{28,24},{1,5},{5... | collective-permute-start | bytes 442376 | tf_op jit(solution)/shard_map/ppermute | solution.py:23
  14.2 7.8 %collective-permute-start.4 = (bf16[384,192]{0,1:T(8,128)(2,1)S(1)}, bf16[384,192]{0,1:T(8,128)(2,1)S(1)}, u32[]{:S(2)}, u32[]{:S(2)}) collective-permute-start(bf16[384,192]{0,1:T(8,128)(2,1)S(1)} %collective-permute-done), channel_id=1, source_target_pairs={{0,4},{4,0},{8,12},{12,8},{16,20},{20,16},{24,28},{28,24},{1,5},{5... | collective-permute-start | bytes 442376 | tf_op jit(solution)/shard_map/ppermute | solution.py:23
  16.0 6.0 %collective-permute-start.5 = (bf16[384,192]{0,1:T(8,128)(2,1)S(1)}, bf16[384,192]{0,1:T(8,128)(2,1)S(1)}, u32[]{:S(2)}, u32[]{:S(2)}) collective-permute-start(bf16[384,192]{0,1:T(8,128)(2,1)S(1)} %collective-permute-done.1), channel_id=1, source_target_pairs={{0,4},{4,0},{8,12},{12,8},{16,20},{20,16},{24,28},{28,24},{1,5},{5... | collective-permute-start | bytes 442376 | tf_op jit(solution)/shard_map/ppermute | solution.py:23
  20.6 1.4 %collective-permute-start.6 = (bf16[384,192]{0,1:T(8,128)(2,1)S(1)}, bf16[384,192]{0,1:T(8,128)(2,1)S(1)}, u32[]{:S(2)}, u32[]{:S(2)}) collective-permute-start(bf16[384,192]{0,1:T(8,128)(2,1)S(1)} %collective-permute-done.2), channel_id=1, source_target_pairs={{0,4},{4,0},{8,12},{12,8},{16,20},{20,16},{24,28},{28,24},{1,5},{5... | collective-permute-start | bytes 442376 | tf_op jit(solution)/shard_map/ppermute | solution.py:23
  22.4 4.1 %copy-start.1 = (s32[1,13]{1,0:T(1,128)S(1)}, s32[1,13]{1,0:T(1,128)}, u32[]{:S(2)}) copy-start(s32[1,13]{1,0:T(1,128)} %param.5) | copy-start | bytes 160
  22.9 9.9 %collective-permute-start.10 = (f32[384,192]{0,1:T(8,128)S(1)}, f32[384,192]{0,1:T(8,128)S(1)}, u32[]{:S(2)}, u32[]{:S(2)}) collective-permute-start(f32[384,192]{0,1:T(8,128)S(1)} %bitcast.72), channel_id=1, source_target_pairs={{0,8},{4,12},{8,0},{12,4},{16,24},{20,28},{24,16},{28,20},{1,9},{5... | collective-permute-start | bytes 884744 | tf_op jit(solution)/shard_map/ppermute | solution.py:22
  24.5 15.5 %collective-permute-start.11 = (f32[384,192]{0,1:T(8,128)S(1)}, f32[384,192]{0,1:T(8,128)S(1)}, u32[]{:S(2)}, u32[]{:S(2)}) collective-permute-start(f32[384,192]{0,1:T(8,128)S(1)} %bitcast.73), channel_id=1, source_target_pairs={{0,16},{4,20},{8,24},{12,28},{16,0},{20,4},{24,8},{28,12},{1,17},{... | collective-permute-start | bytes 884744 | tf_op jit(solution)/shard_map/ppermute | solution.py:22
  26.0 13.9 %collective-permute-start.12 = (f32[384,192]{0,1:T(8,128)S(1)}, f32[384,192]{0,1:T(8,128)S(1)}, u32[]{:S(2)}, u32[]{:S(2)}) collective-permute-start(f32[384,192]{0,1:T(8,128)S(1)} %bitcast.74), channel_id=1, source_target_pairs={{0,24},{4,28},{8,16},{12,20},{16,8},{20,12},{24,0},{28,4},{1,25},{... | collective-permute-start | bytes 884744 | tf_op jit(solution)/shard_map/ppermute | solution.py:22
  26.5 14.1 %collective-permute-start.13 = (f32[384,192]{0,1:T(8,128)S(1)}, f32[384,192]{0,1:T(8,128)S(1)}, u32[]{:S(2)}, u32[]{:S(2)}) collective-permute-start(f32[384,192]{0,1:T(8,128)S(1)} %bitcast.75), channel_id=1, source_target_pairs={{0,4},{4,0},{8,12},{12,8},{16,20},{20,16},{24,28},{28,24},{1,5},{5... | collective-permute-start | bytes 884744 | tf_op jit(solution)/shard_map/ppermute | solution.py:23
  32.9 7.7 %collective-permute-start.14 = (f32[384,192]{0,1:T(8,128)S(1)}, f32[384,192]{0,1:T(8,128)S(1)}, u32[]{:S(2)}, u32[]{:S(2)}) collective-permute-start(f32[384,192]{0,1:T(8,128)S(1)} %collective-permute-done.10), channel_id=1, source_target_pairs={{0,4},{4,0},{8,12},{12,8},{16,20},{20,16},{24,28},{28,24},{1,5},{5... | collective-permute-start | bytes 884744 | tf_op jit(solution)/shard_map/ppermute | solution.py:23
  39.9 1.6 %collective-permute-start.15 = (f32[384,192]{0,1:T(8,128)S(1)}, f32[384,192]{0,1:T(8,128)S(1)}, u32[]{:S(2)}, u32[]{:S(2)}) collective-permute-start(f32[384,192]{0,1:T(8,128)S(1)} %collective-permute-done.11), channel_id=1, source_target_pairs={{0,4},{4,0},{8,12},{12,8},{16,20},{20,16},{24,28},{28,24},{1,5},{5... | collective-permute-start | bytes 884744 | tf_op jit(solution)/shard_map/ppermute | solution.py:23
  39.9 2.0 %collective-permute-start.16 = (f32[384,192]{0,1:T(8,128)S(1)}, f32[384,192]{0,1:T(8,128)S(1)}, u32[]{:S(2)}, u32[]{:S(2)}) collective-permute-start(f32[384,192]{0,1:T(8,128)S(1)} %collective-permute-done.12), channel_id=1, source_target_pairs={{0,4},{4,0},{8,12},{12,8},{16,20},{20,16},{24,28},{28,24},{1,5},{5... | collective-permute-start | bytes 884744 | tf_op jit(solution)/shard_map/ppermute | solution.py:23

commit v7 on v6

--- a/solution.py
+++ b/solution.py
@@ -68,8 +68,10 @@
     new_grid = combined.reshape(rows_dev, block_edge, COLS_DEV, block_edge).transpose(0, 2, 1, 3)
     new_grid = new_grid.reshape(cells, area)
     out_ids = out_slots[0]
-    picked = new_grid[jnp.minimum(out_ids, cells - 1)]
-    picked = jnp.where((out_ids < cells)[:, None], picked, jnp.zeros_like(picked))
+    choose = (out_ids[:, None] == jnp.arange(cells, dtype=jnp.int32)[None, :]).astype(jnp.float32)
+    picked = jnp.dot(
+        choose, new_grid, precision=lax.Precision.HIGHEST, preferred_element_type=jnp.float32
+    )
     return picked[None]
 
 

time: 46.2 us -> 45.6 us (0.987)
  starting transfers between devices: 16.1 us -> 13.5 us
  waiting for transfers between devices: 20.8 us -> 23.2 us
    ppermute x3, waiting for transfers between devices: 5.94 us -> 8.69 us  [shifted_copies(): pieces.append(lax.ppermute(value, axis, pairs))]
    ppermute x3, starting transfers between devices: 6.92 us -> 5.4 us  [shifted_copies(): pieces.append(lax.ppermute(value, axis, pairs))]
    ppermute x6, starting transfers between devices: 8.12 us -> 7.04 us  [paired_copies(): pieces.append(lax.ppermute(value, axis, pairs))]
    broadcast_in_dim x0 -> x1, local copies, waits for them, and re-layouts: none -> 0.9 us  [on_device(): return picked[None]]
    select_n x1 -> x0, local copies, waits for them, and re-layouts: 0.9 us -> none  [on_device(): jnp.where((out_ids < cells)[:, None], picked, jnp.zeros_like(picked))]
    gather x1 -> x0, local copies, waits for them, and re-layouts: 0.63 us -> none  [on_device(): picked = new_grid[jnp.minimum(out_ids, cells - 1)]]
where the time goes in v7:
time: 45.6 us; the launch traced here: 45.5 us
  waiting for transfers between devices  23.2 us (51%)
  starting transfers between devices  13.5 us (30%)
  local copies, waits for them, and re-layouts  4.97 us (11%)
  matrix products  2.22 us (5%)
  other arithmetic  1.43 us (3%)
    ppermute x6, waiting for transfers between devices, paired_copies(): pieces.append(lax.ppermute(value, axis, pairs))  13 us
    ppermute x3, waiting for transfers between devices, shifted_copies(): pieces.append(lax.ppermute(value, axis, pairs))  8.69 us
    ppermute x6, starting transfers between devices, paired_copies(): pieces.append(lax.ppermute(value, axis, pairs))  7.04 us
    ppermute x3, starting transfers between devices, shifted_copies(): pieces.append(lax.ppermute(value, axis, pairs))  5.4 us
    ppermute x8, waiting for transfers between devices, paired_copies(): lax.ppermute(piece, axis, [(i, i ^ 1) for i in range(size)])  1.48 us
    dot_general x1, matrix products, on_device(): jnp.einsum('pab,pbn->an', square_panel, column_panel.astype(jnp.float32),...  1.38 us
    ppermute x8, starting transfers between devices, paired_copies(): lax.ppermute(piece, axis, [(i, i ^ 1) for i in range(size)])  1.03 us
  transfers between devices with their start and end apart: 17, of which 6 were waited for; matrix products, arithmetic and copies ran while one was open for 3% of the time, Pallas kernels for 0%

profile of v7, /device:TPU:0, one launch (start us, length us, event | category | flops | bytes accessed | tf_op | source)
XLA Modules:
  0.0 45.5 jit_solution(14955579532613324839)
XLA Ops:
  0.0 0.7 %fusion.14 = s32[9]{0:T(128)S(1)} fusion(s32[1,9]{1,0:T(1,128)} %param.4), kind=kLoop, calls=%fused_computation.38 | loop fusion | flops 45 | bytes 72 | tf_op jit(solution)/shard_map/select_n | solution.py:44
  0.9 0.8 %scatter_custom_fusion = bf16[18,4096]{1,0:T(8,128)(2,1)S(1)} fusion(s32[9]{0:T(128)S(1)} %fusion.14, bf16[1,9,4096]{2,1,0:T(8,128)(2,1)S(1)} %copy-done, bf16[]{:T(256)} %constant.46.clone.1), kind=kCustom, calls=%fused_computation.18 | custom fusion | bytes 278530 | tf_op jit(solution)/shard_map/scatter | solution.py:44
  1.7 0.3 reshape.172
  2.5 5.1 %collective-permute-start.9 = (bf16[384,192]{0,1:T(8,128)(2,1)S(1)}, bf16[384,192]{0,1:T(8,128)(2,1)S(1)}, u32[]{:S(2)}, u32[]{:S(2)}) collective-permute-start(bf16[384,192]{0,1:T(8,128)(2,1)S(1)} %reshape.173), channel_id=1, source_target_pairs={{0,3},{1,0},{2,1},{3,2},{4,7},{5,4},{6,5},{7,6},{8,11},{9,8},{10,9... | collective-permute-start | bytes 442376 | tf_op jit(solution)/shard_map/ppermute | solution.py:14
  7.7 2.4 %collective-permute-start.2 = (bf16[384,192]{0,1:T(8,128)(2,1)S(1)}, bf16[384,192]{0,1:T(8,128)(2,1)S(1)}, u32[]{:S(2)}, u32[]{:S(2)}) collective-permute-start(bf16[384,192]{0,1:T(8,128)(2,1)S(1)} %reshape.173), channel_id=1, source_target_pairs={{0,24},{4,28},{8,16},{12,20},{16,8},{20,12},{24,0},{28,4},{1,25},{... | collective-permute-start | bytes 442376 | tf_op jit(solution)/shard_map/ppermute | solution.py:22
  10.1 0.5 %collective-permute-start.1 = (bf16[384,192]{0,1:T(8,128)(2,1)S(1)}, bf16[384,192]{0,1:T(8,128)(2,1)S(1)}, u32[]{:S(2)}, u32[]{:S(2)}) collective-permute-start(bf16[384,192]{0,1:T(8,128)(2,1)S(1)} %reshape.173), channel_id=1, source_target_pairs={{0,16},{4,20},{8,24},{12,28},{16,0},{20,4},{24,8},{28,12},{1,17},{... | collective-permute-start | bytes 442376 | tf_op jit(solution)/shard_map/ppermute | solution.py:22
  10.6 0.5 %collective-permute-start = (bf16[384,192]{0,1:T(8,128)(2,1)S(1)}, bf16[384,192]{0,1:T(8,128)(2,1)S(1)}, u32[]{:S(2)}, u32[]{:S(2)}) collective-permute-start(bf16[384,192]{0,1:T(8,128)(2,1)S(1)} %reshape.173), channel_id=1, source_target_pairs={{0,8},{4,12},{8,0},{12,4},{16,24},{20,28},{24,16},{28,20},{1,9},{5... | collective-permute-start | bytes 442376 | tf_op jit(solution)/shard_map/ppermute | solution.py:22
  11.2 0.7 %collective-permute-done.9 = bf16[384,192]{0,1:T(8,128)(2,1)S(1)} collective-permute-done((bf16[384,192]{0,1:T(8,128)(2,1)S(1)}, bf16[384,192]{0,1:T(8,128)(2,1)S(1)}, u32[]{:S(2)}, u32[]{:S(2)}) %collective-permute-start.9) | collective-permute-done | bytes 147488 | tf_op jit(solution)/shard_map/ppermute | solution.py:14
  12.2 7.9 %collective-permute-done.8 = bf16[384,192]{0,1:T(8,128)(2,1)S(1)} collective-permute-done((bf16[384,192]{0,1:T(8,128)(2,1)S(1)}, bf16[384,192]{0,1:T(8,128)(2,1)S(1)}, u32[]{:S(2)}, u32[]{:S(2)}) %collective-permute-start.8) | collective-permute-done | bytes 147488 | tf_op jit(solution)/shard_map/ppermute | solution.py:14
  20.1 0.5 %collective-permute-start.6 = (bf16[384,192]{0,1:T(8,128)(2,1)S(1)}, bf16[384,192]{0,1:T(8,128)(2,1)S(1)}, u32[]{:S(2)}, u32[]{:S(2)}) collective-permute-start(bf16[384,192]{0,1:T(8,128)(2,1)S(1)} %collective-permute-done.2), channel_id=1, source_target_pairs={{0,4},{4,0},{8,12},{12,8},{16,20},{20,16},{24,28},{28,24},{1,5},{5... | collective-permute-start | bytes 442376 | tf_op jit(solution)/shard_map/ppermute | solution.py:23
  20.7 0.4 collective-permute-start.4
  21.6 0.3 copy.18
  21.9 0.6 %gather_fusion = bf16[8,192,192]{2,1,0:T(8,128)(2,1)S(1)} fusion(bf16[8,192,192]{2,1,0:T(8,128)(2,1)S(1)} %bitcast.67, s32[1024]{0:T(1024)S(1)} %pad_clamp_fusion), kind=kCustom, calls=%fused_computation | custom fusion | bytes 1179680 | tf_op jit(solution)/shard_map/gather | solution.py:54
  22.9 0.5 %fusion.16 = f32[384,192,1]{0,1,2:T(8,128)S(1)} fusion(bf16[8,384,192]{1,2,0:T(8,128)(2,1)S(1)} %bitcast.66, bf16[8,192,192]{2,1,0:T(8,128)(2,1)S(1)} %gather_fusion), kind=kOutput, calls=%fused_computation.40 | convolution fusion | flops 226492416 | bytes 2064384 | tf_op jit(solution)/shard_map/pab,pbn->an/dot_general | solution.py:56
  23.5 1.6 %collective-permute-start.11 = (f32[384,192]{0,1:T(8,128)S(1)}, f32[384,192]{0,1:T(8,128)S(1)}, u32[]{:S(2)}, u32[]{:S(2)}) collective-permute-start(f32[384,192]{0,1:T(8,128)S(1)} %bitcast.69), channel_id=1, source_target_pairs={{0,16},{4,20},{8,24},{12,28},{16,0},{20,4},{24,8},{28,12},{1,17},{... | collective-permute-start | bytes 884744 | tf_op jit(solution)/shard_map/ppermute | solution.py:22
  25.1 1.5 %collective-permute-start.10 = (f32[384,192]{0,1:T(8,128)S(1)}, f32[384,192]{0,1:T(8,128)S(1)}, u32[]{:S(2)}, u32[]{:S(2)}) collective-permute-start(f32[384,192]{0,1:T(8,128)S(1)} %bitcast.70), channel_id=1, source_target_pairs={{0,8},{4,12},{8,0},{12,4},{16,24},{20,28},{24,16},{28,20},{1,9},{5... | collective-permute-start | bytes 884744 | tf_op jit(solution)/shard_map/ppermute | solution.py:22
  26.6 0.5 %collective-permute-start.12 = (f32[384,192]{0,1:T(8,128)S(1)}, f32[384,192]{0,1:T(8,128)S(1)}, u32[]{:S(2)}, u32[]{:S(2)}) collective-permute-start(f32[384,192]{0,1:T(8,128)S(1)} %bitcast.71), channel_id=1, source_target_pairs={{0,24},{4,28},{8,16},{12,20},{16,8},{20,12},{24,0},{28,4},{1,25},{... | collective-permute-start | bytes 884744 | tf_op jit(solution)/shard_map/ppermute | solution.py:22
  27.0 5.5 %collective-permute-done.11 = f32[384,192]{0,1:T(8,128)S(1)} collective-permute-done((f32[384,192]{0,1:T(8,128)S(1)}, f32[384,192]{0,1:T(8,128)S(1)}, u32[]{:S(2)}, u32[]{:S(2)}) %collective-permute-start.11) | collective-permute-done | bytes 294944 | tf_op jit(solution)/shard_map/ppermute | solution.py:22
  32.5 2.4 %collective-permute-done.10 = f32[384,192]{0,1:T(8,128)S(1)} collective-permute-done((f32[384,192]{0,1:T(8,128)S(1)}, f32[384,192]{0,1:T(8,128)S(1)}, u32[]{:S(2)}, u32[]{:S(2)}) %collective-permute-start.10) | collective-permute-done | bytes 294944 | tf_op jit(solution)/shard_map/ppermute | solution.py:22
  35.0 5.1 %collective-permute-done.12 = f32[384,192]{0,1:T(8,128)S(1)} collective-permute-done((f32[384,192]{0,1:T(8,128)S(1)}, f32[384,192]{0,1:T(8,128)S(1)}, u32[]{:S(2)}, u32[]{:S(2)}) %collective-permute-start.12) | collective-permute-done | bytes 294944 | tf_op jit(solution)/shard_map/ppermute | solution.py:22
  40.1 1.5 %collective-permute-done.16 = f32[384,192]{0,1:T(8,128)S(1)} collective-permute-done((f32[384,192]{0,1:T(8,128)S(1)}, f32[384,192]{0,1:T(8,128)S(1)}, u32[]{:S(2)}, u32[]{:S(2)}) %collective-permute-start.16) | collective-permute-done | bytes 294944 | tf_op jit(solution)/shard_map/ppermute | solution.py:23
  42.0 1.4 %fusion.1 = f32[384,192]{0,1:T(8,128)S(1)} fusion(f32[8,384,192]{1,2,0:T(8,128)S(1)} %bitcast.65, bf16[8,192,192]{2,1,0:T(8,128)(2,1)S(1)} %gather_fusion, f32[384,192,1]{0,1,2:T(8,128)S(1)} %fusion.16), kind=kOutput, calls=%fused_computation.9 | convolution fusion | flops 1359175680 | bytes 3538944 | tf_op jit(solution)/shard_map/pab,pbn->an/dot_general | solution.py:60
  44.2 0.3 convolution_bitcast_fusion
  44.6 0.9 %copy.15 = f32[1,13,4096]{2,0,1:T(1,128)} copy(f32[1,13,4096]{2,1,0:T(8,128)S(1)} %convolution_bitcast_fusion) | data formatting | bytes 425984 | tf_op jit(solution)/shard_map/broadcast_in_dim | solution.py:75
  (39 shorter events, 3.2 us)
Async XLA Ops:
  0.0 0.9 %copy-start = (bf16[1,9,4096]{2,1,0:T(8,128)(2,1)S(1)}, bf16[1,9,4096]{2,1,0:T(8,128)(2,1)}, u32[]{:S(2)}) copy-start(bf16[1,9,4096]{2,1,0:T(8,128)(2,1)} %param.3) | copy-start | bytes 221188
  2.5 9.4 %collective-permute-start.9 = (bf16[384,192]{0,1:T(8,128)(2,1)S(1)}, bf16[384,192]{0,1:T(8,128)(2,1)S(1)}, u32[]{:S(2)}, u32[]{:S(2)}) collective-permute-start(bf16[384,192]{0,1:T(8,128)(2,1)S(1)} %reshape.173), channel_id=1, source_target_pairs={{0,3},{1,0},{2,1},{3,2},{4,7},{5,4},{6,5},{7,6},{8,11},{9,8},{10,9... | collective-permute-start | bytes 442376 | tf_op jit(solution)/shard_map/ppermute | solution.py:14
  7.7 12.5 %collective-permute-start.8 = (bf16[384,192]{0,1:T(8,128)(2,1)S(1)}, bf16[384,192]{0,1:T(8,128)(2,1)S(1)}, u32[]{:S(2)}, u32[]{:S(2)}) collective-permute-start(bf16[384,192]{0,1:T(8,128)(2,1)S(1)} %reshape.173), channel_id=1, source_target_pairs={{0,2},{1,3},{2,0},{3,1},{4,6},{5,7},{6,4},{7,5},{8,10},{9,11},{10,... | collective-permute-start | bytes 442376 | tf_op jit(solution)/shard_map/ppermute | solution.py:14
  7.7 12.5 %collective-permute-start.2 = (bf16[384,192]{0,1:T(8,128)(2,1)S(1)}, bf16[384,192]{0,1:T(8,128)(2,1)S(1)}, u32[]{:S(2)}, u32[]{:S(2)}) collective-permute-start(bf16[384,192]{0,1:T(8,128)(2,1)S(1)} %reshape.173), channel_id=1, source_target_pairs={{0,24},{4,28},{8,16},{12,20},{16,8},{20,12},{24,0},{28,4},{1,25},{... | collective-permute-start | bytes 442376 | tf_op jit(solution)/shard_map/ppermute | solution.py:22
  10.1 10.5 %collective-permute-start.1 = (bf16[384,192]{0,1:T(8,128)(2,1)S(1)}, bf16[384,192]{0,1:T(8,128)(2,1)S(1)}, u32[]{:S(2)}, u32[]{:S(2)}) collective-permute-start(bf16[384,192]{0,1:T(8,128)(2,1)S(1)} %reshape.173), channel_id=1, source_target_pairs={{0,16},{4,20},{8,24},{12,28},{16,0},{20,4},{24,8},{28,12},{1,17},{... | collective-permute-start | bytes 442376 | tf_op jit(solution)/shard_map/ppermute | solution.py:22
  10.6 10.1 %collective-permute-start = (bf16[384,192]{0,1:T(8,128)(2,1)S(1)}, bf16[384,192]{0,1:T(8,128)(2,1)S(1)}, u32[]{:S(2)}, u32[]{:S(2)}) collective-permute-start(bf16[384,192]{0,1:T(8,128)(2,1)S(1)} %reshape.173), channel_id=1, source_target_pairs={{0,8},{4,12},{8,0},{12,4},{16,24},{20,28},{24,16},{28,20},{1,9},{5... | collective-permute-start | bytes 442376 | tf_op jit(solution)/shard_map/ppermute | solution.py:22
  11.9 9.6 %collective-permute-start.7 = (bf16[384,192]{0,1:T(8,128)(2,1)S(1)}, bf16[384,192]{0,1:T(8,128)(2,1)S(1)}, u32[]{:S(2)}, u32[]{:S(2)}) collective-permute-start(bf16[384,192]{0,1:T(8,128)(2,1)S(1)} %reshape.173), channel_id=1, source_target_pairs={{0,1},{1,2},{2,3},{3,0},{4,5},{5,6},{6,7},{7,4},{8,9},{9,10},{10,1... | collective-permute-start | bytes 442376 | tf_op jit(solution)/shard_map/ppermute | solution.py:14
  20.1 2.4 %collective-permute-start.3 = (bf16[384,192]{0,1:T(8,128)(2,1)S(1)}, bf16[384,192]{0,1:T(8,128)(2,1)S(1)}, u32[]{:S(2)}, u32[]{:S(2)}) collective-permute-start(bf16[384,192]{0,1:T(8,128)(2,1)S(1)} %reshape.173), channel_id=1, source_target_pairs={{0,4},{4,0},{8,12},{12,8},{16,20},{20,16},{24,28},{28,24},{1,5},{5... | collective-permute-start | bytes 442376 | tf_op jit(solution)/shard_map/ppermute | solution.py:23
  20.1 2.4 %collective-permute-start.6 = (bf16[384,192]{0,1:T(8,128)(2,1)S(1)}, bf16[384,192]{0,1:T(8,128)(2,1)S(1)}, u32[]{:S(2)}, u32[]{:S(2)}) collective-permute-start(bf16[384,192]{0,1:T(8,128)(2,1)S(1)} %collective-permute-done.2), channel_id=1, source_target_pairs={{0,4},{4,0},{8,12},{12,8},{16,20},{20,16},{24,28},{28,24},{1,5},{5... | collective-permute-start | bytes 442376 | tf_op jit(solution)/shard_map/ppermute | solution.py:23
  20.7 1.9 %collective-permute-start.5 = (bf16[384,192]{0,1:T(8,128)(2,1)S(1)}, bf16[384,192]{0,1:T(8,128)(2,1)S(1)}, u32[]{:S(2)}, u32[]{:S(2)}) collective-permute-start(bf16[384,192]{0,1:T(8,128)(2,1)S(1)} %collective-permute-done.1), channel_id=1, source_target_pairs={{0,4},{4,0},{8,12},{12,8},{16,20},{20,16},{24,28},{28,24},{1,5},{5... | collective-permute-start | bytes 442376 | tf_op jit(solution)/shard_map/ppermute | solution.py:23
  20.7 1.8 %collective-permute-start.4 = (bf16[384,192]{0,1:T(8,128)(2,1)S(1)}, bf16[384,192]{0,1:T(8,128)(2,1)S(1)}, u32[]{:S(2)}, u32[]{:S(2)}) collective-permute-start(bf16[384,192]{0,1:T(8,128)(2,1)S(1)} %collective-permute-done), channel_id=1, source_target_pairs={{0,4},{4,0},{8,12},{12,8},{16,20},{20,16},{24,28},{28,24},{1,5},{5... | collective-permute-start | bytes 442376 | tf_op jit(solution)/shard_map/ppermute | solution.py:23
  23.5 9.0 %collective-permute-start.11 = (f32[384,192]{0,1:T(8,128)S(1)}, f32[384,192]{0,1:T(8,128)S(1)}, u32[]{:S(2)}, u32[]{:S(2)}) collective-permute-start(f32[384,192]{0,1:T(8,128)S(1)} %bitcast.69), channel_id=1, source_target_pairs={{0,16},{4,20},{8,24},{12,28},{16,0},{20,4},{24,8},{28,12},{1,17},{... | collective-permute-start | bytes 884744 | tf_op jit(solution)/shard_map/ppermute | solution.py:22
  25.1 9.9 %collective-permute-start.10 = (f32[384,192]{0,1:T(8,128)S(1)}, f32[384,192]{0,1:T(8,128)S(1)}, u32[]{:S(2)}, u32[]{:S(2)}) collective-permute-start(f32[384,192]{0,1:T(8,128)S(1)} %bitcast.70), channel_id=1, source_target_pairs={{0,8},{4,12},{8,0},{12,4},{16,24},{20,28},{24,16},{28,20},{1,9},{5... | collective-permute-start | bytes 884744 | tf_op jit(solution)/shard_map/ppermute | solution.py:22
  26.6 13.5 %collective-permute-start.12 = (f32[384,192]{0,1:T(8,128)S(1)}, f32[384,192]{0,1:T(8,128)S(1)}, u32[]{:S(2)}, u32[]{:S(2)}) collective-permute-start(f32[384,192]{0,1:T(8,128)S(1)} %bitcast.71), channel_id=1, source_target_pairs={{0,24},{4,28},{8,16},{12,20},{16,8},{20,12},{24,0},{28,4},{1,25},{... | collective-permute-start | bytes 884744 | tf_op jit(solution)/shard_map/ppermute | solution.py:22
  27.0 13.1 %collective-permute-start.13 = (f32[384,192]{0,1:T(8,128)S(1)}, f32[384,192]{0,1:T(8,128)S(1)}, u32[]{:S(2)}, u32[]{:S(2)}) collective-permute-start(f32[384,192]{0,1:T(8,128)S(1)} %bitcast.72), channel_id=1, source_target_pairs={{0,4},{4,0},{8,12},{12,8},{16,20},{20,16},{24,28},{28,24},{1,5},{5... | collective-permute-start | bytes 884744 | tf_op jit(solution)/shard_map/ppermute | solution.py:23
  32.5 7.6 %collective-permute-start.15 = (f32[384,192]{0,1:T(8,128)S(1)}, f32[384,192]{0,1:T(8,128)S(1)}, u32[]{:S(2)}, u32[]{:S(2)}) collective-permute-start(f32[384,192]{0,1:T(8,128)S(1)} %collective-permute-done.11), channel_id=1, source_target_pairs={{0,4},{4,0},{8,12},{12,8},{16,20},{20,16},{24,28},{28,24},{1,5},{5... | collective-permute-start | bytes 884744 | tf_op jit(solution)/shard_map/ppermute | solution.py:23
  34.9 5.2 %collective-permute-start.14 = (f32[384,192]{0,1:T(8,128)S(1)}, f32[384,192]{0,1:T(8,128)S(1)}, u32[]{:S(2)}, u32[]{:S(2)}) collective-permute-start(f32[384,192]{0,1:T(8,128)S(1)} %collective-permute-done.10), channel_id=1, source_target_pairs={{0,4},{4,0},{8,12},{12,8},{16,20},{20,16},{24,28},{28,24},{1,5},{5... | collective-permute-start | bytes 884744 | tf_op jit(solution)/shard_map/ppermute | solution.py:23
  40.0 1.6 %collective-permute-start.16 = (f32[384,192]{0,1:T(8,128)S(1)}, f32[384,192]{0,1:T(8,128)S(1)}, u32[]{:S(2)}, u32[]{:S(2)}) collective-permute-start(f32[384,192]{0,1:T(8,128)S(1)} %collective-permute-done.12), channel_id=1, source_target_pairs={{0,4},{4,0},{8,12},{12,8},{16,20},{20,16},{24,28},{28,24},{1,5},{5... | collective-permute-start | bytes 884744 | tf_op jit(solution)/shard_map/ppermute | solution.py:23
  43.6 0.7 %copy-start.1 = (s32[1,13]{1,0:T(1,128)S(1)}, s32[1,13]{1,0:T(1,128)}, u32[]{:S(2)}) copy-start(s32[1,13]{1,0:T(1,128)} %param.5) | copy-start | bytes 160

commit v8 on v7

--- a/solution.py
+++ b/solution.py
@@ -49,9 +49,13 @@
     )
 
     row_panel = paired_copies(tile, "col", n_col)
-    down = shifted_copies(tile, "row", n_row).reshape(n_row * group, width, width)
+    down = [tile]
+    for shift in range(1, n_row):
+        pairs = [(i, (i - shift) % n_row) for i in range(n_row)]
+        down.append(lax.ppermute(tile, "row", pairs))
+    down = jnp.stack(down).reshape(n_row * group, width, width)
     source = col_idx ^ jnp.arange(n_col, dtype=jnp.int32)
-    column_panel = down[((row_idx - source // group) % n_row) * group + source % group]
+    column_panel = down[((source // group - row_idx) % n_row) * group + source % group]
 
     square = jnp.einsum(
         "pab,pbn->an", row_panel, column_panel, preferred_element_type=jnp.float32

time: 45.6 us -> 43.5 us (0.954)
  waiting for transfers between devices: 23.2 us -> 19.5 us
  starting transfers between devices: 13.5 us -> 15 us
    ppermute x3, waiting for transfers between devices: 8.69 us -> 5.31 us  [on_device(): down.append(lax.ppermute(tile, 'row', pairs))]
    ppermute x3, starting transfers between devices: 5.4 us -> 6.95 us  [on_device(): down.append(lax.ppermute(tile, 'row', pairs))]
  transfers between devices with their start and end apart: 17 -> 17, of which waited for: 6 -> 7; matrix products, arithmetic and copies ran while one was open for 3% -> 3% of each run, Pallas kernels for 0% -> 0%
where the time goes in v8:
time: 43.5 us; the launch traced here: 43.3 us
  waiting for transfers between devices  19.5 us (45%)
  starting transfers between devices  15 us (34%)
  local copies, waits for them, and re-layouts  4.97 us (11%)
  matrix products  2.22 us (5%)
  other arithmetic  1.42 us (3%)
    ppermute x6, waiting for transfers between devices, paired_copies(): pieces.append(lax.ppermute(value, axis, pairs))  12.7 us
    ppermute x6, starting transfers between devices, paired_copies(): pieces.append(lax.ppermute(value, axis, pairs))  7.04 us
    ppermute x3, starting transfers between devices, on_device(): down.append(lax.ppermute(tile, 'row', pairs))  6.95 us
    ppermute x3, waiting for transfers between devices, on_device(): down.append(lax.ppermute(tile, 'row', pairs))  5.31 us
    ppermute x8, waiting for transfers between devices, paired_copies(): lax.ppermute(piece, axis, [(i, i ^ 1) for i in range(size)])  1.48 us
    dot_general x1, matrix products, on_device(): jnp.einsum('pab,pbn->an', square_panel, column_panel.astype(jnp.float32),...  1.38 us
    ppermute x8, starting transfers between devices, paired_copies(): lax.ppermute(piece, axis, [(i, i ^ 1) for i in range(size)])  1.03 us
    broadcast_in_dim x1, local copies, waits for them, and re-layouts, on_device(): return picked[None]  0.9 us
  transfers between devices with their start and end apart: 17, of which 7 were waited for; matrix products, arithmetic and copies ran while one was open for 3% of the time, Pallas kernels for 0%

profile of v8, /device:TPU:0, one launch (start us, length us, event | category | flops | bytes accessed | tf_op | source)
XLA Modules:
  0.0 43.3 jit_solution(12227310051030861285)
XLA Ops:
  0.0 0.7 %fusion.14 = s32[9]{0:T(128)S(1)} fusion(s32[1,9]{1,0:T(1,128)} %param.4), kind=kLoop, calls=%fused_computation.38 | loop fusion | flops 45 | bytes 72 | tf_op jit(solution)/shard_map/select_n | solution.py:44
  0.9 0.8 %scatter_custom_fusion = bf16[18,4096]{1,0:T(8,128)(2,1)S(1)} fusion(s32[9]{0:T(128)S(1)} %fusion.14, bf16[1,9,4096]{2,1,0:T(8,128)(2,1)S(1)} %copy-done, bf16[]{:T(256)} %constant.46.clone.1), kind=kCustom, calls=%fused_computation.18 | custom fusion | bytes 278530 | tf_op jit(solution)/shard_map/scatter | solution.py:44
  2.5 3.1 %collective-permute-start.9 = (bf16[384,192]{0,1:T(8,128)(2,1)S(1)}, bf16[384,192]{0,1:T(8,128)(2,1)S(1)}, u32[]{:S(2)}, u32[]{:S(2)}) collective-permute-start(bf16[384,192]{0,1:T(8,128)(2,1)S(1)} %reshape.173), channel_id=1, source_target_pairs={{0,1},{1,2},{2,3},{3,0},{4,5},{5,6},{6,7},{7,4},{8,9},{9,10},{10,1... | collective-permute-start | bytes 442376 | tf_op jit(solution)/shard_map/ppermute | solution.py:55
  5.6 2.6 %collective-permute-start.8 = (bf16[384,192]{0,1:T(8,128)(2,1)S(1)}, bf16[384,192]{0,1:T(8,128)(2,1)S(1)}, u32[]{:S(2)}, u32[]{:S(2)}) collective-permute-start(bf16[384,192]{0,1:T(8,128)(2,1)S(1)} %reshape.173), channel_id=1, source_target_pairs={{0,2},{1,3},{2,0},{3,1},{4,6},{5,7},{6,4},{7,5},{8,10},{9,11},{10,... | collective-permute-start | bytes 442376 | tf_op jit(solution)/shard_map/ppermute | solution.py:55
  8.2 2.4 %collective-permute-start.2 = (bf16[384,192]{0,1:T(8,128)(2,1)S(1)}, bf16[384,192]{0,1:T(8,128)(2,1)S(1)}, u32[]{:S(2)}, u32[]{:S(2)}) collective-permute-start(bf16[384,192]{0,1:T(8,128)(2,1)S(1)} %reshape.173), channel_id=1, source_target_pairs={{0,24},{4,28},{8,16},{12,20},{16,8},{20,12},{24,0},{28,4},{1,25},{... | collective-permute-start | bytes 442376 | tf_op jit(solution)/shard_map/ppermute | solution.py:22
  10.7 0.5 %collective-permute-start.1 = (bf16[384,192]{0,1:T(8,128)(2,1)S(1)}, bf16[384,192]{0,1:T(8,128)(2,1)S(1)}, u32[]{:S(2)}, u32[]{:S(2)}) collective-permute-start(bf16[384,192]{0,1:T(8,128)(2,1)S(1)} %reshape.173), channel_id=1, source_target_pairs={{0,16},{4,20},{8,24},{12,28},{16,0},{20,4},{24,8},{28,12},{1,17},{... | collective-permute-start | bytes 442376 | tf_op jit(solution)/shard_map/ppermute | solution.py:22
  11.2 0.5 %collective-permute-start = (bf16[384,192]{0,1:T(8,128)(2,1)S(1)}, bf16[384,192]{0,1:T(8,128)(2,1)S(1)}, u32[]{:S(2)}, u32[]{:S(2)}) collective-permute-start(bf16[384,192]{0,1:T(8,128)(2,1)S(1)} %reshape.173), channel_id=1, source_target_pairs={{0,8},{4,12},{8,0},{12,4},{16,24},{20,28},{24,16},{28,20},{1,9},{5... | collective-permute-start | bytes 442376 | tf_op jit(solution)/shard_map/ppermute | solution.py:22
  11.7 0.7 %collective-permute-done.9 = bf16[384,192]{0,1:T(8,128)(2,1)S(1)} collective-permute-done((bf16[384,192]{0,1:T(8,128)(2,1)S(1)}, bf16[384,192]{0,1:T(8,128)(2,1)S(1)}, u32[]{:S(2)}, u32[]{:S(2)}) %collective-permute-start.9) | collective-permute-done | bytes 147488 | tf_op jit(solution)/shard_map/ppermute | solution.py:55
  12.5 1.3 %collective-permute-start.7 = (bf16[384,192]{0,1:T(8,128)(2,1)S(1)}, bf16[384,192]{0,1:T(8,128)(2,1)S(1)}, u32[]{:S(2)}, u32[]{:S(2)}) collective-permute-start(bf16[384,192]{0,1:T(8,128)(2,1)S(1)} %reshape.173), channel_id=1, source_target_pairs={{0,3},{1,0},{2,1},{3,2},{4,7},{5,4},{6,5},{7,6},{8,11},{9,8},{10,9... | collective-permute-start | bytes 442376 | tf_op jit(solution)/shard_map/ppermute | solution.py:55
  13.7 4.2 %collective-permute-done.8 = bf16[384,192]{0,1:T(8,128)(2,1)S(1)} collective-permute-done((bf16[384,192]{0,1:T(8,128)(2,1)S(1)}, bf16[384,192]{0,1:T(8,128)(2,1)S(1)}, u32[]{:S(2)}, u32[]{:S(2)}) %collective-permute-start.8) | collective-permute-done | bytes 147488 | tf_op jit(solution)/shard_map/ppermute | solution.py:55
  18.0 0.5 %collective-permute-start.6 = (bf16[384,192]{0,1:T(8,128)(2,1)S(1)}, bf16[384,192]{0,1:T(8,128)(2,1)S(1)}, u32[]{:S(2)}, u32[]{:S(2)}) collective-permute-start(bf16[384,192]{0,1:T(8,128)(2,1)S(1)} %collective-permute-done.2), channel_id=1, source_target_pairs={{0,4},{4,0},{8,12},{12,8},{16,20},{20,16},{24,28},{28,24},{1,5},{5... | collective-permute-start | bytes 442376 | tf_op jit(solution)/shard_map/ppermute | solution.py:23
  18.6 0.4 %collective-permute-start.4 = (bf16[384,192]{0,1:T(8,128)(2,1)S(1)}, bf16[384,192]{0,1:T(8,128)(2,1)S(1)}, u32[]{:S(2)}, u32[]{:S(2)}) collective-permute-start(bf16[384,192]{0,1:T(8,128)(2,1)S(1)} %collective-permute-done), channel_id=1, source_target_pairs={{0,4},{4,0},{8,12},{12,8},{16,20},{20,16},{24,28},{28,24},{1,5},{5... | collective-permute-start | bytes 442376 | tf_op jit(solution)/shard_map/ppermute | solution.py:23
  19.3 0.3 collective-permute-done.7
  20.1 0.6 %gather_fusion = bf16[8,192,192]{2,1,0:T(8,128)(2,1)S(1)} fusion(bf16[8,192,192]{2,1,0:T(8,128)(2,1)S(1)} %bitcast.67, s32[1024]{0:T(1024)S(1)} %pad_clamp_fusion), kind=kCustom, calls=%fused_computation | custom fusion | bytes 1179680 | tf_op jit(solution)/shard_map/gather | solution.py:58
  21.1 0.5 %fusion.16 = f32[384,192,1]{0,1,2:T(8,128)S(1)} fusion(bf16[8,384,192]{1,2,0:T(8,128)(2,1)S(1)} %bitcast.66, bf16[8,192,192]{2,1,0:T(8,128)(2,1)S(1)} %gather_fusion), kind=kOutput, calls=%fused_computation.40 | convolution fusion | flops 226492416 | bytes 2064384 | tf_op jit(solution)/shard_map/pab,pbn->an/dot_general | solution.py:60
  21.6 1.4 %collective-permute-start.11 = (f32[384,192]{0,1:T(8,128)S(1)}, f32[384,192]{0,1:T(8,128)S(1)}, u32[]{:S(2)}, u32[]{:S(2)}) collective-permute-start(f32[384,192]{0,1:T(8,128)S(1)} %bitcast.69), channel_id=1, source_target_pairs={{0,16},{4,20},{8,24},{12,28},{16,0},{20,4},{24,8},{28,12},{1,17},{... | collective-permute-start | bytes 884744 | tf_op jit(solution)/shard_map/ppermute | solution.py:22
  23.0 1.5 %collective-permute-start.10 = (f32[384,192]{0,1:T(8,128)S(1)}, f32[384,192]{0,1:T(8,128)S(1)}, u32[]{:S(2)}, u32[]{:S(2)}) collective-permute-start(f32[384,192]{0,1:T(8,128)S(1)} %bitcast.70), channel_id=1, source_target_pairs={{0,8},{4,12},{8,0},{12,4},{16,24},{20,28},{24,16},{28,20},{1,9},{5... | collective-permute-start | bytes 884744 | tf_op jit(solution)/shard_map/ppermute | solution.py:22
  24.5 0.7 %collective-permute-start.12 = (f32[384,192]{0,1:T(8,128)S(1)}, f32[384,192]{0,1:T(8,128)S(1)}, u32[]{:S(2)}, u32[]{:S(2)}) collective-permute-start(f32[384,192]{0,1:T(8,128)S(1)} %bitcast.71), channel_id=1, source_target_pairs={{0,24},{4,28},{8,16},{12,20},{16,8},{20,12},{24,0},{28,4},{1,25},{... | collective-permute-start | bytes 884744 | tf_op jit(solution)/shard_map/ppermute | solution.py:22
  25.2 5.5 %collective-permute-done.11 = f32[384,192]{0,1:T(8,128)S(1)} collective-permute-done((f32[384,192]{0,1:T(8,128)S(1)}, f32[384,192]{0,1:T(8,128)S(1)}, u32[]{:S(2)}, u32[]{:S(2)}) %collective-permute-start.11) | collective-permute-done | bytes 294944 | tf_op jit(solution)/shard_map/ppermute | solution.py:22
  30.7 2.2 %collective-permute-done.10 = f32[384,192]{0,1:T(8,128)S(1)} collective-permute-done((f32[384,192]{0,1:T(8,128)S(1)}, f32[384,192]{0,1:T(8,128)S(1)}, u32[]{:S(2)}, u32[]{:S(2)}) %collective-permute-start.10) | collective-permute-done | bytes 294944 | tf_op jit(solution)/shard_map/ppermute | solution.py:22
  32.9 5.0 %collective-permute-done.12 = f32[384,192]{0,1:T(8,128)S(1)} collective-permute-done((f32[384,192]{0,1:T(8,128)S(1)}, f32[384,192]{0,1:T(8,128)S(1)}, u32[]{:S(2)}, u32[]{:S(2)}) %collective-permute-start.12) | collective-permute-done | bytes 294944 | tf_op jit(solution)/shard_map/ppermute | solution.py:22
  38.0 1.5 %collective-permute-done.16 = f32[384,192]{0,1:T(8,128)S(1)} collective-permute-done((f32[384,192]{0,1:T(8,128)S(1)}, f32[384,192]{0,1:T(8,128)S(1)}, u32[]{:S(2)}, u32[]{:S(2)}) %collective-permute-start.16) | collective-permute-done | bytes 294944 | tf_op jit(solution)/shard_map/ppermute | solution.py:23
  39.9 1.4 %fusion.1 = f32[384,192]{0,1:T(8,128)S(1)} fusion(f32[8,384,192]{1,2,0:T(8,128)S(1)} %bitcast.65, bf16[8,192,192]{2,1,0:T(8,128)(2,1)S(1)} %gather_fusion, f32[384,192,1]{0,1,2:T(8,128)S(1)} %fusion.16), kind=kOutput, calls=%fused_computation.9 | convolution fusion | flops 1359175680 | bytes 3538944 | tf_op jit(solution)/shard_map/pab,pbn->an/dot_general | solution.py:64
  42.4 0.9 %copy.15 = f32[1,13,4096]{2,0,1:T(1,128)} copy(f32[1,13,4096]{2,1,0:T(8,128)S(1)} %convolution_bitcast_fusion) | data formatting | bytes 425984 | tf_op jit(solution)/shard_map/broadcast_in_dim | solution.py:79
  (39 shorter events, 3.8 us)
Async XLA Ops:
  0.0 0.9 %copy-start = (bf16[1,9,4096]{2,1,0:T(8,128)(2,1)S(1)}, bf16[1,9,4096]{2,1,0:T(8,128)(2,1)}, u32[]{:S(2)}) copy-start(bf16[1,9,4096]{2,1,0:T(8,128)(2,1)} %param.3) | copy-start | bytes 221188
  2.5 9.9 %collective-permute-start.9 = (bf16[384,192]{0,1:T(8,128)(2,1)S(1)}, bf16[384,192]{0,1:T(8,128)(2,1)S(1)}, u32[]{:S(2)}, u32[]{:S(2)}) collective-permute-start(bf16[384,192]{0,1:T(8,128)(2,1)S(1)} %reshape.173), channel_id=1, source_target_pairs={{0,1},{1,2},{2,3},{3,0},{4,5},{5,6},{6,7},{7,4},{8,9},{9,10},{10,1... | collective-permute-start | bytes 442376 | tf_op jit(solution)/shard_map/ppermute | solution.py:55
  5.6 12.3 %collective-permute-start.8 = (bf16[384,192]{0,1:T(8,128)(2,1)S(1)}, bf16[384,192]{0,1:T(8,128)(2,1)S(1)}, u32[]{:S(2)}, u32[]{:S(2)}) collective-permute-start(bf16[384,192]{0,1:T(8,128)(2,1)S(1)} %reshape.173), channel_id=1, source_target_pairs={{0,2},{1,3},{2,0},{3,1},{4,6},{5,7},{6,4},{7,5},{8,10},{9,11},{10,... | collective-permute-start | bytes 442376 | tf_op jit(solution)/shard_map/ppermute | solution.py:55
  8.2 9.8 %collective-permute-start.2 = (bf16[384,192]{0,1:T(8,128)(2,1)S(1)}, bf16[384,192]{0,1:T(8,128)(2,1)S(1)}, u32[]{:S(2)}, u32[]{:S(2)}) collective-permute-start(bf16[384,192]{0,1:T(8,128)(2,1)S(1)} %reshape.173), channel_id=1, source_target_pairs={{0,24},{4,28},{8,16},{12,20},{16,8},{20,12},{24,0},{28,4},{1,25},{... | collective-permute-start | bytes 442376 | tf_op jit(solution)/shard_map/ppermute | solution.py:22
  10.7 7.8 %collective-permute-start.1 = (bf16[384,192]{0,1:T(8,128)(2,1)S(1)}, bf16[384,192]{0,1:T(8,128)(2,1)S(1)}, u32[]{:S(2)}, u32[]{:S(2)}) collective-permute-start(bf16[384,192]{0,1:T(8,128)(2,1)S(1)} %reshape.173), channel_id=1, source_target_pairs={{0,16},{4,20},{8,24},{12,28},{16,0},{20,4},{24,8},{28,12},{1,17},{... | collective-permute-start | bytes 442376 | tf_op jit(solution)/shard_map/ppermute | solution.py:22
  11.2 7.4 %collective-permute-start = (bf16[384,192]{0,1:T(8,128)(2,1)S(1)}, bf16[384,192]{0,1:T(8,128)(2,1)S(1)}, u32[]{:S(2)}, u32[]{:S(2)}) collective-permute-start(bf16[384,192]{0,1:T(8,128)(2,1)S(1)} %reshape.173), channel_id=1, source_target_pairs={{0,8},{4,12},{8,0},{12,4},{16,24},{20,28},{24,16},{28,20},{1,9},{5... | collective-permute-start | bytes 442376 | tf_op jit(solution)/shard_map/ppermute | solution.py:22
  12.5 7.2 %collective-permute-start.7 = (bf16[384,192]{0,1:T(8,128)(2,1)S(1)}, bf16[384,192]{0,1:T(8,128)(2,1)S(1)}, u32[]{:S(2)}, u32[]{:S(2)}) collective-permute-start(bf16[384,192]{0,1:T(8,128)(2,1)S(1)} %reshape.173), channel_id=1, source_target_pairs={{0,3},{1,0},{2,1},{3,2},{4,7},{5,4},{6,5},{7,6},{8,11},{9,8},{10,9... | collective-permute-start | bytes 442376 | tf_op jit(solution)/shard_map/ppermute | solution.py:55
  18.0 2.7 %collective-permute-start.3 = (bf16[384,192]{0,1:T(8,128)(2,1)S(1)}, bf16[384,192]{0,1:T(8,128)(2,1)S(1)}, u32[]{:S(2)}, u32[]{:S(2)}) collective-permute-start(bf16[384,192]{0,1:T(8,128)(2,1)S(1)} %reshape.173), channel_id=1, source_target_pairs={{0,4},{4,0},{8,12},{12,8},{16,20},{20,16},{24,28},{28,24},{1,5},{5... | collective-permute-start | bytes 442376 | tf_op jit(solution)/shard_map/ppermute | solution.py:23
  18.0 2.7 %collective-permute-start.6 = (bf16[384,192]{0,1:T(8,128)(2,1)S(1)}, bf16[384,192]{0,1:T(8,128)(2,1)S(1)}, u32[]{:S(2)}, u32[]{:S(2)}) collective-permute-start(bf16[384,192]{0,1:T(8,128)(2,1)S(1)} %collective-permute-done.2), channel_id=1, source_target_pairs={{0,4},{4,0},{8,12},{12,8},{16,20},{20,16},{24,28},{28,24},{1,5},{5... | collective-permute-start | bytes 442376 | tf_op jit(solution)/shard_map/ppermute | solution.py:23
  18.5 2.2 %collective-permute-start.5 = (bf16[384,192]{0,1:T(8,128)(2,1)S(1)}, bf16[384,192]{0,1:T(8,128)(2,1)S(1)}, u32[]{:S(2)}, u32[]{:S(2)}) collective-permute-start(bf16[384,192]{0,1:T(8,128)(2,1)S(1)} %collective-permute-done.1), channel_id=1, source_target_pairs={{0,4},{4,0},{8,12},{12,8},{16,20},{20,16},{24,28},{28,24},{1,5},{5... | collective-permute-start | bytes 442376 | tf_op jit(solution)/shard_map/ppermute | solution.py:23
  18.6 2.2 %collective-permute-start.4 = (bf16[384,192]{0,1:T(8,128)(2,1)S(1)}, bf16[384,192]{0,1:T(8,128)(2,1)S(1)}, u32[]{:S(2)}, u32[]{:S(2)}) collective-permute-start(bf16[384,192]{0,1:T(8,128)(2,1)S(1)} %collective-permute-done), channel_id=1, source_target_pairs={{0,4},{4,0},{8,12},{12,8},{16,20},{20,16},{24,28},{28,24},{1,5},{5... | collective-permute-start | bytes 442376 | tf_op jit(solution)/shard_map/ppermute | solution.py:23
  21.6 9.0 %collective-permute-start.11 = (f32[384,192]{0,1:T(8,128)S(1)}, f32[384,192]{0,1:T(8,128)S(1)}, u32[]{:S(2)}, u32[]{:S(2)}) collective-permute-start(f32[384,192]{0,1:T(8,128)S(1)} %bitcast.69), channel_id=1, source_target_pairs={{0,16},{4,20},{8,24},{12,28},{16,0},{20,4},{24,8},{28,12},{1,17},{... | collective-permute-start | bytes 884744 | tf_op jit(solution)/shard_map/ppermute | solution.py:22
  23.0 9.9 %collective-permute-start.10 = (f32[384,192]{0,1:T(8,128)S(1)}, f32[384,192]{0,1:T(8,128)S(1)}, u32[]{:S(2)}, u32[]{:S(2)}) collective-permute-start(f32[384,192]{0,1:T(8,128)S(1)} %bitcast.70), channel_id=1, source_target_pairs={{0,8},{4,12},{8,0},{12,4},{16,24},{20,28},{24,16},{28,20},{1,9},{5... | collective-permute-start | bytes 884744 | tf_op jit(solution)/shard_map/ppermute | solution.py:22
  24.5 13.4 %collective-permute-start.12 = (f32[384,192]{0,1:T(8,128)S(1)}, f32[384,192]{0,1:T(8,128)S(1)}, u32[]{:S(2)}, u32[]{:S(2)}) collective-permute-start(f32[384,192]{0,1:T(8,128)S(1)} %bitcast.71), channel_id=1, source_target_pairs={{0,24},{4,28},{8,16},{12,20},{16,8},{20,12},{24,0},{28,4},{1,25},{... | collective-permute-start | bytes 884744 | tf_op jit(solution)/shard_map/ppermute | solution.py:22
  25.2 12.8 %collective-permute-start.13 = (f32[384,192]{0,1:T(8,128)S(1)}, f32[384,192]{0,1:T(8,128)S(1)}, u32[]{:S(2)}, u32[]{:S(2)}) collective-permute-start(f32[384,192]{0,1:T(8,128)S(1)} %bitcast.72), channel_id=1, source_target_pairs={{0,4},{4,0},{8,12},{12,8},{16,20},{20,16},{24,28},{28,24},{1,5},{5... | collective-permute-start | bytes 884744 | tf_op jit(solution)/shard_map/ppermute | solution.py:23
  30.7 7.3 %collective-permute-start.15 = (f32[384,192]{0,1:T(8,128)S(1)}, f32[384,192]{0,1:T(8,128)S(1)}, u32[]{:S(2)}, u32[]{:S(2)}) collective-permute-start(f32[384,192]{0,1:T(8,128)S(1)} %collective-permute-done.11), channel_id=1, source_target_pairs={{0,4},{4,0},{8,12},{12,8},{16,20},{20,16},{24,28},{28,24},{1,5},{5... | collective-permute-start | bytes 884744 | tf_op jit(solution)/shard_map/ppermute | solution.py:23
  32.9 5.1 %collective-permute-start.14 = (f32[384,192]{0,1:T(8,128)S(1)}, f32[384,192]{0,1:T(8,128)S(1)}, u32[]{:S(2)}, u32[]{:S(2)}) collective-permute-start(f32[384,192]{0,1:T(8,128)S(1)} %collective-permute-done.10), channel_id=1, source_target_pairs={{0,4},{4,0},{8,12},{12,8},{16,20},{20,16},{24,28},{28,24},{1,5},{5... | collective-permute-start | bytes 884744 | tf_op jit(solution)/shard_map/ppermute | solution.py:23
  37.9 1.6 %collective-permute-start.16 = (f32[384,192]{0,1:T(8,128)S(1)}, f32[384,192]{0,1:T(8,128)S(1)}, u32[]{:S(2)}, u32[]{:S(2)}) collective-permute-start(f32[384,192]{0,1:T(8,128)S(1)} %collective-permute-done.12), channel_id=1, source_target_pairs={{0,4},{4,0},{8,12},{12,8},{16,20},{20,16},{24,28},{28,24},{1,5},{5... | collective-permute-start | bytes 884744 | tf_op jit(solution)/shard_map/ppermute | solution.py:23
  41.4 0.7 %copy-start.1 = (s32[1,13]{1,0:T(1,128)S(1)}, s32[1,13]{1,0:T(1,128)}, u32[]{:S(2)}) copy-start(s32[1,13]{1,0:T(1,128)} %param.5) | copy-start | bytes 160
